TPU v7x, 32 devices: a whole 2x2x4 slice. The times are simulated.
32 devices in a mesh: lat: 8 (over z, y), lon: 4 (over x, core).
Axes of the slice: x: 2, y: 2, z: 4, core: 2. Of those that a mesh axis runs over, the one named last changes fastest.
Arguments:
- fields: float32 [6, 32, 32, 4096], P(None, None, 'lat', 'lon'), may hold values from -6 to 6
- weights: float32 [16, 32, 4096], P(None, 'lat', 'lon'), may hold values from -2 to 2
- stencil: int32 [2, 32, 4096], P(None, 'lat', 'lon'), may hold values from -3 to 4095, as said below
- bands: float32 [6, 5, 32], replicated, may hold values from -3 to 3
Outputs:
- spectral_real: float32 [192, 32, 1280], P('lon', 'lat')
- spectral_imag: float32 [192, 32, 1280], P('lon', 'lat')
Inputs may be any that keep to these rules, and one draw needn't show every extreme that they name: stencil[0, i, j] lies in i - 3 to i; stencil[1, i, j] is (j - 16 + d) mod 4096 for some d of 0 to 29.
All inputs are finite; a program needn't handle non-finite values.
Results may differ from a plain program's by a relative error of at most 0.00007.
Values sent between devices are 32-bit elements; how exact they have to be, the bound alone decides.
No kernel may reach another device: no remote copies, remote signals or barrier semaphores. Data moves between devices by JAX's collectives and lax.ppermute only.
A program may use at most 128 MiB of HBM per device.

v0:
```python
import functools
import math

import jax
import jax.numpy as jnp
from jax import lax
from jax.experimental import pallas as pl
from jax.experimental.pallas import tpu as pltpu
from jax.sharding import PartitionSpec as P

RADIX = 64
NK = 1280
HALO = 16
ROWS_OUT = 3
TAPS = 4
LANES = 128
WINDOW = 256


def shifted(block, axis, width, dim, periodic):
    count = lax.axis_size(axis)
    forward = [(i, i + 1) for i in range(count - 1)]
    if periodic:
        forward.append((count - 1, 0))
    backward = [(target, source) for source, target in forward]
    low = lax.ppermute(
        lax.slice_in_dim(block, block.shape[dim] - width, None, axis=dim), axis, forward
    )
    high = lax.ppermute(lax.slice_in_dim(block, 0, width, axis=dim), axis, backward)
    return low, high


def spectrum(pieces, owners):
    n_rows, n_items, piece_len = pieces[0].shape
    line_len = piece_len * len(pieces)
    highest = lax.Precision.HIGH
    digits = jnp.arange(RADIX, dtype=jnp.int32)
    angle_one = (
        2.0 * math.pi / RADIX * (digits[:, None] * digits[None, :] % RADIX).astype(jnp.float32)
    )
    first_table = jnp.concatenate([jnp.cos(angle_one), -jnp.sin(angle_one)], axis=1)
    per_piece = piece_len // RADIX
    folded = jnp.concatenate(
        [piece.reshape(n_rows * n_items, per_piece, RADIX) for piece in pieces], axis=1
    )
    table = jnp.concatenate(
        [lax.dynamic_slice_in_dim(first_table, owner * per_piece, per_piece, axis=0) for owner in owners],
        axis=0,
    )
    partial_value = jnp.einsum("rab,ac->rbc", folded, table, precision=highest)
    angle_two = (
        2.0
        * math.pi
        / line_len
        * (digits[:, None] * digits[None, :] % line_len).astype(jnp.float32)
    )
    cos_two = jnp.cos(angle_two)
    sin_two = jnp.sin(angle_two)
    part_re = partial_value[..., :RADIX]
    part_im = partial_value[..., RADIX:]
    twisted = jnp.concatenate(
        [part_re * cos_two + part_im * sin_two, part_im * cos_two - part_re * sin_two], axis=-1
    )
    quotients = jnp.arange(NK // RADIX, dtype=jnp.int32)
    angle_three = (
        2.0 * math.pi / RADIX * (digits[:, None] * quotients[None, :] % RADIX).astype(jnp.float32)
    )
    with_cos = jnp.einsum("rbc,bq->rqc", twisted, jnp.cos(angle_three), precision=highest)
    with_sin = jnp.einsum("rbc,bq->rqc", twisted, jnp.sin(angle_three), precision=highest)
    scale = 1.0 / math.sqrt(line_len)
    real_part = (with_cos[..., :RADIX] + with_sin[..., RADIX:]) * scale
    imag_part = (with_cos[..., RADIX:] - with_sin[..., :RADIX]) * scale
    return (real_part.reshape(n_rows, n_items, NK), imag_part.reshape(n_rows, n_items, NK))


def interp_kernel(local, lat_rows, *refs):
    if local:
        hi_ref, lo_ref, info_ref, out_ref = refs
    else:
        hi_ref, lo_ref, info_ref, base_ref, out_ref = refs
    block = pl.program_id(0)
    start = pl.multiple_of(block * LANES, LANES)
    c_index = lax.broadcasted_iota(jnp.int32, (WINDOW, LANES), 0).astype(jnp.float32)
    j_index = lax.broadcasted_iota(jnp.int32, (WINDOW, LANES), 1).astype(jnp.float32)
    for row in range(lat_rows):
        info = info_ref[row]
        offset_r = info[16:17, :]
        offset_d = info[17:18, :]
        tap = c_index - j_index - offset_d
        masks = [tap == float(b) for b in range(TAPS)]
        if local:
            acc = jnp.zeros(out_ref.shape[1:], jnp.float32)
        else:
            acc = base_ref[row]
        for p in range(2 * ROWS_OUT + 1):
            h = row + p
            inside = ROWS_OUT <= h < ROWS_OUT + lat_rows
            if inside != local:
                continue
            if local:
                index = h - ROWS_OUT
            else:
                index = h if h < ROWS_OUT else h - lat_rows
            picked = []
            for b in range(TAPS):
                value = jnp.zeros_like(offset_r)
                for a in range(TAPS):
                    if 0 <= p - a <= ROWS_OUT:
                        value = jnp.where(offset_r == float(p - a), info[4 * a + b : 4 * a + b + 1, :], value)
                picked.append(value)
            matrix = jnp.where(
                masks[0],
                picked[0],
                jnp.where(masks[1], picked[1], jnp.where(masks[2], picked[2], jnp.where(masks[3], picked[3], 0.0))),
            )
            m_hi = matrix.astype(jnp.bfloat16)
            m_lo = (matrix - m_hi.astype(jnp.float32)).astype(jnp.bfloat16)
            x_hi = hi_ref[index, :, pl.ds(start, WINDOW)]
            x_lo = lo_ref[index, :, pl.ds(start, WINDOW)]
            acc = acc + jnp.dot(x_hi, m_hi, preferred_element_type=jnp.float32)
            acc = acc + jnp.dot(x_hi, m_lo, preferred_element_type=jnp.float32)
            acc = acc + jnp.dot(x_lo, m_hi, preferred_element_type=jnp.float32)
        out_ref[row] = acc


def interpolate(x_hi, x_lo, info, lat_rows, lon_cols, base=None):
    n_rows, n_items, width = x_hi.shape
    blocks = lon_cols // LANES
    whole = pl.BlockSpec((n_rows, n_items, width), lambda jb: (0, 0, 0))
    tile = pl.BlockSpec((lat_rows, n_items, LANES), lambda jb: (0, 0, jb))
    specs = [whole, whole, pl.BlockSpec((lat_rows, info.shape[1], LANES), lambda jb: (0, 0, jb))]
    operands = [x_hi, x_lo, info]
    if base is not None:
        specs.append(tile)
        operands.append(base)
    return pl.pallas_call(
        functools.partial(interp_kernel, base is None, lat_rows),
        out_shape=jax.ShapeDtypeStruct((lat_rows, n_items, lon_cols), jnp.float32),
        grid=(blocks,),
        in_specs=specs,
        out_specs=tile,
        compiler_params=pltpu.CompilerParams(vmem_limit_bytes=48 * 1024 * 1024),
    )(*operands)


def vertical_mix(raw, bands):
    n_levels = raw.shape[-2]
    pad = [(0, 0)] * raw.ndim
    pad[-2] = (2, 2)
    stacked = jnp.pad(raw, pad)
    lead = (None,) * (raw.ndim - 3)
    mixed = bands[lead + (slice(None), 0, slice(None), None)] * stacked[..., 0:n_levels, :]
    for shift_k in range(1, 5):
        mixed = mixed + bands[lead + (slice(None), shift_k, slice(None), None)] * stacked[
            ..., shift_k : shift_k + n_levels, :
        ]
    return mixed


def widen(block):
    left, right = shifted(block, "lon", HALO, block.ndim - 1, True)
    return jnp.concatenate([left, block, right], axis=block.ndim - 1)


def split_rows(rows, width):
    pad = [(0, 0)] * (rows.ndim - 1) + [(0, width - rows.shape[-1])]
    padded = jnp.pad(rows, pad)
    rounded = lax.reduce_precision(padded, exponent_bits=8, mantissa_bits=7)
    return rounded.astype(jnp.bfloat16), (padded - rounded).astype(jnp.bfloat16)


def on_device(fields, weights, stencil, bands):
    n_fields, n_levels, lat_rows, lon_cols = fields.shape
    n_items = n_fields * n_levels
    below_raw, above_raw = shifted(fields, "lat", ROWS_OUT, 2, False)

    width = lon_cols + LANES
    local_rows = vertical_mix(jnp.transpose(fields, (2, 0, 1, 3)), bands)
    local_hi, local_lo = split_rows(widen(local_rows.reshape(lat_rows, n_items, lon_cols)), width)

    lat_start = lax.axis_index("lat") * lat_rows
    lon_start = lax.axis_index("lon") * lon_cols
    line_len = lon_cols * lax.axis_size("lon")
    row_g = lat_start + jnp.arange(lat_rows, dtype=jnp.int32)[:, None]
    col_g = lon_start + jnp.arange(lon_cols, dtype=jnp.int32)[None, :]
    offset_r = (stencil[0] - row_g + ROWS_OUT).astype(jnp.float32)
    offset_d = jnp.mod(stencil[1] - col_g + HALO, line_len).astype(jnp.float32)
    info = jnp.concatenate(
        [
            jnp.transpose(weights, (1, 0, 2)),
            offset_r[:, None, :],
            offset_d[:, None, :],
            jnp.zeros((lat_rows, 6, lon_cols), jnp.float32),
        ],
        axis=1,
    )
    partial = interpolate(local_hi, local_lo, info, lat_rows, lon_cols)

    below_raw, above_raw, partial = lax.optimization_barrier((below_raw, above_raw, partial))
    halo_raw = jnp.concatenate([below_raw, above_raw], axis=2)
    halo_rows = vertical_mix(jnp.transpose(halo_raw, (2, 0, 1, 3)), bands)
    halo_hi, halo_lo = split_rows(widen(halo_rows.reshape(2 * ROWS_OUT, n_items, lon_cols)), width)
    departed = interpolate(halo_hi, halo_lo, info, lat_rows, lon_cols, base=partial)

    parts = lax.axis_size("lon")
    me = lax.axis_index("lon")
    chunk = n_items // parts
    pieces = []
    owners = []
    for shift in range(parts):
        target = lax.rem(me + shift, parts)
        piece = lax.dynamic_slice_in_dim(departed, target * chunk, chunk, axis=1)
        if shift:
            piece = lax.ppermute(piece, "lon", [(i, (i + shift) % parts) for i in range(parts)])
        pieces.append(piece)
        owners.append(lax.rem(me - shift + parts, parts))
    real_part, imag_part = spectrum(pieces, owners)
    return (jnp.transpose(real_part, (1, 0, 2)), jnp.transpose(imag_part, (1, 0, 2)))


def solution(mesh):
    placed = (P(None, None, "lat", "lon"), P(None, "lat", "lon"), P(None, "lat", "lon"), P())
    return jax.shard_map(
        on_device,
        mesh=mesh,
        in_specs=placed,
        out_specs=(P("lon", "lat", None), P("lon", "lat", None)),
        check_vma=False,
    )
```

profile of v0, /device:TPU:11, one launch (start us, length us, event | category | flops | bytes accessed | tf_op | source)
XLA Modules:
  0.0 230.0 jit_solution(18179178152920598355)
XLA Ops:
  0.6 5.6 %fusion.81 = (f32[6,32,3,1024]{3,2,1,0:T(4,128)S(1)}, f32[6,32,3,1024]{3,2,1,0:T(4,128)S(1)}) fusion(f32[6,32,4,1024]{3,2,1,0:T(4,128)} %param.4), kind=kLoop, calls=%fused_computation.132 | loop fusion | bytes 9437184 | tf_op jit(solution)/shard_map/slice | solution.py:29
  6.3 2.7 %copy.44 = f32[6,32,3,1024]{3,1,2,0:T(8,128)} copy(f32[6,32,3,1024]{3,2,1,0:T(4,128)S(1)} %get-tuple-element.29) | data formatting | bytes 4718592
  9.0 3.1 %collective-permute-start = (f32[6,32,3,1024]{3,1,2,0:T(8,128)}, f32[6,32,3,1024]{3,1,2,0:T(8,128)}, u32[]{:S(2)}, u32[]{:S(2)}) collective-permute-start(f32[6,32,3,1024]{3,1,2,0:T(8,128)} %copy.44), channel_id=1, source_target_pairs={{0,4},{4,8},{8,12},{12,16},{16,20},{20,24},{24,28},{1,5},{5,9},{9,... | collective-permute-start | bytes 7077896 | tf_op jit(solution)/shard_map/ppermute | solution.py:26
  12.2 2.8 %copy.45 = f32[6,32,3,1024]{3,1,2,0:T(8,128)} copy(f32[6,32,3,1024]{3,2,1,0:T(4,128)S(1)} %get-tuple-element.28) | data formatting | bytes 4718592
  14.9 3.0 %collective-permute-start.1 = (f32[6,32,3,1024]{3,1,2,0:T(8,128)}, f32[6,32,3,1024]{3,1,2,0:T(8,128)}, u32[]{:S(2)}, u32[]{:S(2)}) collective-permute-start(f32[6,32,3,1024]{3,1,2,0:T(8,128)} %copy.45), channel_id=1, source_target_pairs={{4,0},{8,4},{12,8},{16,12},{20,16},{24,20},{28,24},{5,1},{9,5},{13... | collective-permute-start | bytes 7077896 | tf_op jit(solution)/shard_map/ppermute | solution.py:29
  18.0 2.8 %multiply_add_fusion.1 = f32[4,6,32,1024]{3,0,2,1:T(4,128)S(1)} fusion(f32[4,6,32,1024]{3,0,2,1:T(4,128)S(1)} %bitcast.49, f32[6,32]{1,0:T(8,128)S(1)} %get-tuple-element.39, f32[6,32]{1,0:T(8,128)S(1)} %get-tuple-element.40, f32[6,32]{1,0:T(8,128)S(1)} %get-tuple-element.37, f32[6,32]{1,0:T(8,128)S(1)} %get-tuple-element.38, f32[6,32]{1,0:T(8,128)S(1)} %get-tuple-element.36), kind=kLoop, calls=%fused_computation.30 | loop fusion | flops 7077888 | bytes 6295296 | tf_op jit(solution)/shard_map/add | solution.py:154
  20.8 1.8 copy.29
  22.7 1.0 fusion.80
  23.7 1.4 collective-permute-start.2
  25.0 0.9 copy.63
  26.1 1.1 maximum_maximum_fusion.refs_2_
  27.1 5.3 %collective-permute-done.2 = f32[4,192,16]{2,1,0:T(8,128)} collective-permute-done((f32[4,192,16]{2,1,0:T(8,128)}, f32[4,192,16]{2,1,0:T(8,128)}, u32[]{:S(2)}, u32[]{:S(2)}) %collective-permute-start.2) | collective-permute-done | bytes 49184 | tf_op jit(solution)/shard_map/ppermute | solution.py:26
  32.4 3.8 %collective-permute-done.3 = f32[4,192,16]{2,1,0:T(8,128)} collective-permute-done((f32[4,192,16]{2,1,0:T(8,128)}, f32[4,192,16]{2,1,0:T(8,128)}, u32[]{:S(2)}, u32[]{:S(2)}) %collective-permute-start.3) | collective-permute-done | bytes 49184 | tf_op jit(solution)/shard_map/ppermute | solution.py:29
  36.2 4.4 %concatenate.24 = f32[4,192,1056]{2,1,0:T(8,128)} concatenate(f32[4,192,16]{2,1,0:T(8,128)} %collective-permute-done.2, f32[4,192,1024]{2,1,0:T(8,128)S(1)} %bitcast.53, f32[4,192,16]{2,1,0:T(8,128)} %collective-permute-done.3), dimensions={2} | concatenate | bytes 6488064 | tf_op jit(solution)/shard_map/concatenate | solution.py:162
  40.6 2.6 %fusion.17 = (bf16[4,192,1152]{2,1,0:T(8,128)(2,1)S(1)}, bf16[4,192,1152]{2,1,0:T(8,128)(2,1)S(1)}) fusion(f32[4,192,1056]{2,1,0:T(8,128)} %concatenate.24), kind=kLoop, calls=%fused_computation.29 | loop fusion | flops 3538944 | bytes 6782976 | tf_op jit(solution)/shard_map/convert_element_type | solution.py:169
  43.2 13.6 %shard_map.59.refs_3_ = f32[4,192,1024]{2,1,0:T(8,128)} custom-call(bf16[4,192,1152]{2,1,0:T(8,128)(2,1)S(1)} %get-tuple-element.21.refs_0_, bf16[4,192,1152]{2,1,0:T(8,128)(2,1)S(1)} %get-tuple-element.20.refs_1_, f32[4,24,1024]{2,1,0:T(8,128)S(1)} %maximum_maximum_fusion.refs_2_), custom_call_target="tpu_custom_call" | custom-call | tf_op jit(solution)/shard_map/pallas_call | solution.py:136
  56.8 56.1 %collective-permute-done = f32[6,32,3,1024]{3,1,2,0:T(8,128)} collective-permute-done((f32[6,32,3,1024]{3,1,2,0:T(8,128)}, f32[6,32,3,1024]{3,1,2,0:T(8,128)}, u32[]{:S(2)}, u32[]{:S(2)}) %collective-permute-start) | collective-permute-done | bytes 2359328 | tf_op jit(solution)/shard_map/ppermute | solution.py:26
  112.9 2.9 %collective-permute-done.1 = f32[6,32,3,1024]{3,1,2,0:T(8,128)} collective-permute-done((f32[6,32,3,1024]{3,1,2,0:T(8,128)}, f32[6,32,3,1024]{3,1,2,0:T(8,128)}, u32[]{:S(2)}, u32[]{:S(2)}) %collective-permute-start.1) | collective-permute-done | bytes 2359328 | tf_op jit(solution)/shard_map/ppermute | solution.py:29
  115.9 2.8 %maximum_bitcast_fusion = f32[6,6,32,1024]{3,2,0,1:T(8,128)S(1)} fusion(f32[6,32,3,1024]{3,1,2,0:T(8,128)} %collective-permute-done.1, f32[6,32,3,1024]{3,1,2,0:T(8,128)} %collective-permute-done), kind=kLoop, calls=%fused_computation.28 | loop fusion | flops 1179648 | bytes 9437184 | tf_op jit(solution)/shard_map/transpose | solution.py:201
  118.6 2.9 %fusion.13 = f32[6,6,32,1024]{3,2,0,1:T(8,128)S(1)} fusion(f32[6,6,32,1024]{3,2,0,1:T(8,128)S(1)} %maximum_bitcast_fusion, f32[6,32]{1,0:T(8,128)S(1)} %get-tuple-element.39, f32[6,32]{1,0:T(8,128)S(1)} %copy-done.4, f32[6,32]{1,0:T(8,128)S(1)} %get-tuple-element.37, f32[6,32]{1,0:T(8,128)S(1)} %get-tuple-element.38, f32[6,32]{1,0:T(8,128)S(1)} %get-tuple-element.36), kind=kLoop, calls=%fused_computation.24 | loop fusion | flops 10616832 | bytes 9441024 | tf_op jit(solution)/shard_map/add | solution.py:154
  121.9 2.2 copy-done.1
  124.6 0.7 collective-permute-start.4
  125.5 1.3 collective-permute-done.4
  127.1 2.4 %collective-permute-done.5 = f32[6,192,16]{1,2,0:T(8,128)S(1)} collective-permute-done((f32[6,192,16]{1,2,0:T(8,128)S(1)}, f32[6,192,16]{1,2,0:T(8,128)S(1)}, u32[]{:S(2)}, u32[]{:S(2)}) %collective-permute-start.5) | collective-permute-done | bytes 73760 | tf_op jit(solution)/shard_map/ppermute | solution.py:29
  129.7 6.9 %concatenate.27 = f32[6,192,1056]{2,1,0:T(8,128)} concatenate(f32[6,192,16]{2,1,0:T(8,128)S(1)} %copy.36, f32[6,192,1024]{2,1,0:T(8,128)} %bitcast.51, f32[6,192,16]{2,1,0:T(8,128)S(1)} %copy.37), dimensions={2} | concatenate | bytes 9732096 | tf_op jit(solution)/shard_map/concatenate | solution.py:162
  136.6 3.6 %fusion.8 = (bf16[6,192,1152]{2,1,0:T(8,128)(2,1)S(1)}, bf16[6,192,1152]{2,1,0:T(8,128)(2,1)S(1)}) fusion(f32[6,192,1056]{2,1,0:T(8,128)} %concatenate.27), kind=kLoop, calls=%fused_computation.17 | loop fusion | flops 5308416 | bytes 10174464 | tf_op jit(solution)/shard_map/convert_element_type | solution.py:169
  140.2 11.7 %shard_map.60 = f32[4,192,1024]{2,1,0:T(8,128)} custom-call(bf16[6,192,1152]{2,1,0:T(8,128)(2,1)S(1)} %get-tuple-element.15.refs_0_, bf16[6,192,1152]{2,1,0:T(8,128)(2,1)S(1)} %get-tuple-element.14.refs_1_, f32[4,24,1024]{2,1,0:T(8,128)S(1)} %maximum_maximum_fusion.refs_2_, f32[4,192,1024]{2,1,0:T(8,128)} %shard_map.59.refs_3_), custom_call_target="tpu_custom_call" | custom-call | tf_op jit(solution)/shard_map/pallas_call | solution.py:136
  151.9 3.3 %constant_dynamic-slice_fusion.3 = (f32[4,48,1024]{2,1,0:T(8,128)S(1)}, f32[4,48,1024]{2,1,0:T(8,128)}, f32[4,48,1024]{2,1,0:T(8,128)}, f32[4,48,1024]{2,1,0:T(8,128)}) fusion(f32[4,192,1024]{2,1,0:T(8,128)} %shard_map.60, s32[]{:T(128)S(6)} %select_n.73, s32[]{:T(128)S(6)} %select_n.76, s32[]{:T(128)S(6)} %select_n.75, s32[]{:T(128)S(6)} %select_n.74), kind=kLoop, calls=%fused_computation.118 | loop fusion | bytes 6291472 | tf_op jit(solution)/shard_map/dynamic_slice | solution.py:212
  155.2 1.2 collective-permute-start.7
  156.4 0.8 collective-permute-start.8
  157.6 0.4 reshape.182
  158.0 4.0 %copy.38 = f32[192,16,64]{1,2,0:T(8,128)} copy(f32[192,16,64]{2,1,0:T(8,128)S(1)} %reshape.182) | data formatting | bytes 1572864 | tf_op jit(solution)/shard_map/reshape | solution.py:44
  162.1 8.6 %collective-permute-done.6 = f32[4,48,1024]{2,1,0:T(8,128)} collective-permute-done((f32[4,48,1024]{2,1,0:T(8,128)}, f32[4,48,1024]{2,1,0:T(8,128)}, u32[]{:S(2)}, u32[]{:S(2)}) %collective-permute-start.6) | collective-permute-done | bytes 786464 | tf_op jit(solution)/shard_map/ppermute | solution.py:214
  170.6 1.6 reshape.183
  172.2 4.1 %copy.39 = f32[192,16,64]{1,2,0:T(8,128)} copy(f32[192,16,64]{2,1,0:T(8,128)S(1)} %reshape.183) | data formatting | bytes 1572864 | tf_op jit(solution)/shard_map/reshape | solution.py:44
  176.3 13.8 %collective-permute-done.7 = f32[4,48,1024]{2,1,0:T(8,128)} collective-permute-done((f32[4,48,1024]{2,1,0:T(8,128)}, f32[4,48,1024]{2,1,0:T(8,128)}, u32[]{:S(2)}, u32[]{:S(2)}) %collective-permute-start.7) | collective-permute-done | bytes 786464 | tf_op jit(solution)/shard_map/ppermute | solution.py:214
  190.1 1.6 reshape.184
  191.7 4.1 %copy.40 = f32[192,16,64]{1,2,0:T(8,128)} copy(f32[192,16,64]{2,1,0:T(8,128)S(1)} %reshape.184) | data formatting | bytes 1572864 | tf_op jit(solution)/shard_map/reshape | solution.py:44
  196.2 4.0 %copy.41 = f32[192,16,64]{1,2,0:T(8,128)} copy(f32[192,16,64]{2,1,0:T(8,128)S(1)} %reshape.185) | data formatting | bytes 1572864 | tf_op jit(solution)/shard_map/reshape | solution.py:44
  200.2 12.8 %fusion = f32[192,64,128]{2,1,0:T(8,128)S(1)} fusion(f32[192,16,64]{1,2,0:T(8,128)} %copy.41, f32[192,16,64]{1,2,0:T(8,128)} %copy.40, f32[192,16,64]{1,2,0:T(8,128)} %copy.39, f32[192,16,64]{1,2,0:T(8,128)} %copy.38, f32[16,128]{1,0:T(8,128)S(1)} %get-tuple-element.33, f32[16,128]{1,0:T(8,128)S(1)} %get-tuple-element.32, ...), kind=kOutput, calls=%fused_computation.6 | convolution fusion | flops 606363648 | bytes 9469952 | tf_op jit(solution)/shard_map/rab,ac->rbc/dot_general | solution.py:50
  213.0 3.3 %multiply_add_fusion = (f32[192,64,64]{2,1,0:T(8,128)S(1)}, f32[192,64,64]{2,1,0:T(8,128)S(1)}) fusion(f32[192,64,128]{2,1,0:T(8,128)S(1)} %fusion, f32[64,64]{1,0:T(8,128)S(1)} %get-tuple-element.45, f32[64,64]{1,0:T(8,128)S(1)} %get-tuple-element.46), kind=kLoop, calls=%fused_computation.16 | loop fusion | flops 4718592 | bytes 12615680 | tf_op jit(solution)/shard_map/add | solution.py:62
  216.3 2.7 %fusion.23 = f32[192,20,128]{2,1,0:T(8,128)S(1)} fusion(f32[192,64,64]{2,1,0:T(8,128)S(1)} %get-tuple-element.13, f32[192,64,64]{2,1,0:T(8,128)S(1)} %get-tuple-element.12), kind=kOutput, calls=%fused_computation.39 | convolution fusion | flops 190334464 | bytes 8257536 | tf_op jit(solution)/shard_map/rbc,bq->rqc/dot_general | solution.py:68
  219.0 2.7 %fusion.24 = f32[192,20,128]{2,1,0:T(8,128)S(1)} fusion(f32[192,64,64]{2,1,0:T(8,128)S(1)} %get-tuple-element.13, f32[192,64,64]{2,1,0:T(8,128)S(1)} %get-tuple-element.12), kind=kOutput, calls=%fused_computation.40 | convolution fusion | flops 190334464 | bytes 8257536 | tf_op jit(solution)/shard_map/rbc,bq->rqc/dot_general | solution.py:69
  221.7 2.7 %fusion.19 = (f32[192,20,64]{2,1,0:T(8,128)S(1)}, f32[192,20,64]{2,1,0:T(8,128)}) fusion(f32[192,20,128]{2,1,0:T(8,128)S(1)} %fusion.24, f32[192,20,128]{2,1,0:T(8,128)S(1)} %fusion.23), kind=kLoop, calls=%fused_computation.34 | loop fusion | flops 983040 | bytes 5898240 | tf_op jit(solution)/shard_map/mul | solution.py:72
  224.4 2.0 reshape.186
  226.4 1.6 copy.42
  228.0 0.5 reshape.187
  228.5 1.6 copy.43
  (34 shorter events, 2.5 us)
Async XLA Ops:
  6.3 11.7 %copy-start.6 = (f32[6,5,32]{2,0,1:T(8,128)S(1)}, f32[6,5,32]{2,0,1:T(8,128)}, u32[]{:S(2)}) copy-start(f32[6,5,32]{2,0,1:T(8,128)} %param.7) | copy-start | bytes 11524
  6.3 11.7 %copy-start = (f32[6,32,4,1024]{3,2,1,0:T(4,128)S(1)}, f32[6,32,4,1024]{3,2,1,0:T(4,128)}, u32[]{:S(2)}) copy-start(f32[6,32,4,1024]{3,2,1,0:T(4,128)} %param.4) | copy-start | bytes 9437188
  9.0 103.9 %collective-permute-start = (f32[6,32,3,1024]{3,1,2,0:T(8,128)}, f32[6,32,3,1024]{3,1,2,0:T(8,128)}, u32[]{:S(2)}, u32[]{:S(2)}) collective-permute-start(f32[6,32,3,1024]{3,1,2,0:T(8,128)} %copy.44), channel_id=1, source_target_pairs={{0,4},{4,8},{8,12},{12,16},{16,20},{20,24},{24,28},{1,5},{5,9},{9,... | collective-permute-start | bytes 7077896 | tf_op jit(solution)/shard_map/ppermute | solution.py:26
  14.9 100.9 %collective-permute-start.1 = (f32[6,32,3,1024]{3,1,2,0:T(8,128)}, f32[6,32,3,1024]{3,1,2,0:T(8,128)}, u32[]{:S(2)}, u32[]{:S(2)}) collective-permute-start(f32[6,32,3,1024]{3,1,2,0:T(8,128)} %copy.45), channel_id=1, source_target_pairs={{4,0},{8,4},{12,8},{16,12},{20,16},{24,20},{28,24},{5,1},{9,5},{13... | collective-permute-start | bytes 7077896 | tf_op jit(solution)/shard_map/ppermute | solution.py:29
  18.0 4.7 %copy-start.3 = (f32[6,32]{1,0:T(8,128)}, f32[6,32]{1,0:T(8,128)S(1)}, u32[]{:S(2)}) copy-start(f32[6,32]{1,0:T(8,128)S(1)} %get-tuple-element.40) | copy-start | bytes 2308
  20.8 4.2 %copy-start.2 = (f32[16,4,1024]{2,1,0:T(4,128)S(1)}, f32[16,4,1024]{2,1,0:T(4,128)}, u32[]{:S(2)}) copy-start(f32[16,4,1024]{2,1,0:T(4,128)} %param.5) | copy-start | bytes 786436
  20.8 5.2 %copy-start.5 = (s32[2,4,1024]{2,1,0:T(4,128)S(1)}, s32[2,4,1024]{2,1,0:T(4,128)}, u32[]{:S(2)}) copy-start(s32[2,4,1024]{2,1,0:T(4,128)} %param.6) | copy-start | bytes 98308
  23.7 8.8 %collective-permute-start.2 = (f32[4,192,16]{2,1,0:T(8,128)}, f32[4,192,16]{2,1,0:T(8,128)}, u32[]{:S(2)}, u32[]{:S(2)}) collective-permute-start(f32[4,192,16]{2,1,0:T(8,128)} %get-tuple-element.27), channel_id=1, source_target_pairs={{0,1},{1,2},{2,3},{3,0},{4,5},{5,6},{6,7},{7,4},{8,9},{9,10},{10,1... | collective-permute-start | bytes 147464 | tf_op jit(solution)/shard_map/ppermute | solution.py:26
  25.0 11.2 %collective-permute-start.3 = (f32[4,192,16]{2,1,0:T(8,128)}, f32[4,192,16]{2,1,0:T(8,128)}, u32[]{:S(2)}, u32[]{:S(2)}) collective-permute-start(f32[4,192,16]{2,1,0:T(8,128)} %get-tuple-element.26), channel_id=1, source_target_pairs={{1,0},{2,1},{3,2},{0,3},{5,4},{6,5},{7,6},{4,7},{9,8},{10,9},{11,1... | collective-permute-start | bytes 147464 | tf_op jit(solution)/shard_map/ppermute | solution.py:29
  56.8 61.8 %copy-start.4 = (f32[6,32]{1,0:T(8,128)S(1)}, f32[6,32]{1,0:T(8,128)}, u32[]{:S(2)}) copy-start(f32[6,32]{1,0:T(8,128)} %copy-done.3) | copy-start | bytes 2308
  121.9 2.2 copy-start.1
  124.6 2.3 %collective-permute-start.4 = (f32[6,192,16]{1,2,0:T(8,128)S(1)}, f32[6,192,16]{1,2,0:T(8,128)S(1)}, u32[]{:S(2)}, u32[]{:S(2)}) collective-permute-start(f32[6,192,16]{1,2,0:T(8,128)S(1)} %copy.34), channel_id=1, source_target_pairs={{0,1},{1,2},{2,3},{3,0},{4,5},{5,6},{6,7},{7,4},{8,9},{9,10},{10,1... | collective-permute-start | bytes 221192 | tf_op jit(solution)/shard_map/ppermute | solution.py:26
  125.4 4.1 %collective-permute-start.5 = (f32[6,192,16]{1,2,0:T(8,128)S(1)}, f32[6,192,16]{1,2,0:T(8,128)S(1)}, u32[]{:S(2)}, u32[]{:S(2)}) collective-permute-start(f32[6,192,16]{1,2,0:T(8,128)S(1)} %copy.35), channel_id=1, source_target_pairs={{1,0},{2,1},{3,2},{0,3},{5,4},{6,5},{7,6},{4,7},{9,8},{10,9},{11,1... | collective-permute-start | bytes 221192 | tf_op jit(solution)/shard_map/ppermute | solution.py:29
  155.2 15.4 %collective-permute-start.6 = (f32[4,48,1024]{2,1,0:T(8,128)}, f32[4,48,1024]{2,1,0:T(8,128)}, u32[]{:S(2)}, u32[]{:S(2)}) collective-permute-start(f32[4,48,1024]{2,1,0:T(8,128)} %get-tuple-element.25), channel_id=1, source_target_pairs={{0,1},{1,2},{2,3},{3,0},{4,5},{5,6},{6,7},{7,4},{8,9},{9,10},{10,1... | collective-permute-start | bytes 2359304 | tf_op jit(solution)/shard_map/ppermute | solution.py:214
  155.2 34.9 %collective-permute-start.7 = (f32[4,48,1024]{2,1,0:T(8,128)}, f32[4,48,1024]{2,1,0:T(8,128)}, u32[]{:S(2)}, u32[]{:S(2)}) collective-permute-start(f32[4,48,1024]{2,1,0:T(8,128)} %get-tuple-element.24), channel_id=1, source_target_pairs={{0,2},{1,3},{2,0},{3,1},{4,6},{5,7},{6,4},{7,5},{8,10},{9,11},{10,... | collective-permute-start | bytes 2359304 | tf_op jit(solution)/shard_map/ppermute | solution.py:214
  156.4 39.4 %collective-permute-start.8 = (f32[4,48,1024]{2,1,0:T(8,128)}, f32[4,48,1024]{2,1,0:T(8,128)S(1)}, u32[]{:S(2)}, u32[]{:S(2)}) collective-permute-start(f32[4,48,1024]{2,1,0:T(8,128)} %get-tuple-element.23), channel_id=1, source_target_pairs={{0,3},{1,0},{2,1},{3,2},{4,7},{5,4},{6,5},{7,6},{8,11},{9,8},{10,9... | collective-permute-start | bytes 2359304 | tf_op jit(solution)/shard_map/ppermute | solution.py:214
where the time goes:
time: 231 us; the launch traced here: 230 us
  waiting for transfers between devices  94.2 us (41%)
  local copies, waits for them, and re-layouts  59 us (26%)
  Pallas kernels  25.3 us (11%)
  other arithmetic  22.1 us (10%)
  matrix products  18.2 us (8%)
  starting transfers between devices  10.2 us (4%)
    ppermute x3, waiting for transfers between devices, shifted(): lax.ppermute(lax.slice_in_dim(block, block.shape[dim] - width, None, axis...  62.7 us
    pallas_call x2, Pallas kernels, interpolate(): pl.pallas_call(functools.partial(interp_kernel, base is None, lat_rows),...  25.3 us
    ppermute x3, waiting for transfers between devices, on_device(): lax.ppermute(piece, 'lon', [(i, (i + shift) % parts) for i in range(parts)])  22.4 us
    reshape x8, local copies, waits for them, and re-layouts, spectrum(): piece.reshape(n_rows * n_items, per_piece, RADIX)  20.2 us
    dot_general x1, matrix products, spectrum(): partial_value = jnp.einsum('rab,ac->rbc', folded, table, precision=highest)  12.8 us
    unnamed x19, local copies, waits for them, and re-layouts  11.7 us
    concatenate x2, local copies, waits for them, and re-layouts, widen(): return jnp.concatenate([left, block, right], axis=block.ndim - 1)  11.2 us
    ppermute x3, waiting for transfers between devices, shifted(): lax.ppermute(lax.slice_in_dim(block, 0, width, axis=dim), axis, backward)  9.15 us
  transfers between devices with their start and end apart: 9, of which 8 were waited for; matrix products, arithmetic and copies ran while one was open for 15% of the time, Pallas kernels for 6%

commit v1 on v0

--- a/solution.py
+++ b/solution.py
@@ -173,6 +173,23 @@
     n_fields, n_levels, lat_rows, lon_cols = fields.shape
     n_items = n_fields * n_levels
     below_raw, above_raw = shifted(fields, "lat", ROWS_OUT, 2, False)
+    n_lat = lax.axis_size("lat")
+    n_lon = lax.axis_size("lon")
+
+    def diagonal(block, lat_step, lon_step):
+        pairs = []
+        for b in range(n_lat):
+            if 0 <= b + lat_step < n_lat:
+                for k in range(n_lon):
+                    pairs.append((b * n_lon + k, (b + lat_step) * n_lon + (k + lon_step) % n_lon))
+        return lax.ppermute(block, ("lat", "lon"), pairs)
+
+    low_rows = fields[:, :, lat_rows - ROWS_OUT :, :]
+    high_rows = fields[:, :, :ROWS_OUT, :]
+    below_left = diagonal(low_rows[..., lon_cols - HALO :], 1, 1)
+    below_right = diagonal(low_rows[..., :HALO], 1, -1)
+    above_left = diagonal(high_rows[..., lon_cols - HALO :], -1, 1)
+    above_right = diagonal(high_rows[..., :HALO], -1, -1)
 
     width = lon_cols + LANES
     local_rows = vertical_mix(jnp.transpose(fields, (2, 0, 1, 3)), bands)
@@ -197,9 +214,18 @@
     partial = interpolate(local_hi, local_lo, info, lat_rows, lon_cols)
 
     below_raw, above_raw, partial = lax.optimization_barrier((below_raw, above_raw, partial))
-    halo_raw = jnp.concatenate([below_raw, above_raw], axis=2)
+    below_left, below_right, above_left, above_right = lax.optimization_barrier(
+        (below_left, below_right, above_left, above_right)
+    )
+    halo_raw = jnp.concatenate(
+        [
+            jnp.concatenate([below_left, below_raw, below_right], axis=3),
+            jnp.concatenate([above_left, above_raw, above_right], axis=3),
+        ],
+        axis=2,
+    )
     halo_rows = vertical_mix(jnp.transpose(halo_raw, (2, 0, 1, 3)), bands)
-    halo_hi, halo_lo = split_rows(widen(halo_rows.reshape(2 * ROWS_OUT, n_items, lon_cols)), width)
+    halo_hi, halo_lo = split_rows(halo_rows.reshape(2 * ROWS_OUT, n_items, lon_cols + 2 * HALO), width)
     departed = interpolate(halo_hi, halo_lo, info, lat_rows, lon_cols, base=partial)
 
     parts = lax.axis_size("lon")

time: 231 us -> 275 us (1.19)
  the two profiles are of different devices: /device:TPU:11 before, /device:TPU:23 now
where the time goes in v1:
time: 275 us
  waiting for transfers between devices  127 us (46%)
  local copies, waits for them, and re-layouts  61.9 us (23%)
  Pallas kernels  25.3 us (9%)
  starting transfers between devices  23 us (8%)
  other arithmetic  18.4 us (7%)
  matrix products  18.2 us (7%)
    ppermute x4, waiting for transfers between devices, diagonal(): return lax.ppermute(block, ('lat', 'lon'), pairs)  103 us
    pallas_call x2, Pallas kernels, interpolate(): pl.pallas_call(functools.partial(interp_kernel, base is None, lat_rows),...  25.3 us
    ppermute x3, waiting for transfers between devices, on_device(): lax.ppermute(piece, 'lon', [(i, (i + shift) % parts) for i in range(parts)])  23.8 us
    reshape x8, local copies, waits for them, and re-layouts, spectrum(): piece.reshape(n_rows * n_items, per_piece, RADIX)  20.2 us
    ppermute x4, starting transfers between devices, diagonal(): return lax.ppermute(block, ('lat', 'lon'), pairs)  14.7 us
    unnamed x17, local copies, waits for them, and re-layouts  13.5 us
    dot_general x1, matrix products, spectrum(): partial_value = jnp.einsum('rab,ac->rbc', folded, table, precision=highest)  12.8 us
    add x2, other arithmetic, vertical_mix(): mixed + bands[lead + (slice(None), shift_k, slice(None), None)] * stacked...  6.05 us
  transfers between devices with their start and end apart: 11, of which 4 were waited for; matrix products, arithmetic and copies ran while one was open for 14% of the time, Pallas kernels for 5%

profile of v1, /device:TPU:23, one launch (start us, length us, event | category | flops | bytes accessed | tf_op | source)
XLA Modules:
  0.0 274.6 jit_solution(2799441168266942571)
XLA Ops:
  0.6 5.6 %fusion.80 = (f32[6,32,3,1024]{3,2,1,0:T(4,128)S(1)}, f32[6,32,3,1024]{3,2,1,0:T(4,128)S(1)}) fusion(f32[6,32,4,1024]{3,2,1,0:T(4,128)} %param.4), kind=kLoop, calls=%fused_computation.131 | loop fusion | bytes 9437184 | tf_op jit(solution)/shard_map/slice | solution.py:188
  6.3 2.8 %copy.48 = f32[6,32,3,1024]{3,1,2,0:T(8,128)} copy(f32[6,32,3,1024]{3,2,1,0:T(4,128)S(1)} %get-tuple-element.35) | data formatting | bytes 4718592
  9.1 3.1 %collective-permute-start.4 = (f32[6,32,3,1024]{3,1,2,0:T(8,128)}, f32[6,32,3,1024]{3,1,2,0:T(8,128)}, u32[]{:S(2)}, u32[]{:S(2)}) collective-permute-start(f32[6,32,3,1024]{3,1,2,0:T(8,128)} %copy.48), channel_id=1, source_target_pairs={{0,4},{4,8},{8,12},{12,16},{16,20},{20,24},{24,28},{1,5},{5,9},{9,... | collective-permute-start | bytes 7077896 | tf_op jit(solution)/shard_map/ppermute | solution.py:26
  12.3 2.7 copy.49
  15.0 2.1 collective-permute-start.5
  17.7 0.8 copy.44
  18.5 5.1 %collective-permute-start = (f32[6,32,3,16]{3,1,2,0:T(8,128)}, f32[6,32,3,16]{3,1,2,0:T(8,128)}, u32[]{:S(2)}, u32[]{:S(2)}) collective-permute-start(f32[6,32,3,16]{3,1,2,0:T(8,128)} %copy.44), channel_id=1, source_target_pairs={{0,5},{1,6},{2,7},{3,4},{4,9},{5,10},{6,11},{7,8},{8,13},{9,14},{1... | collective-permute-start | bytes 110600 | tf_op jit(solution)/shard_map/ppermute | solution.py:185
  23.6 0.8 copy.45
  24.3 2.8 %collective-permute-start.1 = (f32[6,32,3,16]{3,1,2,0:T(8,128)}, f32[6,32,3,16]{3,1,2,0:T(8,128)}, u32[]{:S(2)}, u32[]{:S(2)}) collective-permute-start(f32[6,32,3,16]{3,1,2,0:T(8,128)} %copy.45), channel_id=1, source_target_pairs={{0,7},{1,4},{2,5},{3,6},{4,11},{5,8},{6,9},{7,10},{8,15},{9,12},{1... | collective-permute-start | bytes 110600 | tf_op jit(solution)/shard_map/ppermute | solution.py:185
  27.2 0.8 copy.46
  27.9 3.6 %collective-permute-start.2 = (f32[6,32,3,16]{3,1,2,0:T(8,128)}, f32[6,32,3,16]{3,1,2,0:T(8,128)}, u32[]{:S(2)}, u32[]{:S(2)}) collective-permute-start(f32[6,32,3,16]{3,1,2,0:T(8,128)} %copy.46), channel_id=1, source_target_pairs={{4,1},{5,2},{6,3},{7,0},{8,5},{9,6},{10,7},{11,4},{12,9},{13,10},{... | collective-permute-start | bytes 110600 | tf_op jit(solution)/shard_map/ppermute | solution.py:185
  32.2 2.8 %multiply_add_fusion.1 = f32[4,6,32,1024]{3,0,2,1:T(4,128)S(1)} fusion(f32[4,6,32,1024]{3,0,2,1:T(4,128)S(1)} %bitcast.49, f32[6,32]{1,0:T(8,128)S(1)} %get-tuple-element.49, f32[6,32]{1,0:T(8,128)S(1)} %get-tuple-element.50, f32[6,32]{1,0:T(8,128)S(1)} %get-tuple-element.47, f32[6,32]{1,0:T(8,128)S(1)} %get-tuple-element.48, f32[6,32]{1,0:T(8,128)S(1)} %get-tuple-element.46), kind=kLoop, calls=%fused_computation.30 | loop fusion | flops 7077888 | bytes 6295296 | tf_op jit(solution)/shard_map/add | solution.py:154
  34.9 1.8 copy.33
  36.8 0.7 fusion.82
  37.5 1.0 fusion.79
  38.6 1.1 copy.67
  39.7 0.8 copy.47
  40.6 93.2 %collective-permute-done = f32[6,32,3,16]{3,1,2,0:T(8,128)} collective-permute-done((f32[6,32,3,16]{3,1,2,0:T(8,128)}, f32[6,32,3,16]{3,1,2,0:T(8,128)}, u32[]{:S(2)}, u32[]{:S(2)}) %collective-permute-start) | collective-permute-done | bytes 36896 | tf_op jit(solution)/shard_map/ppermute | solution.py:185
  134.3 3.2 %collective-permute-start.3 = (f32[6,32,3,16]{3,1,2,0:T(8,128)}, f32[6,32,3,16]{3,1,2,0:T(8,128)}, u32[]{:S(2)}, u32[]{:S(2)}) collective-permute-start(f32[6,32,3,16]{3,1,2,0:T(8,128)} %copy.47), channel_id=1, source_target_pairs={{4,3},{5,0},{6,1},{7,2},{8,7},{9,4},{10,5},{11,6},{12,11},{13,8},{... | collective-permute-start | bytes 110600 | tf_op jit(solution)/shard_map/ppermute | solution.py:185
  137.6 9.6 %collective-permute-done.3 = f32[6,32,3,16]{3,1,2,0:T(8,128)} collective-permute-done((f32[6,32,3,16]{3,1,2,0:T(8,128)}, f32[6,32,3,16]{3,1,2,0:T(8,128)}, u32[]{:S(2)}, u32[]{:S(2)}) %collective-permute-start.3) | collective-permute-done | bytes 36896 | tf_op jit(solution)/shard_map/ppermute | solution.py:185
  147.3 4.4 %concatenate.27 = f32[4,192,1056]{2,1,0:T(8,128)} concatenate(f32[4,192,16]{2,1,0:T(8,128)} %collective-permute-done.6, f32[4,192,1024]{2,1,0:T(8,128)S(1)} %bitcast.52, f32[4,192,16]{2,1,0:T(8,128)} %collective-permute-done.7), dimensions={2} | concatenate | bytes 6488064 | tf_op jit(solution)/shard_map/concatenate | solution.py:162
  151.7 2.6 fusion.17
  154.3 13.6 %shard_map.59.refs_3_ = f32[4,192,1024]{2,1,0:T(8,128)} custom-call(bf16[4,192,1152]{2,1,0:T(8,128)(2,1)S(1)} %get-tuple-element.27.refs_0_, bf16[4,192,1152]{2,1,0:T(8,128)(2,1)S(1)} %get-tuple-element.26.refs_1_, f32[4,24,1024]{2,1,0:T(8,128)S(1)} %maximum_maximum_fusion.refs_2_), custom_call_target="tpu_custom_call" | custom-call | tf_op jit(solution)/shard_map/pallas_call | solution.py:136
  167.9 3.3 %concatenate.29 = f32[6,32,3,1056]{3,1,2,0:T(8,128)S(1)} concatenate(f32[6,32,3,16]{3,1,2,0:T(8,128)} %collective-permute-done, f32[6,32,3,1024]{3,1,2,0:T(8,128)} %collective-permute-done.4, f32[6,32,3,16]{3,1,2,0:T(8,128)} %collective-permute-done.1), dimensions={3} | concatenate | bytes 4866048 | tf_op jit(solution)/shard_map/concatenate | solution.py:222
  171.2 4.5 %concatenate.30 = f32[6,32,3,1056]{3,1,2,0:T(8,128)} concatenate(f32[6,32,3,16]{3,1,2,0:T(8,128)} %collective-permute-done.2, f32[6,32,3,1024]{3,1,2,0:T(8,128)} %collective-permute-done.5, f32[6,32,3,16]{3,1,2,0:T(8,128)} %collective-permute-done.3), dimensions={3} | concatenate | bytes 4866048 | tf_op jit(solution)/shard_map/concatenate | solution.py:223
  175.8 2.1 maximum_bitcast_fusion
  177.9 3.3 %fusion.12 = f32[6,6,32,1056]{3,2,0,1:T(8,128)S(1)} fusion(f32[6,6,32,1056]{3,2,0,1:T(8,128)S(1)} %maximum_bitcast_fusion, f32[6,32]{1,0:T(8,128)S(1)} %get-tuple-element.49, f32[6,32]{1,0:T(8,128)S(1)} %copy-done.2, f32[6,32]{1,0:T(8,128)S(1)} %get-tuple-element.47, f32[6,32]{1,0:T(8,128)S(1)} %get-tuple-element.48, f32[6,32]{1,0:T(8,128)S(1)} %get-tuple-element.46), kind=kLoop, calls=%fused_computation.21 | loop fusion | flops 10948608 | bytes 9735936 | tf_op jit(solution)/shard_map/add | solution.py:154
  181.6 1.1 fusion.16
  182.7 11.7 %shard_map.60 = f32[4,192,1024]{2,1,0:T(8,128)} custom-call(bf16[6,192,1152]{2,1,0:T(8,128)(2,1)S(1)} %get-tuple-element.23.refs_0_, bf16[6,192,1152]{2,1,0:T(8,128)(2,1)S(1)} %get-tuple-element.22.refs_1_, f32[4,24,1024]{2,1,0:T(8,128)S(1)} %maximum_maximum_fusion.refs_2_, f32[4,192,1024]{2,1,0:T(8,128)} %shard_map.59.refs_3_), custom_call_target="tpu_custom_call" | custom-call | tf_op jit(solution)/shard_map/pallas_call | solution.py:136
  194.4 3.3 %constant_dynamic-slice_fusion.3 = (f32[4,48,1024]{2,1,0:T(8,128)S(1)}, f32[4,48,1024]{2,1,0:T(8,128)}, f32[4,48,1024]{2,1,0:T(8,128)}, f32[4,48,1024]{2,1,0:T(8,128)}) fusion(f32[4,192,1024]{2,1,0:T(8,128)} %shard_map.60, s32[]{:T(128)S(6)} %select_n.73, s32[]{:T(128)S(6)} %select_n.76, s32[]{:T(128)S(6)} %select_n.75, s32[]{:T(128)S(6)} %select_n.74), kind=kLoop, calls=%fused_computation.118 | loop fusion | bytes 6291472 | tf_op jit(solution)/shard_map/dynamic_slice | solution.py:238
  197.7 1.3 collective-permute-start.8
  199.0 1.2 collective-permute-start.9
  201.0 4.0 %copy.38 = f32[192,16,64]{1,2,0:T(8,128)} copy(f32[192,16,64]{2,1,0:T(8,128)S(1)} %reshape.182) | data formatting | bytes 1572864 | tf_op jit(solution)/shard_map/reshape | solution.py:44
  205.1 11.0 %collective-permute-done.8 = f32[4,48,1024]{2,1,0:T(8,128)} collective-permute-done((f32[4,48,1024]{2,1,0:T(8,128)}, f32[4,48,1024]{2,1,0:T(8,128)}, u32[]{:S(2)}, u32[]{:S(2)}) %collective-permute-start.8) | collective-permute-done | bytes 786464 | tf_op jit(solution)/shard_map/ppermute | solution.py:240
  216.1 1.6 reshape.183
  217.7 4.1 %copy.39 = f32[192,16,64]{1,2,0:T(8,128)} copy(f32[192,16,64]{2,1,0:T(8,128)S(1)} %reshape.183) | data formatting | bytes 1572864 | tf_op jit(solution)/shard_map/reshape | solution.py:44
  221.8 12.8 %collective-permute-done.9 = f32[4,48,1024]{2,1,0:T(8,128)} collective-permute-done((f32[4,48,1024]{2,1,0:T(8,128)}, f32[4,48,1024]{2,1,0:T(8,128)}, u32[]{:S(2)}, u32[]{:S(2)}) %collective-permute-start.9) | collective-permute-done | bytes 786464 | tf_op jit(solution)/shard_map/ppermute | solution.py:240
  234.6 1.6 reshape.184
  236.2 4.1 %copy.40 = f32[192,16,64]{1,2,0:T(8,128)} copy(f32[192,16,64]{2,1,0:T(8,128)S(1)} %reshape.184) | data formatting | bytes 1572864 | tf_op jit(solution)/shard_map/reshape | solution.py:44
  240.7 4.0 %copy.41 = f32[192,16,64]{1,2,0:T(8,128)} copy(f32[192,16,64]{2,1,0:T(8,128)S(1)} %reshape.185) | data formatting | bytes 1572864 | tf_op jit(solution)/shard_map/reshape | solution.py:44
  244.7 12.8 %fusion = f32[192,64,128]{2,1,0:T(8,128)S(1)} fusion(f32[192,16,64]{1,2,0:T(8,128)} %copy.41, f32[192,16,64]{1,2,0:T(8,128)} %copy.40, f32[192,16,64]{1,2,0:T(8,128)} %copy.39, f32[192,16,64]{1,2,0:T(8,128)} %copy.38, f32[16,128]{1,0:T(8,128)S(1)} %get-tuple-element.43, f32[16,128]{1,0:T(8,128)S(1)} %get-tuple-element.42, ...), kind=kOutput, calls=%fused_computation.6 | convolution fusion | flops 606363648 | bytes 9469952 | tf_op jit(solution)/shard_map/rab,ac->rbc/dot_general | solution.py:50
  257.5 3.3 %multiply_add_fusion = (f32[192,64,64]{2,1,0:T(8,128)S(1)}, f32[192,64,64]{2,1,0:T(8,128)S(1)}) fusion(f32[192,64,128]{2,1,0:T(8,128)S(1)} %fusion, f32[64,64]{1,0:T(8,128)S(1)} %get-tuple-element.55, f32[64,64]{1,0:T(8,128)S(1)} %get-tuple-element.56), kind=kLoop, calls=%fused_computation.16 | loop fusion | flops 4718592 | bytes 12615680 | tf_op jit(solution)/shard_map/add | solution.py:62
  260.8 2.7 fusion.23
  263.5 2.7 fusion.24
  266.2 2.7 fusion.19
  268.9 2.0 reshape.186
  270.9 1.6 copy.42
  273.0 1.6 copy.43
  (33 shorter events, 4.1 us)
Async XLA Ops:
  6.3 10.9 %copy-start = (f32[6,32,4,1024]{3,2,1,0:T(4,128)S(1)}, f32[6,32,4,1024]{3,2,1,0:T(4,128)}, u32[]{:S(2)}) copy-start(f32[6,32,4,1024]{3,2,1,0:T(4,128)} %param.4) | copy-start | bytes 9437188
  9.1 158.8 %collective-permute-start.4 = (f32[6,32,3,1024]{3,1,2,0:T(8,128)}, f32[6,32,3,1024]{3,1,2,0:T(8,128)}, u32[]{:S(2)}, u32[]{:S(2)}) collective-permute-start(f32[6,32,3,1024]{3,1,2,0:T(8,128)} %copy.48), channel_id=1, source_target_pairs={{0,4},{4,8},{8,12},{12,16},{16,20},{20,24},{24,28},{1,5},{5,9},{9,... | collective-permute-start | bytes 7077896 | tf_op jit(solution)/shard_map/ppermute | solution.py:26
  12.3 19.3 %copy-start.3 = (f32[6,5,32]{2,0,1:T(8,128)S(1)}, f32[6,5,32]{2,0,1:T(8,128)}, u32[]{:S(2)}) copy-start(f32[6,5,32]{2,0,1:T(8,128)} %param.7) | copy-start | bytes 11524
  15.0 152.9 %collective-permute-start.5 = (f32[6,32,3,1024]{3,1,2,0:T(8,128)}, f32[6,32,3,1024]{3,1,2,0:T(8,128)}, u32[]{:S(2)}, u32[]{:S(2)}) collective-permute-start(f32[6,32,3,1024]{3,1,2,0:T(8,128)} %copy.49), channel_id=1, source_target_pairs={{4,0},{8,4},{12,8},{16,12},{20,16},{24,20},{28,24},{5,1},{9,5},{13... | collective-permute-start | bytes 7077896 | tf_op jit(solution)/shard_map/ppermute | solution.py:29
  18.5 115.3 %collective-permute-start = (f32[6,32,3,16]{3,1,2,0:T(8,128)}, f32[6,32,3,16]{3,1,2,0:T(8,128)}, u32[]{:S(2)}, u32[]{:S(2)}) collective-permute-start(f32[6,32,3,16]{3,1,2,0:T(8,128)} %copy.44), channel_id=1, source_target_pairs={{0,5},{1,6},{2,7},{3,4},{4,9},{5,10},{6,11},{7,8},{8,13},{9,14},{1... | collective-permute-start | bytes 110600 | tf_op jit(solution)/shard_map/ppermute | solution.py:185
  24.3 109.5 %collective-permute-start.1 = (f32[6,32,3,16]{3,1,2,0:T(8,128)}, f32[6,32,3,16]{3,1,2,0:T(8,128)}, u32[]{:S(2)}, u32[]{:S(2)}) collective-permute-start(f32[6,32,3,16]{3,1,2,0:T(8,128)} %copy.45), channel_id=1, source_target_pairs={{0,7},{1,4},{2,5},{3,6},{4,11},{5,8},{6,9},{7,10},{8,15},{9,12},{1... | collective-permute-start | bytes 110600 | tf_op jit(solution)/shard_map/ppermute | solution.py:185
  27.9 106.4 %collective-permute-start.2 = (f32[6,32,3,16]{3,1,2,0:T(8,128)}, f32[6,32,3,16]{3,1,2,0:T(8,128)}, u32[]{:S(2)}, u32[]{:S(2)}) collective-permute-start(f32[6,32,3,16]{3,1,2,0:T(8,128)} %copy.46), channel_id=1, source_target_pairs={{4,1},{5,2},{6,3},{7,0},{8,5},{9,6},{10,7},{11,4},{12,9},{13,10},{... | collective-permute-start | bytes 110600 | tf_op jit(solution)/shard_map/ppermute | solution.py:185
  31.6 0.6 copy-start.1
  133.8 13.5 %collective-permute-start.6 = (f32[4,192,16]{2,1,0:T(8,128)}, f32[4,192,16]{2,1,0:T(8,128)}, u32[]{:S(2)}, u32[]{:S(2)}) collective-permute-start(f32[4,192,16]{2,1,0:T(8,128)} %get-tuple-element.33), channel_id=1, source_target_pairs={{0,1},{1,2},{2,3},{3,0},{4,5},{5,6},{6,7},{7,4},{8,9},{9,10},{10,1... | collective-permute-start | bytes 147464 | tf_op jit(solution)/shard_map/ppermute | solution.py:26
  133.8 13.5 %collective-permute-start.7 = (f32[4,192,16]{2,1,0:T(8,128)}, f32[4,192,16]{2,1,0:T(8,128)}, u32[]{:S(2)}, u32[]{:S(2)}) collective-permute-start(f32[4,192,16]{2,1,0:T(8,128)} %get-tuple-element.32), channel_id=1, source_target_pairs={{1,0},{2,1},{3,2},{0,3},{5,4},{6,5},{7,6},{4,7},{9,8},{10,9},{11,1... | collective-permute-start | bytes 147464 | tf_op jit(solution)/shard_map/ppermute | solution.py:29
  134.3 12.9 %collective-permute-start.3 = (f32[6,32,3,16]{3,1,2,0:T(8,128)}, f32[6,32,3,16]{3,1,2,0:T(8,128)}, u32[]{:S(2)}, u32[]{:S(2)}) collective-permute-start(f32[6,32,3,16]{3,1,2,0:T(8,128)} %copy.47), channel_id=1, source_target_pairs={{4,3},{5,0},{6,1},{7,2},{8,7},{9,4},{10,5},{11,6},{12,11},{13,8},{... | collective-permute-start | bytes 110600 | tf_op jit(solution)/shard_map/ppermute | solution.py:185
  175.8 2.1 copy-start.2
  197.7 18.4 %collective-permute-start.8 = (f32[4,48,1024]{2,1,0:T(8,128)}, f32[4,48,1024]{2,1,0:T(8,128)}, u32[]{:S(2)}, u32[]{:S(2)}) collective-permute-start(f32[4,48,1024]{2,1,0:T(8,128)} %get-tuple-element.31), channel_id=1, source_target_pairs={{0,1},{1,2},{2,3},{3,0},{4,5},{5,6},{6,7},{7,4},{8,9},{9,10},{10,1... | collective-permute-start | bytes 2359304 | tf_op jit(solution)/shard_map/ppermute | solution.py:240
  199.0 35.6 %collective-permute-start.9 = (f32[4,48,1024]{2,1,0:T(8,128)}, f32[4,48,1024]{2,1,0:T(8,128)}, u32[]{:S(2)}, u32[]{:S(2)}) collective-permute-start(f32[4,48,1024]{2,1,0:T(8,128)} %get-tuple-element.30), channel_id=1, source_target_pairs={{0,2},{1,3},{2,0},{3,1},{4,6},{5,7},{6,4},{7,5},{8,10},{9,11},{10,... | collective-permute-start | bytes 2359304 | tf_op jit(solution)/shard_map/ppermute | solution.py:240
  200.2 40.1 %collective-permute-start.10 = (f32[4,48,1024]{2,1,0:T(8,128)}, f32[4,48,1024]{2,1,0:T(8,128)S(1)}, u32[]{:S(2)}, u32[]{:S(2)}) collective-permute-start(f32[4,48,1024]{2,1,0:T(8,128)} %get-tuple-element.29), channel_id=1, source_target_pairs={{0,3},{1,0},{2,1},{3,2},{4,7},{5,4},{6,5},{7,6},{8,11},{9,8},{10,9... | collective-permute-start | bytes 2359304 | tf_op jit(solution)/shard_map/ppermute | solution.py:240

commit v2 on v1

--- a/solution.py
+++ b/solution.py
@@ -213,10 +213,10 @@
     )
     partial = interpolate(local_hi, local_lo, info, lat_rows, lon_cols)
 
-    below_raw, above_raw, partial = lax.optimization_barrier((below_raw, above_raw, partial))
-    below_left, below_right, above_left, above_right = lax.optimization_barrier(
-        (below_left, below_right, above_left, above_right)
-    )
+    below_raw, above_raw, corners, partial = lax.optimization_barrier(
+        (below_raw, above_raw, (below_left, below_right, above_left, above_right), partial)
+    )
+    below_left, below_right, above_left, above_right = corners
     halo_raw = jnp.concatenate(
         [
             jnp.concatenate([below_left, below_raw, below_right], axis=3),

time: 275 us -> 264 us (0.960)
  the two profiles are of different devices: /device:TPU:23 before, /device:TPU:17 now
where the time goes in v2:
time: 264 us; the launch traced here: 263 us
  waiting for transfers between devices  92.1 us (35%)
  local copies, waits for them, and re-layouts  64.4 us (24%)
  starting transfers between devices  42.9 us (16%)
  Pallas kernels  25.3 us (10%)
  other arithmetic  19.4 us (7%)
  matrix products  18.2 us (7%)
    ppermute x4, waiting for transfers between devices, diagonal(): return lax.ppermute(block, ('lat', 'lon'), pairs)  68.3 us
    pallas_call x2, Pallas kernels, interpolate(): pl.pallas_call(functools.partial(interp_kernel, base is None, lat_rows),...  25.3 us
    ppermute x3, waiting for transfers between devices, on_device(): lax.ppermute(piece, 'lon', [(i, (i + shift) % parts) for i in range(parts)])  23.8 us
    ppermute x3, starting transfers between devices, on_device(): lax.ppermute(piece, 'lon', [(i, (i + shift) % parts) for i in range(parts)])  21.3 us
    reshape x8, local copies, waits for them, and re-layouts, spectrum(): piece.reshape(n_rows * n_items, per_piece, RADIX)  20.3 us
    unnamed x21, local copies, waits for them, and re-layouts  15.6 us
    ppermute x4, starting transfers between devices, diagonal(): return lax.ppermute(block, ('lat', 'lon'), pairs)  13.1 us
    dot_general x1, matrix products, spectrum(): partial_value = jnp.einsum('rab,ac->rbc', folded, table, precision=highest)  12.8 us
  transfers between devices with their start and end apart: 11, of which 5 were waited for; matrix products, arithmetic and copies ran while one was open for 16% of the time, Pallas kernels for 5%

profile of v2, /device:TPU:17, one launch (start us, length us, event | category | flops | bytes accessed | tf_op | source)
XLA Modules:
  0.0 263.3 jit_solution(7310624943258137663)
XLA Ops:
  0.6 5.6 %fusion.81 = (f32[6,32,3,1024]{3,2,1,0:T(4,128)S(1)}, f32[6,32,3,1024]{3,2,1,0:T(4,128)S(1)}) fusion(f32[6,32,4,1024]{3,2,1,0:T(4,128)} %param.4), kind=kLoop, calls=%fused_computation.132 | loop fusion | bytes 9437184 | tf_op jit(solution)/shard_map/slice | solution.py:29
  6.3 2.8 %copy.44 = f32[6,32,3,1024]{3,1,2,0:T(8,128)} copy(f32[6,32,3,1024]{3,2,1,0:T(4,128)S(1)} %get-tuple-element.39) | data formatting | bytes 4718592
  9.1 3.1 %collective-permute-start = (f32[6,32,3,1024]{3,1,2,0:T(8,128)}, f32[6,32,3,1024]{3,1,2,0:T(8,128)}, u32[]{:S(2)}, u32[]{:S(2)}) collective-permute-start(f32[6,32,3,1024]{3,1,2,0:T(8,128)} %copy.44), channel_id=1, source_target_pairs={{0,4},{4,8},{8,12},{12,16},{16,20},{20,24},{24,28},{1,5},{5,9},{9,... | collective-permute-start | bytes 7077896 | tf_op jit(solution)/shard_map/ppermute | solution.py:26
  12.3 2.7 %copy.45 = f32[6,32,3,1024]{3,1,2,0:T(8,128)} copy(f32[6,32,3,1024]{3,2,1,0:T(4,128)S(1)} %get-tuple-element.38) | data formatting | bytes 4718592
  15.0 3.0 %collective-permute-start.1 = (f32[6,32,3,1024]{3,1,2,0:T(8,128)}, f32[6,32,3,1024]{3,1,2,0:T(8,128)}, u32[]{:S(2)}, u32[]{:S(2)}) collective-permute-start(f32[6,32,3,1024]{3,1,2,0:T(8,128)} %copy.45), channel_id=1, source_target_pairs={{4,0},{8,4},{12,8},{16,12},{20,16},{24,20},{28,24},{5,1},{9,5},{13... | collective-permute-start | bytes 7077896 | tf_op jit(solution)/shard_map/ppermute | solution.py:29
  18.1 2.8 %multiply_add_fusion.1 = f32[4,6,32,1024]{3,0,2,1:T(4,128)S(1)} fusion(f32[4,6,32,1024]{3,0,2,1:T(4,128)S(1)} %bitcast.49, f32[6,32]{1,0:T(8,128)S(1)} %get-tuple-element.49, f32[6,32]{1,0:T(8,128)S(1)} %get-tuple-element.50, f32[6,32]{1,0:T(8,128)S(1)} %get-tuple-element.47, f32[6,32]{1,0:T(8,128)S(1)} %get-tuple-element.48, f32[6,32]{1,0:T(8,128)S(1)} %get-tuple-element.46), kind=kLoop, calls=%fused_computation.30 | loop fusion | flops 7077888 | bytes 6295296 | tf_op jit(solution)/shard_map/add | solution.py:154
  20.9 1.8 copy.33
  23.8 2.3 collective-permute-start.6
  26.1 1.5 fusion.80
  28.4 3.7 %collective-permute-start.2 = (f32[6,32,3,16]{3,1,2,0:T(8,128)}, f32[6,32,3,16]{3,1,2,0:T(8,128)}, u32[]{:S(2)}, u32[]{:S(2)}) collective-permute-start(f32[6,32,3,16]{3,1,2,0:T(8,128)} %copy.46), channel_id=1, source_target_pairs={{0,5},{1,6},{2,7},{3,4},{4,9},{5,10},{6,11},{7,8},{8,13},{9,14},{1... | collective-permute-start | bytes 110600 | tf_op jit(solution)/shard_map/ppermute | solution.py:185
  33.2 1.1 maximum_maximum_fusion.refs_2_
  34.3 1.7 copy.47
  36.0 1.7 copy.48
  37.7 1.7 copy.49
  39.5 2.9 %collective-permute-start.3 = (f32[6,32,3,16]{3,1,2,0:T(8,128)}, f32[6,32,3,16]{3,1,2,0:T(8,128)}, u32[]{:S(2)}, u32[]{:S(2)}) collective-permute-start(f32[6,32,3,16]{3,1,2,0:T(8,128)} %copy.47), channel_id=1, source_target_pairs={{0,7},{1,4},{2,5},{3,6},{4,11},{5,8},{6,9},{7,10},{8,15},{9,12},{1... | collective-permute-start | bytes 110600 | tf_op jit(solution)/shard_map/ppermute | solution.py:185
  42.3 4.5 %collective-permute-start.4 = (f32[6,32,3,16]{3,1,2,0:T(8,128)}, f32[6,32,3,16]{3,1,2,0:T(8,128)}, u32[]{:S(2)}, u32[]{:S(2)}) collective-permute-start(f32[6,32,3,16]{3,1,2,0:T(8,128)} %copy.48), channel_id=1, source_target_pairs={{4,1},{5,2},{6,3},{7,0},{8,5},{9,6},{10,7},{11,4},{12,9},{13,10},{... | collective-permute-start | bytes 110600 | tf_op jit(solution)/shard_map/ppermute | solution.py:185
  46.8 4.4 %concatenate.27 = f32[4,192,1056]{2,1,0:T(8,128)} concatenate(f32[4,192,16]{2,1,0:T(8,128)} %collective-permute-done.6, f32[4,192,1024]{2,1,0:T(8,128)S(1)} %bitcast.52, f32[4,192,16]{2,1,0:T(8,128)} %collective-permute-done.7), dimensions={2} | concatenate | bytes 6488064 | tf_op jit(solution)/shard_map/concatenate | solution.py:162
  51.2 25.4 %collective-permute-done.2 = f32[6,32,3,16]{3,1,2,0:T(8,128)} collective-permute-done((f32[6,32,3,16]{3,1,2,0:T(8,128)}, f32[6,32,3,16]{3,1,2,0:T(8,128)}, u32[]{:S(2)}, u32[]{:S(2)}) %collective-permute-start.2) | collective-permute-done | bytes 36896 | tf_op jit(solution)/shard_map/ppermute | solution.py:185
  76.6 2.1 collective-permute-start.5
  78.7 2.6 %fusion.17 = (bf16[4,192,1152]{2,1,0:T(8,128)(2,1)S(1)}, bf16[4,192,1152]{2,1,0:T(8,128)(2,1)S(1)}) fusion(f32[4,192,1056]{2,1,0:T(8,128)} %concatenate.27), kind=kLoop, calls=%fused_computation.29 | loop fusion | flops 3538944 | bytes 6782976 | tf_op jit(solution)/shard_map/convert_element_type | solution.py:169
  81.4 13.6 %shard_map.59.refs_3_ = f32[4,192,1024]{2,1,0:T(8,128)} custom-call(bf16[4,192,1152]{2,1,0:T(8,128)(2,1)S(1)} %get-tuple-element.27.refs_0_, bf16[4,192,1152]{2,1,0:T(8,128)(2,1)S(1)} %get-tuple-element.26.refs_1_, f32[4,24,1024]{2,1,0:T(8,128)S(1)} %maximum_maximum_fusion.refs_2_), custom_call_target="tpu_custom_call" | custom-call | tf_op jit(solution)/shard_map/pallas_call | solution.py:136
  95.0 40.2 %collective-permute-done.3 = f32[6,32,3,16]{3,1,2,0:T(8,128)} collective-permute-done((f32[6,32,3,16]{3,1,2,0:T(8,128)}, f32[6,32,3,16]{3,1,2,0:T(8,128)}, u32[]{:S(2)}, u32[]{:S(2)}) %collective-permute-start.3) | collective-permute-done | bytes 36896 | tf_op jit(solution)/shard_map/ppermute | solution.py:185
  135.2 2.7 %collective-permute-done.4 = f32[6,32,3,16]{3,1,2,0:T(8,128)} collective-permute-done((f32[6,32,3,16]{3,1,2,0:T(8,128)}, f32[6,32,3,16]{3,1,2,0:T(8,128)}, u32[]{:S(2)}, u32[]{:S(2)}) %collective-permute-start.4) | collective-permute-done | bytes 36896 | tf_op jit(solution)/shard_map/ppermute | solution.py:185
  137.9 3.3 %concatenate.29 = f32[6,32,3,1056]{3,1,2,0:T(8,128)S(1)} concatenate(f32[6,32,3,16]{3,1,2,0:T(8,128)} %collective-permute-done.2, f32[6,32,3,1024]{3,1,2,0:T(8,128)} %collective-permute-done, f32[6,32,3,16]{3,1,2,0:T(8,128)} %collective-permute-done.3), dimensions={3} | concatenate | bytes 4866048 | tf_op jit(solution)/shard_map/concatenate | solution.py:222
  141.2 4.6 %concatenate.30 = f32[6,32,3,1056]{3,1,2,0:T(8,128)} concatenate(f32[6,32,3,16]{3,1,2,0:T(8,128)} %collective-permute-done.4, f32[6,32,3,1024]{3,1,2,0:T(8,128)} %collective-permute-done.1, f32[6,32,3,16]{3,1,2,0:T(8,128)S(1)} %collective-permute-done.5), dimensions={3} | concatenate | bytes 4866048 | tf_op jit(solution)/shard_map/concatenate | solution.py:223
  145.8 2.1 maximum_bitcast_fusion
  147.9 3.3 %fusion.12 = f32[6,6,32,1056]{3,2,0,1:T(8,128)S(1)} fusion(f32[6,6,32,1056]{3,2,0,1:T(8,128)S(1)} %maximum_bitcast_fusion, f32[6,32]{1,0:T(8,128)S(1)} %get-tuple-element.49, f32[6,32]{1,0:T(8,128)S(1)} %copy-done.3, f32[6,32]{1,0:T(8,128)S(1)} %get-tuple-element.47, f32[6,32]{1,0:T(8,128)S(1)} %get-tuple-element.48, f32[6,32]{1,0:T(8,128)S(1)} %get-tuple-element.46), kind=kLoop, calls=%fused_computation.21 | loop fusion | flops 10948608 | bytes 9735936 | tf_op jit(solution)/shard_map/add | solution.py:154
  151.6 1.1 fusion.16
  152.7 11.7 %shard_map.60 = f32[4,192,1024]{2,1,0:T(8,128)} custom-call(bf16[6,192,1152]{2,1,0:T(8,128)(2,1)S(1)} %get-tuple-element.23.refs_0_, bf16[6,192,1152]{2,1,0:T(8,128)(2,1)S(1)} %get-tuple-element.22.refs_1_, f32[4,24,1024]{2,1,0:T(8,128)S(1)} %maximum_maximum_fusion.refs_2_, f32[4,192,1024]{2,1,0:T(8,128)} %shard_map.59.refs_3_), custom_call_target="tpu_custom_call" | custom-call | tf_op jit(solution)/shard_map/pallas_call | solution.py:136
  164.4 3.3 %constant_dynamic-slice_fusion.3 = (f32[4,48,1024]{2,1,0:T(8,128)S(1)}, f32[4,48,1024]{2,1,0:T(8,128)}, f32[4,48,1024]{2,1,0:T(8,128)}, f32[4,48,1024]{2,1,0:T(8,128)}) fusion(f32[4,192,1024]{2,1,0:T(8,128)} %shard_map.60, s32[]{:T(128)S(6)} %select_n.73, s32[]{:T(128)S(6)} %select_n.76, s32[]{:T(128)S(6)} %select_n.75, s32[]{:T(128)S(6)} %select_n.74), kind=kLoop, calls=%fused_computation.118 | loop fusion | bytes 6291472 | tf_op jit(solution)/shard_map/dynamic_slice | solution.py:238
  167.7 20.1 %collective-permute-start.8 = (f32[4,48,1024]{2,1,0:T(8,128)}, f32[4,48,1024]{2,1,0:T(8,128)}, u32[]{:S(2)}, u32[]{:S(2)}) collective-permute-start(f32[4,48,1024]{2,1,0:T(8,128)} %get-tuple-element.31), channel_id=1, source_target_pairs={{0,1},{1,2},{2,3},{3,0},{4,5},{5,6},{6,7},{7,4},{8,9},{9,10},{10,1... | collective-permute-start | bytes 2359304 | tf_op jit(solution)/shard_map/ppermute | solution.py:240
  187.8 1.2 collective-permute-start.9
  189.8 4.1 %copy.38 = f32[192,16,64]{1,2,0:T(8,128)} copy(f32[192,16,64]{2,1,0:T(8,128)S(1)} %reshape.182) | data formatting | bytes 1572864 | tf_op jit(solution)/shard_map/reshape | solution.py:44
  193.9 11.0 %collective-permute-done.8 = f32[4,48,1024]{2,1,0:T(8,128)} collective-permute-done((f32[4,48,1024]{2,1,0:T(8,128)}, f32[4,48,1024]{2,1,0:T(8,128)}, u32[]{:S(2)}, u32[]{:S(2)}) %collective-permute-start.8) | collective-permute-done | bytes 786464 | tf_op jit(solution)/shard_map/ppermute | solution.py:240
  204.9 1.6 reshape.183
  206.5 4.1 %copy.39 = f32[192,16,64]{1,2,0:T(8,128)} copy(f32[192,16,64]{2,1,0:T(8,128)S(1)} %reshape.183) | data formatting | bytes 1572864 | tf_op jit(solution)/shard_map/reshape | solution.py:44
  210.6 12.8 %collective-permute-done.9 = f32[4,48,1024]{2,1,0:T(8,128)} collective-permute-done((f32[4,48,1024]{2,1,0:T(8,128)}, f32[4,48,1024]{2,1,0:T(8,128)}, u32[]{:S(2)}, u32[]{:S(2)}) %collective-permute-start.9) | collective-permute-done | bytes 786464 | tf_op jit(solution)/shard_map/ppermute | solution.py:240
  223.4 1.6 reshape.184
  225.0 4.0 %copy.40 = f32[192,16,64]{1,2,0:T(8,128)} copy(f32[192,16,64]{2,1,0:T(8,128)S(1)} %reshape.184) | data formatting | bytes 1572864 | tf_op jit(solution)/shard_map/reshape | solution.py:44
  229.5 4.0 %copy.41 = f32[192,16,64]{1,2,0:T(8,128)} copy(f32[192,16,64]{2,1,0:T(8,128)S(1)} %reshape.185) | data formatting | bytes 1572864 | tf_op jit(solution)/shard_map/reshape | solution.py:44
  233.5 12.8 %fusion = f32[192,64,128]{2,1,0:T(8,128)S(1)} fusion(f32[192,16,64]{1,2,0:T(8,128)} %copy.41, f32[192,16,64]{1,2,0:T(8,128)} %copy.40, f32[192,16,64]{1,2,0:T(8,128)} %copy.39, f32[192,16,64]{1,2,0:T(8,128)} %copy.38, f32[16,128]{1,0:T(8,128)S(1)} %get-tuple-element.43, f32[16,128]{1,0:T(8,128)S(1)} %get-tuple-element.42, ...), kind=kOutput, calls=%fused_computation.6 | convolution fusion | flops 606363648 | bytes 9469952 | tf_op jit(solution)/shard_map/rab,ac->rbc/dot_general | solution.py:50
  246.3 3.3 %multiply_add_fusion = (f32[192,64,64]{2,1,0:T(8,128)S(1)}, f32[192,64,64]{2,1,0:T(8,128)S(1)}) fusion(f32[192,64,128]{2,1,0:T(8,128)S(1)} %fusion, f32[64,64]{1,0:T(8,128)S(1)} %get-tuple-element.55, f32[64,64]{1,0:T(8,128)S(1)} %get-tuple-element.56), kind=kLoop, calls=%fused_computation.16 | loop fusion | flops 4718592 | bytes 12615680 | tf_op jit(solution)/shard_map/add | solution.py:62
  249.6 2.7 %fusion.23 = f32[192,20,128]{2,1,0:T(8,128)S(1)} fusion(f32[192,64,64]{2,1,0:T(8,128)S(1)} %get-tuple-element.21, f32[192,64,64]{2,1,0:T(8,128)S(1)} %get-tuple-element.20), kind=kOutput, calls=%fused_computation.39 | convolution fusion | flops 190334464 | bytes 8257536 | tf_op jit(solution)/shard_map/rbc,bq->rqc/dot_general | solution.py:68
  252.3 2.7 %fusion.24 = f32[192,20,128]{2,1,0:T(8,128)S(1)} fusion(f32[192,64,64]{2,1,0:T(8,128)S(1)} %get-tuple-element.21, f32[192,64,64]{2,1,0:T(8,128)S(1)} %get-tuple-element.20), kind=kOutput, calls=%fused_computation.40 | convolution fusion | flops 190334464 | bytes 8257536 | tf_op jit(solution)/shard_map/rbc,bq->rqc/dot_general | solution.py:69
  255.0 2.7 %fusion.19 = (f32[192,20,64]{2,1,0:T(8,128)S(1)}, f32[192,20,64]{2,1,0:T(8,128)}) fusion(f32[192,20,128]{2,1,0:T(8,128)S(1)} %fusion.24, f32[192,20,128]{2,1,0:T(8,128)S(1)} %fusion.23), kind=kLoop, calls=%fused_computation.34 | loop fusion | flops 983040 | bytes 5898240 | tf_op jit(solution)/shard_map/mul | solution.py:72
  257.7 2.0 reshape.186
  259.7 1.6 copy.42
  261.8 1.6 copy.43
  (37 shorter events, 5.0 us)
Async XLA Ops:
  6.3 11.8 %copy-start.5 = (f32[6,5,32]{2,0,1:T(8,128)S(1)}, f32[6,5,32]{2,0,1:T(8,128)}, u32[]{:S(2)}) copy-start(f32[6,5,32]{2,0,1:T(8,128)} %param.7) | copy-start | bytes 11524
  6.3 11.8 %copy-start = (f32[6,32,4,1024]{3,2,1,0:T(4,128)S(1)}, f32[6,32,4,1024]{3,2,1,0:T(4,128)}, u32[]{:S(2)}) copy-start(f32[6,32,4,1024]{3,2,1,0:T(4,128)} %param.4) | copy-start | bytes 9437188
  9.1 128.8 %collective-permute-start = (f32[6,32,3,1024]{3,1,2,0:T(8,128)}, f32[6,32,3,1024]{3,1,2,0:T(8,128)}, u32[]{:S(2)}, u32[]{:S(2)}) collective-permute-start(f32[6,32,3,1024]{3,1,2,0:T(8,128)} %copy.44), channel_id=1, source_target_pairs={{0,4},{4,8},{8,12},{12,16},{16,20},{20,24},{24,28},{1,5},{5,9},{9,... | collective-permute-start | bytes 7077896 | tf_op jit(solution)/shard_map/ppermute | solution.py:26
  15.0 122.9 %collective-permute-start.1 = (f32[6,32,3,1024]{3,1,2,0:T(8,128)}, f32[6,32,3,1024]{3,1,2,0:T(8,128)}, u32[]{:S(2)}, u32[]{:S(2)}) collective-permute-start(f32[6,32,3,1024]{3,1,2,0:T(8,128)} %copy.45), channel_id=1, source_target_pairs={{4,0},{8,4},{12,8},{16,12},{20,16},{24,20},{28,24},{5,1},{9,5},{13... | collective-permute-start | bytes 7077896 | tf_op jit(solution)/shard_map/ppermute | solution.py:29
  18.1 4.7 %copy-start.2 = (f32[6,32]{1,0:T(8,128)}, f32[6,32]{1,0:T(8,128)S(1)}, u32[]{:S(2)}) copy-start(f32[6,32]{1,0:T(8,128)S(1)} %get-tuple-element.50) | copy-start | bytes 2308
  20.9 11.2 %copy-start.1 = (f32[16,4,1024]{2,1,0:T(4,128)S(1)}, f32[16,4,1024]{2,1,0:T(4,128)}, u32[]{:S(2)}) copy-start(f32[16,4,1024]{2,1,0:T(4,128)} %param.5) | copy-start | bytes 786436
  20.9 12.2 %copy-start.4 = (s32[2,4,1024]{2,1,0:T(4,128)S(1)}, s32[2,4,1024]{2,1,0:T(4,128)}, u32[]{:S(2)}) copy-start(s32[2,4,1024]{2,1,0:T(4,128)} %param.6) | copy-start | bytes 98308
  23.8 15.7 %collective-permute-start.6 = (f32[4,192,16]{2,1,0:T(8,128)}, f32[4,192,16]{2,1,0:T(8,128)}, u32[]{:S(2)}, u32[]{:S(2)}) collective-permute-start(f32[4,192,16]{2,1,0:T(8,128)} %get-tuple-element.33), channel_id=1, source_target_pairs={{0,1},{1,2},{2,3},{3,0},{4,5},{5,6},{6,7},{7,4},{8,9},{9,10},{10,1... | collective-permute-start | bytes 147464 | tf_op jit(solution)/shard_map/ppermute | solution.py:26
  26.1 16.2 %collective-permute-start.7 = (f32[4,192,16]{2,1,0:T(8,128)}, f32[4,192,16]{2,1,0:T(8,128)}, u32[]{:S(2)}, u32[]{:S(2)}) collective-permute-start(f32[4,192,16]{2,1,0:T(8,128)} %get-tuple-element.32), channel_id=1, source_target_pairs={{1,0},{2,1},{3,2},{0,3},{5,4},{6,5},{7,6},{4,7},{9,8},{10,9},{11,1... | collective-permute-start | bytes 147464 | tf_op jit(solution)/shard_map/ppermute | solution.py:29
  28.4 48.2 %collective-permute-start.2 = (f32[6,32,3,16]{3,1,2,0:T(8,128)}, f32[6,32,3,16]{3,1,2,0:T(8,128)}, u32[]{:S(2)}, u32[]{:S(2)}) collective-permute-start(f32[6,32,3,16]{3,1,2,0:T(8,128)} %copy.46), channel_id=1, source_target_pairs={{0,5},{1,6},{2,7},{3,4},{4,9},{5,10},{6,11},{7,8},{8,13},{9,14},{1... | collective-permute-start | bytes 110600 | tf_op jit(solution)/shard_map/ppermute | solution.py:185
  39.5 95.7 %collective-permute-start.3 = (f32[6,32,3,16]{3,1,2,0:T(8,128)}, f32[6,32,3,16]{3,1,2,0:T(8,128)}, u32[]{:S(2)}, u32[]{:S(2)}) collective-permute-start(f32[6,32,3,16]{3,1,2,0:T(8,128)} %copy.47), channel_id=1, source_target_pairs={{0,7},{1,4},{2,5},{3,6},{4,11},{5,8},{6,9},{7,10},{8,15},{9,12},{1... | collective-permute-start | bytes 110600 | tf_op jit(solution)/shard_map/ppermute | solution.py:185
  42.3 95.5 %collective-permute-start.4 = (f32[6,32,3,16]{3,1,2,0:T(8,128)}, f32[6,32,3,16]{3,1,2,0:T(8,128)}, u32[]{:S(2)}, u32[]{:S(2)}) collective-permute-start(f32[6,32,3,16]{3,1,2,0:T(8,128)} %copy.48), channel_id=1, source_target_pairs={{4,1},{5,2},{6,3},{7,0},{8,5},{9,6},{10,7},{11,4},{12,9},{13,10},{... | collective-permute-start | bytes 110600 | tf_op jit(solution)/shard_map/ppermute | solution.py:185
  76.6 61.3 %collective-permute-start.5 = (f32[6,32,3,16]{3,1,2,0:T(8,128)}, f32[6,32,3,16]{3,1,2,0:T(8,128)S(1)}, u32[]{:S(2)}, u32[]{:S(2)}) collective-permute-start(f32[6,32,3,16]{3,1,2,0:T(8,128)} %copy.49), channel_id=1, source_target_pairs={{4,3},{5,0},{6,1},{7,2},{8,7},{9,4},{10,5},{11,6},{12,11},{13,8},{... | collective-permute-start | bytes 110600 | tf_op jit(solution)/shard_map/ppermute | solution.py:185
  145.8 2.1 copy-start.3
  167.7 37.2 %collective-permute-start.8 = (f32[4,48,1024]{2,1,0:T(8,128)}, f32[4,48,1024]{2,1,0:T(8,128)}, u32[]{:S(2)}, u32[]{:S(2)}) collective-permute-start(f32[4,48,1024]{2,1,0:T(8,128)} %get-tuple-element.31), channel_id=1, source_target_pairs={{0,1},{1,2},{2,3},{3,0},{4,5},{5,6},{6,7},{7,4},{8,9},{9,10},{10,1... | collective-permute-start | bytes 2359304 | tf_op jit(solution)/shard_map/ppermute | solution.py:240
  187.8 35.6 %collective-permute-start.9 = (f32[4,48,1024]{2,1,0:T(8,128)}, f32[4,48,1024]{2,1,0:T(8,128)}, u32[]{:S(2)}, u32[]{:S(2)}) collective-permute-start(f32[4,48,1024]{2,1,0:T(8,128)} %get-tuple-element.30), channel_id=1, source_target_pairs={{0,2},{1,3},{2,0},{3,1},{4,6},{5,7},{6,4},{7,5},{8,10},{9,11},{10,... | collective-permute-start | bytes 2359304 | tf_op jit(solution)/shard_map/ppermute | solution.py:240
  189.0 40.1 %collective-permute-start.10 = (f32[4,48,1024]{2,1,0:T(8,128)}, f32[4,48,1024]{2,1,0:T(8,128)S(1)}, u32[]{:S(2)}, u32[]{:S(2)}) collective-permute-start(f32[4,48,1024]{2,1,0:T(8,128)} %get-tuple-element.29), channel_id=1, source_target_pairs={{0,3},{1,0},{2,1},{3,2},{4,7},{5,4},{6,5},{7,6},{8,11},{9,8},{10,9... | collective-permute-start | bytes 2359304 | tf_op jit(solution)/shard_map/ppermute | solution.py:240

commit v3 on v0

--- a/solution.py
+++ b/solution.py
@@ -40,14 +40,11 @@
     )
     first_table = jnp.concatenate([jnp.cos(angle_one), -jnp.sin(angle_one)], axis=1)
     per_piece = piece_len // RADIX
-    folded = jnp.concatenate(
-        [piece.reshape(n_rows * n_items, per_piece, RADIX) for piece in pieces], axis=1
-    )
-    table = jnp.concatenate(
-        [lax.dynamic_slice_in_dim(first_table, owner * per_piece, per_piece, axis=0) for owner in owners],
-        axis=0,
-    )
-    partial_value = jnp.einsum("rab,ac->rbc", folded, table, precision=highest)
+    folded = jnp.stack([piece.reshape(n_rows * n_items, per_piece, RADIX) for piece in pieces])
+    table = jnp.stack(
+        [lax.dynamic_slice_in_dim(first_table, owner * per_piece, per_piece, axis=0) for owner in owners]
+    )
+    partial_value = jnp.einsum("prab,pac->rbc", folded, table, precision=highest)
     angle_two = (
         2.0
         * math.pi

time: 231 us -> 222 us (0.961)
  the two profiles are of different devices: /device:TPU:11 before, /device:TPU:24 now
where the time goes in v3:
time: 222 us; the launch traced here: 221 us
  waiting for transfers between devices  104 us (47%)
  local copies, waits for them, and re-layouts  46.2 us (21%)
  Pallas kernels  25.3 us (11%)
  other arithmetic  22.1 us (10%)
  matrix products  12.9 us (6%)
  starting transfers between devices  10.3 us (5%)
    ppermute x3, waiting for transfers between devices, shifted(): lax.ppermute(lax.slice_in_dim(block, 0, width, axis=dim), axis, backward)  60.2 us
    ppermute x3, waiting for transfers between devices, on_device(): lax.ppermute(piece, 'lon', [(i, (i + shift) % parts) for i in range(parts)])  31.6 us
    pallas_call x2, Pallas kernels, interpolate(): pl.pallas_call(functools.partial(interp_kernel, base is None, lat_rows),...  25.3 us
    unnamed x19, local copies, waits for them, and re-layouts  11.8 us
    ppermute x3, waiting for transfers between devices, shifted(): lax.ppermute(lax.slice_in_dim(block, block.shape[dim] - width, None, axis...  11.7 us
    concatenate x2, local copies, waits for them, and re-layouts, widen(): return jnp.concatenate([left, block, right], axis=block.ndim - 1)  11.2 us
    dot_general x1, matrix products, spectrum(): jnp.einsum('prab,pac->rbc', folded, table, precision=highest)  7.48 us
    another operation x4, local copies, waits for them, and re-layouts, spectrum(): jnp.stack([piece.reshape(n_rows * n_items, per_piece, RADIX) for piece in...  7.33 us
  transfers between devices with their start and end apart: 9, of which 8 were waited for; matrix products, arithmetic and copies ran while one was open for 11% of the time, Pallas kernels for 6%

profile of v3, /device:TPU:24, one launch (start us, length us, event | category | flops | bytes accessed | tf_op | source)
XLA Modules:
  0.0 221.2 jit_solution(6929657415632030161)
XLA Ops:
  0.6 5.7 %fusion.88 = (f32[6,32,3,1024]{3,2,1,0:T(4,128)S(1)}, f32[6,32,3,1024]{3,2,1,0:T(4,128)S(1)}) fusion(f32[6,32,4,1024]{3,2,1,0:T(4,128)} %param.4), kind=kLoop, calls=%fused_computation.137 | loop fusion | bytes 9437184 | tf_op jit(solution)/shard_map/slice | solution.py:29
  6.3 2.8 %copy.45 = f32[6,32,3,1024]{3,1,2,0:T(8,128)} copy(f32[6,32,3,1024]{3,2,1,0:T(4,128)S(1)} %get-tuple-element.29) | data formatting | bytes 4718592
  9.1 3.7 %collective-permute-start = (f32[6,32,3,1024]{3,1,2,0:T(8,128)}, f32[6,32,3,1024]{3,1,2,0:T(8,128)}, u32[]{:S(2)}, u32[]{:S(2)}) collective-permute-start(f32[6,32,3,1024]{3,1,2,0:T(8,128)} %copy.45), channel_id=1, source_target_pairs={{0,4},{4,8},{8,12},{12,16},{16,20},{20,24},{24,28},{1,5},{5,9},{9,... | collective-permute-start | bytes 7077896 | tf_op jit(solution)/shard_map/ppermute | solution.py:26
  12.8 2.8 %copy.46 = f32[6,32,3,1024]{3,1,2,0:T(8,128)} copy(f32[6,32,3,1024]{3,2,1,0:T(4,128)S(1)} %get-tuple-element.28) | data formatting | bytes 4718592
  15.6 3.3 %collective-permute-start.1 = (f32[6,32,3,1024]{3,1,2,0:T(8,128)}, f32[6,32,3,1024]{3,1,2,0:T(8,128)}, u32[]{:S(2)}, u32[]{:S(2)}) collective-permute-start(f32[6,32,3,1024]{3,1,2,0:T(8,128)} %copy.46), channel_id=1, source_target_pairs={{4,0},{8,4},{12,8},{16,12},{20,16},{24,20},{28,24},{5,1},{9,5},{13... | collective-permute-start | bytes 7077896 | tf_op jit(solution)/shard_map/ppermute | solution.py:29
  19.0 2.8 %multiply_add_fusion.1 = f32[4,6,32,1024]{3,0,2,1:T(4,128)S(1)} fusion(f32[4,6,32,1024]{3,0,2,1:T(4,128)S(1)} %bitcast.64, f32[6,32]{1,0:T(8,128)S(1)} %get-tuple-element.39, f32[6,32]{1,0:T(8,128)S(1)} %get-tuple-element.40, f32[6,32]{1,0:T(8,128)S(1)} %get-tuple-element.37, f32[6,32]{1,0:T(8,128)S(1)} %get-tuple-element.38, f32[6,32]{1,0:T(8,128)S(1)} %get-tuple-element.36), kind=kLoop, calls=%fused_computation.30 | loop fusion | flops 7077888 | bytes 6295296 | tf_op jit(solution)/shard_map/add | solution.py:151
  21.8 1.8 copy.29
  23.6 1.0 fusion.87
  24.6 0.4 collective-permute-start.3
  25.2 0.9 copy.64
  26.2 1.1 maximum_maximum_fusion.refs_2_
  27.3 7.1 %collective-permute-done.3 = f32[4,192,16]{2,1,0:T(8,128)} collective-permute-done((f32[4,192,16]{2,1,0:T(8,128)}, f32[4,192,16]{2,1,0:T(8,128)}, u32[]{:S(2)}, u32[]{:S(2)}) %collective-permute-start.3) | collective-permute-done | bytes 49184 | tf_op jit(solution)/shard_map/ppermute | solution.py:29
  34.4 2.1 collective-permute-done.2
  36.4 4.4 %concatenate.18 = f32[4,192,1056]{2,1,0:T(8,128)} concatenate(f32[4,192,16]{2,1,0:T(8,128)} %collective-permute-done.2, f32[4,192,1024]{2,1,0:T(8,128)S(1)} %bitcast.68, f32[4,192,16]{2,1,0:T(8,128)} %collective-permute-done.3), dimensions={2} | concatenate | bytes 6488064 | tf_op jit(solution)/shard_map/concatenate | solution.py:159
  40.8 2.6 %fusion.17 = (bf16[4,192,1152]{2,1,0:T(8,128)(2,1)S(1)}, bf16[4,192,1152]{2,1,0:T(8,128)(2,1)S(1)}) fusion(f32[4,192,1056]{2,1,0:T(8,128)} %concatenate.18), kind=kLoop, calls=%fused_computation.29 | loop fusion | flops 3538944 | bytes 6782976 | tf_op jit(solution)/shard_map/convert_element_type | solution.py:166
  43.4 13.6 %shard_map.59.refs_3_ = f32[4,192,1024]{2,1,0:T(8,128)} custom-call(bf16[4,192,1152]{2,1,0:T(8,128)(2,1)S(1)} %get-tuple-element.21.refs_0_, bf16[4,192,1152]{2,1,0:T(8,128)(2,1)S(1)} %get-tuple-element.20.refs_1_, f32[4,24,1024]{2,1,0:T(8,128)S(1)} %maximum_maximum_fusion.refs_2_), custom_call_target="tpu_custom_call" | custom-call | tf_op jit(solution)/shard_map/pallas_call | solution.py:133
  57.1 8.5 %collective-permute-done = f32[6,32,3,1024]{3,1,2,0:T(8,128)} collective-permute-done((f32[6,32,3,1024]{3,1,2,0:T(8,128)}, f32[6,32,3,1024]{3,1,2,0:T(8,128)}, u32[]{:S(2)}, u32[]{:S(2)}) %collective-permute-start) | collective-permute-done | bytes 2359328 | tf_op jit(solution)/shard_map/ppermute | solution.py:26
  65.6 50.5 %collective-permute-done.1 = f32[6,32,3,1024]{3,1,2,0:T(8,128)} collective-permute-done((f32[6,32,3,1024]{3,1,2,0:T(8,128)}, f32[6,32,3,1024]{3,1,2,0:T(8,128)}, u32[]{:S(2)}, u32[]{:S(2)}) %collective-permute-start.1) | collective-permute-done | bytes 2359328 | tf_op jit(solution)/shard_map/ppermute | solution.py:29
  116.0 2.8 %maximum_bitcast_fusion = f32[6,6,32,1024]{3,2,0,1:T(8,128)S(1)} fusion(f32[6,32,3,1024]{3,1,2,0:T(8,128)} %collective-permute-done.1, f32[6,32,3,1024]{3,1,2,0:T(8,128)} %collective-permute-done), kind=kLoop, calls=%fused_computation.28 | loop fusion | flops 1179648 | bytes 9437184 | tf_op jit(solution)/shard_map/transpose | solution.py:198
  118.8 2.9 %fusion.13 = f32[6,6,32,1024]{3,2,0,1:T(8,128)S(1)} fusion(f32[6,6,32,1024]{3,2,0,1:T(8,128)S(1)} %maximum_bitcast_fusion, f32[6,32]{1,0:T(8,128)S(1)} %get-tuple-element.39, f32[6,32]{1,0:T(8,128)S(1)} %copy-done.4, f32[6,32]{1,0:T(8,128)S(1)} %get-tuple-element.37, f32[6,32]{1,0:T(8,128)S(1)} %get-tuple-element.38, f32[6,32]{1,0:T(8,128)S(1)} %get-tuple-element.36), kind=kLoop, calls=%fused_computation.24 | loop fusion | flops 10616832 | bytes 9441024 | tf_op jit(solution)/shard_map/add | solution.py:151
  121.7 0.4 copy.33
  122.1 2.1 copy-done.1
  124.4 0.2 copy.35
  124.6 1.1 collective-permute-start.5
  126.1 2.7 %collective-permute-done.5 = f32[6,192,16]{1,2,0:T(8,128)S(1)} collective-permute-done((f32[6,192,16]{1,2,0:T(8,128)S(1)}, f32[6,192,16]{1,2,0:T(8,128)S(1)}, u32[]{:S(2)}, u32[]{:S(2)}) %collective-permute-start.5) | collective-permute-done | bytes 73760 | tf_op jit(solution)/shard_map/ppermute | solution.py:29
  129.0 1.1 collective-permute-done.4
  130.3 6.9 %concatenate.21 = f32[6,192,1056]{2,1,0:T(8,128)} concatenate(f32[6,192,16]{2,1,0:T(8,128)S(1)} %copy.36, f32[6,192,1024]{2,1,0:T(8,128)} %bitcast.66, f32[6,192,16]{2,1,0:T(8,128)S(1)} %copy.37), dimensions={2} | concatenate | bytes 9732096 | tf_op jit(solution)/shard_map/concatenate | solution.py:159
  137.2 3.6 %fusion.8 = (bf16[6,192,1152]{2,1,0:T(8,128)(2,1)S(1)}, bf16[6,192,1152]{2,1,0:T(8,128)(2,1)S(1)}) fusion(f32[6,192,1056]{2,1,0:T(8,128)} %concatenate.21), kind=kLoop, calls=%fused_computation.17 | loop fusion | flops 5308416 | bytes 10174464 | tf_op jit(solution)/shard_map/convert_element_type | solution.py:166
  140.7 11.6 %shard_map.60 = f32[4,192,1024]{2,1,0:T(8,128)} custom-call(bf16[6,192,1152]{2,1,0:T(8,128)(2,1)S(1)} %get-tuple-element.15.refs_0_, bf16[6,192,1152]{2,1,0:T(8,128)(2,1)S(1)} %get-tuple-element.14.refs_1_, f32[4,24,1024]{2,1,0:T(8,128)S(1)} %maximum_maximum_fusion.refs_2_, f32[4,192,1024]{2,1,0:T(8,128)} %shard_map.59.refs_3_), custom_call_target="tpu_custom_call" | custom-call | tf_op jit(solution)/shard_map/pallas_call | solution.py:133
  152.4 3.3 %constant_dynamic-slice_fusion.3 = (f32[4,48,1024]{2,1,0:T(8,128)S(1)}, f32[4,48,1024]{2,1,0:T(8,128)}, f32[4,48,1024]{2,1,0:T(8,128)}, f32[4,48,1024]{2,1,0:T(8,128)}) fusion(f32[4,192,1024]{2,1,0:T(8,128)} %shard_map.60, s32[]{:T(128)S(6)} %select_n.73, s32[]{:T(128)S(6)} %select_n.76, s32[]{:T(128)S(6)} %select_n.75, s32[]{:T(128)S(6)} %select_n.74), kind=kLoop, calls=%fused_computation.123 | loop fusion | bytes 6291472 | tf_op jit(solution)/shard_map/dynamic_slice | solution.py:209
  155.7 1.1 collective-permute-start.8
  156.8 0.3 collective-permute-start.7
  157.1 0.2 collective-permute-start.6
  157.7 0.4 stack_reshape.12
  158.1 16.9 %collective-permute-done.8 = f32[4,48,1024]{2,1,0:T(8,128)} collective-permute-done((f32[4,48,1024]{2,1,0:T(8,128)}, f32[4,48,1024]{2,1,0:T(8,128)}, u32[]{:S(2)}, u32[]{:S(2)}) %collective-permute-start.8) | collective-permute-done | bytes 786464 | tf_op jit(solution)/shard_map/ppermute | solution.py:211
  175.1 2.7 %stack_reshape.15 = f32[1,192,16,64]{3,2,1,0:T(8,128)} reshape(f32[4,48,1024]{2,1,0:T(8,128)} %collective-permute-done.8) | data formatting | bytes 1572864 | tf_op jit(solution)/shard_map/stack;reshape | solution.py:43
  177.7 14.7 %collective-permute-done.7 = f32[4,48,1024]{2,1,0:T(8,128)} collective-permute-done((f32[4,48,1024]{2,1,0:T(8,128)}, f32[4,48,1024]{2,1,0:T(8,128)}, u32[]{:S(2)}, u32[]{:S(2)}) %collective-permute-start.7) | collective-permute-done | bytes 786464 | tf_op jit(solution)/shard_map/ppermute | solution.py:211
  192.5 2.6 %stack_reshape.14 = f32[1,192,16,64]{3,2,1,0:T(8,128)} reshape(f32[4,48,1024]{2,1,0:T(8,128)} %collective-permute-done.7) | data formatting | bytes 1572864 | tf_op jit(solution)/shard_map/stack;reshape | solution.py:43
  195.1 1.6 stack_reshape.13
  196.7 7.5 %fusion.19 = f32[192,64,128]{2,1,0:T(8,128)S(1)} fusion(f32[1,192,16,64]{3,2,0,1:T(8,128)} %bitcast.72, f32[1,192,16,64]{3,2,0,1:T(8,128)} %bitcast.73, f32[1,192,16,64]{3,2,0,1:T(8,128)} %bitcast.74, f32[1,192,16,64]{3,2,0,1:T(8,128)S(1)} %bitcast.71, f32[1,16,128]{2,1,0:T(8,128)S(1)} %get-tuple-element.33, f32[1,16,128]{2,1,0:T(8,128)S(1)} %get-tuple-element.32, ...), kind=kOutput, calls=%fused_computation.33 | convolution fusion | flops 606363648 | bytes 9469952 | tf_op jit(solution)/shard_map/prab,pac->rbc/dot_general | solution.py:47
  204.2 3.3 %multiply_add_fusion = (f32[192,64,64]{2,1,0:T(8,128)S(1)}, f32[192,64,64]{2,1,0:T(8,128)S(1)}) fusion(f32[192,64,128]{2,1,0:T(8,128)S(1)} %fusion.19, f32[64,64]{1,0:T(8,128)S(1)} %get-tuple-element.45, f32[64,64]{1,0:T(8,128)S(1)} %get-tuple-element.46), kind=kLoop, calls=%fused_computation.16 | loop fusion | flops 4718592 | bytes 12615680 | tf_op jit(solution)/shard_map/add | solution.py:59
  207.5 2.7 %fusion.27 = f32[192,20,128]{2,1,0:T(8,128)S(1)} fusion(f32[192,64,64]{2,1,0:T(8,128)S(1)} %get-tuple-element.13, f32[192,64,64]{2,1,0:T(8,128)S(1)} %get-tuple-element.12), kind=kOutput, calls=%fused_computation.41 | convolution fusion | flops 190334464 | bytes 8257536 | tf_op jit(solution)/shard_map/rbc,bq->rqc/dot_general | solution.py:66
  210.2 2.7 %fusion.26 = f32[192,20,128]{2,1,0:T(8,128)S(1)} fusion(f32[192,64,64]{2,1,0:T(8,128)S(1)} %get-tuple-element.13, f32[192,64,64]{2,1,0:T(8,128)S(1)} %get-tuple-element.12), kind=kOutput, calls=%fused_computation.40 | convolution fusion | flops 190334464 | bytes 8257536 | tf_op jit(solution)/shard_map/rbc,bq->rqc/dot_general | solution.py:65
  212.9 2.7 %fusion.22 = (f32[192,20,64]{2,1,0:T(8,128)}, f32[192,20,64]{2,1,0:T(8,128)S(1)}) fusion(f32[192,20,128]{2,1,0:T(8,128)S(1)} %fusion.27, f32[192,20,128]{2,1,0:T(8,128)S(1)} %fusion.26), kind=kLoop, calls=%fused_computation.35 | loop fusion | flops 983040 | bytes 5898240 | tf_op jit(solution)/shard_map/mul | solution.py:69
  215.6 2.0 reshape.171
  217.6 1.6 copy.43
  219.2 0.5 reshape.170
  219.7 1.6 copy.42
  (30 shorter events, 1.7 us)
Async XLA Ops:
  9.1 9.8 %copy-start.6 = (f32[6,5,32]{2,0,1:T(8,128)S(1)}, f32[6,5,32]{2,0,1:T(8,128)}, u32[]{:S(2)}) copy-start(f32[6,5,32]{2,0,1:T(8,128)} %param.7) | copy-start | bytes 11524
  9.1 9.9 %copy-start = (f32[6,32,4,1024]{3,2,1,0:T(4,128)S(1)}, f32[6,32,4,1024]{3,2,1,0:T(4,128)}, u32[]{:S(2)}) copy-start(f32[6,32,4,1024]{3,2,1,0:T(4,128)} %param.4) | copy-start | bytes 9437188
  9.1 56.5 %collective-permute-start = (f32[6,32,3,1024]{3,1,2,0:T(8,128)}, f32[6,32,3,1024]{3,1,2,0:T(8,128)}, u32[]{:S(2)}, u32[]{:S(2)}) collective-permute-start(f32[6,32,3,1024]{3,1,2,0:T(8,128)} %copy.45), channel_id=1, source_target_pairs={{0,4},{4,8},{8,12},{12,16},{16,20},{20,24},{24,28},{1,5},{5,9},{9,... | collective-permute-start | bytes 7077896 | tf_op jit(solution)/shard_map/ppermute | solution.py:26
  15.6 100.4 %collective-permute-start.1 = (f32[6,32,3,1024]{3,1,2,0:T(8,128)}, f32[6,32,3,1024]{3,1,2,0:T(8,128)}, u32[]{:S(2)}, u32[]{:S(2)}) collective-permute-start(f32[6,32,3,1024]{3,1,2,0:T(8,128)} %copy.46), channel_id=1, source_target_pairs={{4,0},{8,4},{12,8},{16,12},{20,16},{24,20},{28,24},{5,1},{9,5},{13... | collective-permute-start | bytes 7077896 | tf_op jit(solution)/shard_map/ppermute | solution.py:29
  19.0 4.7 %copy-start.3 = (f32[6,32]{1,0:T(8,128)}, f32[6,32]{1,0:T(8,128)S(1)}, u32[]{:S(2)}) copy-start(f32[6,32]{1,0:T(8,128)S(1)} %get-tuple-element.40) | copy-start | bytes 2308
  21.8 3.4 %copy-start.2 = (f32[16,4,1024]{2,1,0:T(4,128)S(1)}, f32[16,4,1024]{2,1,0:T(4,128)}, u32[]{:S(2)}) copy-start(f32[16,4,1024]{2,1,0:T(4,128)} %param.5) | copy-start | bytes 786436
  21.8 4.3 %copy-start.5 = (s32[2,4,1024]{2,1,0:T(4,128)S(1)}, s32[2,4,1024]{2,1,0:T(4,128)}, u32[]{:S(2)}) copy-start(s32[2,4,1024]{2,1,0:T(4,128)} %param.6) | copy-start | bytes 98308
  24.6 9.7 %collective-permute-start.3 = (f32[4,192,16]{2,1,0:T(8,128)}, f32[4,192,16]{2,1,0:T(8,128)}, u32[]{:S(2)}, u32[]{:S(2)}) collective-permute-start(f32[4,192,16]{2,1,0:T(8,128)} %get-tuple-element.26), channel_id=1, source_target_pairs={{1,0},{2,1},{3,2},{0,3},{5,4},{6,5},{7,6},{4,7},{9,8},{10,9},{11,1... | collective-permute-start | bytes 147464 | tf_op jit(solution)/shard_map/ppermute | solution.py:29
  25.0 11.4 %collective-permute-start.2 = (f32[4,192,16]{2,1,0:T(8,128)}, f32[4,192,16]{2,1,0:T(8,128)}, u32[]{:S(2)}, u32[]{:S(2)}) collective-permute-start(f32[4,192,16]{2,1,0:T(8,128)} %get-tuple-element.27), channel_id=1, source_target_pairs={{0,1},{1,2},{2,3},{3,0},{4,5},{5,6},{6,7},{7,4},{8,9},{9,10},{10,1... | collective-permute-start | bytes 147464 | tf_op jit(solution)/shard_map/ppermute | solution.py:26
  57.1 61.7 %copy-start.4 = (f32[6,32]{1,0:T(8,128)S(1)}, f32[6,32]{1,0:T(8,128)}, u32[]{:S(2)}) copy-start(f32[6,32]{1,0:T(8,128)} %copy-done.3) | copy-start | bytes 2308
  122.1 2.1 copy-start.1
  124.6 4.1 %collective-permute-start.5 = (f32[6,192,16]{1,2,0:T(8,128)S(1)}, f32[6,192,16]{1,2,0:T(8,128)S(1)}, u32[]{:S(2)}, u32[]{:S(2)}) collective-permute-start(f32[6,192,16]{1,2,0:T(8,128)S(1)} %copy.35), channel_id=1, source_target_pairs={{1,0},{2,1},{3,2},{0,3},{5,4},{6,5},{7,6},{4,7},{9,8},{10,9},{11,1... | collective-permute-start | bytes 221192 | tf_op jit(solution)/shard_map/ppermute | solution.py:29
  126.0 4.1 %collective-permute-start.4 = (f32[6,192,16]{1,2,0:T(8,128)S(1)}, f32[6,192,16]{1,2,0:T(8,128)S(1)}, u32[]{:S(2)}, u32[]{:S(2)}) collective-permute-start(f32[6,192,16]{1,2,0:T(8,128)S(1)} %copy.34), channel_id=1, source_target_pairs={{0,1},{1,2},{2,3},{3,0},{4,5},{5,6},{6,7},{7,4},{8,9},{9,10},{10,1... | collective-permute-start | bytes 221192 | tf_op jit(solution)/shard_map/ppermute | solution.py:26
  155.7 19.3 %collective-permute-start.8 = (f32[4,48,1024]{2,1,0:T(8,128)}, f32[4,48,1024]{2,1,0:T(8,128)}, u32[]{:S(2)}, u32[]{:S(2)}) collective-permute-start(f32[4,48,1024]{2,1,0:T(8,128)} %get-tuple-element.23), channel_id=1, source_target_pairs={{0,3},{1,0},{2,1},{3,2},{4,7},{5,4},{6,5},{7,6},{8,11},{9,8},{10,9... | collective-permute-start | bytes 2359304 | tf_op jit(solution)/shard_map/ppermute | solution.py:211
  156.8 35.6 %collective-permute-start.7 = (f32[4,48,1024]{2,1,0:T(8,128)}, f32[4,48,1024]{2,1,0:T(8,128)}, u32[]{:S(2)}, u32[]{:S(2)}) collective-permute-start(f32[4,48,1024]{2,1,0:T(8,128)} %get-tuple-element.24), channel_id=1, source_target_pairs={{0,2},{1,3},{2,0},{3,1},{4,6},{5,7},{6,4},{7,5},{8,10},{9,11},{10,... | collective-permute-start | bytes 2359304 | tf_op jit(solution)/shard_map/ppermute | solution.py:211
  157.1 38.0 %collective-permute-start.6 = (f32[4,48,1024]{2,1,0:T(8,128)}, f32[4,48,1024]{2,1,0:T(8,128)S(1)}, u32[]{:S(2)}, u32[]{:S(2)}) collective-permute-start(f32[4,48,1024]{2,1,0:T(8,128)} %get-tuple-element.25), channel_id=1, source_target_pairs={{0,1},{1,2},{2,3},{3,0},{4,5},{5,6},{6,7},{7,4},{8,9},{9,10},{10,1... | collective-permute-start | bytes 2359304 | tf_op jit(solution)/shard_map/ppermute | solution.py:211

commit v4 on v3

--- a/solution.py
+++ b/solution.py
@@ -114,8 +114,8 @@
             m_lo = (matrix - m_hi.astype(jnp.float32)).astype(jnp.bfloat16)
             x_hi = hi_ref[index, :, pl.ds(start, WINDOW)]
             x_lo = lo_ref[index, :, pl.ds(start, WINDOW)]
-            acc = acc + jnp.dot(x_hi, m_hi, preferred_element_type=jnp.float32)
-            acc = acc + jnp.dot(x_hi, m_lo, preferred_element_type=jnp.float32)
+            both = jnp.dot(x_hi, jnp.concatenate([m_hi, m_lo], axis=1), preferred_element_type=jnp.float32)
+            acc = acc + both[:, :LANES] + both[:, LANES:]
             acc = acc + jnp.dot(x_lo, m_hi, preferred_element_type=jnp.float32)
         out_ref[row] = acc
 

time: 222 us -> 221 us (level)
  Pallas kernels: 25.3 us -> 20.6 us
  waiting for transfers between devices: 104 us -> 107 us
    pallas_call x2, Pallas kernels: 25.3 us -> 20.6 us  [interpolate(): pl.pallas_call(functools.partial(interp_kernel, base is None, lat_rows),...]
    ppermute x3, waiting for transfers between devices: 11.7 us -> 14.8 us  [shifted(): lax.ppermute(lax.slice_in_dim(block, block.shape[dim] - width, None, axis...]
  transfers between devices with their start and end apart: 9 -> 9, of which waited for: 8 -> 8; matrix products, arithmetic and copies ran while one was open for 11% -> 11% of each run, Pallas kernels for 6% -> 5%
where the time goes in v4:
time: 221 us; the launch traced here: 220 us
  waiting for transfers between devices  107 us (48%)
  local copies, waits for them, and re-layouts  46.2 us (21%)
  other arithmetic  22.1 us (10%)
  Pallas kernels  20.6 us (9%)
  matrix products  12.9 us (6%)
  starting transfers between devices  10.3 us (5%)
    ppermute x3, waiting for transfers between devices, shifted(): lax.ppermute(lax.slice_in_dim(block, 0, width, axis=dim), axis, backward)  60.2 us
    ppermute x3, waiting for transfers between devices, on_device(): lax.ppermute(piece, 'lon', [(i, (i + shift) % parts) for i in range(parts)])  31.6 us
    pallas_call x2, Pallas kernels, interpolate(): pl.pallas_call(functools.partial(interp_kernel, base is None, lat_rows),...  20.6 us
    ppermute x3, waiting for transfers between devices, shifted(): lax.ppermute(lax.slice_in_dim(block, block.shape[dim] - width, None, axis...  14.8 us
    unnamed x19, local copies, waits for them, and re-layouts  11.8 us
    concatenate x2, local copies, waits for them, and re-layouts, widen(): return jnp.concatenate([left, block, right], axis=block.ndim - 1)  11.2 us
    dot_general x1, matrix products, spectrum(): jnp.einsum('prab,pac->rbc', folded, table, precision=highest)  7.48 us
    another operation x4, local copies, waits for them, and re-layouts, spectrum(): jnp.stack([piece.reshape(n_rows * n_items, per_piece, RADIX) for piece in...  7.33 us
  transfers between devices with their start and end apart: 9, of which 8 were waited for; matrix products, arithmetic and copies ran while one was open for 11% of the time, Pallas kernels for 5%

profile of v4, /device:TPU:24, one launch (start us, length us, event | category | flops | bytes accessed | tf_op | source)
XLA Modules:
  0.0 219.6 jit_solution(15763583181753386527)
XLA Ops:
  0.6 5.7 %fusion.88 = (f32[6,32,3,1024]{3,2,1,0:T(4,128)S(1)}, f32[6,32,3,1024]{3,2,1,0:T(4,128)S(1)}) fusion(f32[6,32,4,1024]{3,2,1,0:T(4,128)} %param.4), kind=kLoop, calls=%fused_computation.137 | loop fusion | bytes 9437184 | tf_op jit(solution)/shard_map/slice | solution.py:29
  6.3 2.8 %copy.45 = f32[6,32,3,1024]{3,1,2,0:T(8,128)} copy(f32[6,32,3,1024]{3,2,1,0:T(4,128)S(1)} %get-tuple-element.29) | data formatting | bytes 4718592
  9.1 3.7 %collective-permute-start = (f32[6,32,3,1024]{3,1,2,0:T(8,128)}, f32[6,32,3,1024]{3,1,2,0:T(8,128)}, u32[]{:S(2)}, u32[]{:S(2)}) collective-permute-start(f32[6,32,3,1024]{3,1,2,0:T(8,128)} %copy.45), channel_id=1, source_target_pairs={{0,4},{4,8},{8,12},{12,16},{16,20},{20,24},{24,28},{1,5},{5,9},{9,... | collective-permute-start | bytes 7077896 | tf_op jit(solution)/shard_map/ppermute | solution.py:26
  12.8 2.8 %copy.46 = f32[6,32,3,1024]{3,1,2,0:T(8,128)} copy(f32[6,32,3,1024]{3,2,1,0:T(4,128)S(1)} %get-tuple-element.28) | data formatting | bytes 4718592
  15.6 3.3 %collective-permute-start.1 = (f32[6,32,3,1024]{3,1,2,0:T(8,128)}, f32[6,32,3,1024]{3,1,2,0:T(8,128)}, u32[]{:S(2)}, u32[]{:S(2)}) collective-permute-start(f32[6,32,3,1024]{3,1,2,0:T(8,128)} %copy.46), channel_id=1, source_target_pairs={{4,0},{8,4},{12,8},{16,12},{20,16},{24,20},{28,24},{5,1},{9,5},{13... | collective-permute-start | bytes 7077896 | tf_op jit(solution)/shard_map/ppermute | solution.py:29
  19.0 2.8 %multiply_add_fusion.1 = f32[4,6,32,1024]{3,0,2,1:T(4,128)S(1)} fusion(f32[4,6,32,1024]{3,0,2,1:T(4,128)S(1)} %bitcast.64, f32[6,32]{1,0:T(8,128)S(1)} %get-tuple-element.39, f32[6,32]{1,0:T(8,128)S(1)} %get-tuple-element.40, f32[6,32]{1,0:T(8,128)S(1)} %get-tuple-element.37, f32[6,32]{1,0:T(8,128)S(1)} %get-tuple-element.38, f32[6,32]{1,0:T(8,128)S(1)} %get-tuple-element.36), kind=kLoop, calls=%fused_computation.30 | loop fusion | flops 7077888 | bytes 6295296 | tf_op jit(solution)/shard_map/add | solution.py:151
  21.8 1.8 copy.29
  23.6 1.0 fusion.87
  24.6 0.4 collective-permute-start.3
  25.2 0.9 copy.64
  26.2 1.1 maximum_maximum_fusion.refs_2_
  27.3 7.1 %collective-permute-done.3 = f32[4,192,16]{2,1,0:T(8,128)} collective-permute-done((f32[4,192,16]{2,1,0:T(8,128)}, f32[4,192,16]{2,1,0:T(8,128)}, u32[]{:S(2)}, u32[]{:S(2)}) %collective-permute-start.3) | collective-permute-done | bytes 49184 | tf_op jit(solution)/shard_map/ppermute | solution.py:29
  34.4 2.1 collective-permute-done.2
  36.4 4.4 %concatenate.18 = f32[4,192,1056]{2,1,0:T(8,128)} concatenate(f32[4,192,16]{2,1,0:T(8,128)} %collective-permute-done.2, f32[4,192,1024]{2,1,0:T(8,128)S(1)} %bitcast.68, f32[4,192,16]{2,1,0:T(8,128)} %collective-permute-done.3), dimensions={2} | concatenate | bytes 6488064 | tf_op jit(solution)/shard_map/concatenate | solution.py:159
  40.8 2.6 %fusion.17 = (bf16[4,192,1152]{2,1,0:T(8,128)(2,1)S(1)}, bf16[4,192,1152]{2,1,0:T(8,128)(2,1)S(1)}) fusion(f32[4,192,1056]{2,1,0:T(8,128)} %concatenate.18), kind=kLoop, calls=%fused_computation.29 | loop fusion | flops 3538944 | bytes 6782976 | tf_op jit(solution)/shard_map/convert_element_type | solution.py:166
  43.4 10.5 %shard_map.59.refs_3_ = f32[4,192,1024]{2,1,0:T(8,128)} custom-call(bf16[4,192,1152]{2,1,0:T(8,128)(2,1)S(1)} %get-tuple-element.21.refs_0_, bf16[4,192,1152]{2,1,0:T(8,128)(2,1)S(1)} %get-tuple-element.20.refs_1_, f32[4,24,1024]{2,1,0:T(8,128)S(1)} %maximum_maximum_fusion.refs_2_), custom_call_target="tpu_custom_call" | custom-call | tf_op jit(solution)/shard_map/pallas_call | solution.py:133
  54.0 11.6 %collective-permute-done = f32[6,32,3,1024]{3,1,2,0:T(8,128)} collective-permute-done((f32[6,32,3,1024]{3,1,2,0:T(8,128)}, f32[6,32,3,1024]{3,1,2,0:T(8,128)}, u32[]{:S(2)}, u32[]{:S(2)}) %collective-permute-start) | collective-permute-done | bytes 2359328 | tf_op jit(solution)/shard_map/ppermute | solution.py:26
  65.6 50.5 %collective-permute-done.1 = f32[6,32,3,1024]{3,1,2,0:T(8,128)} collective-permute-done((f32[6,32,3,1024]{3,1,2,0:T(8,128)}, f32[6,32,3,1024]{3,1,2,0:T(8,128)}, u32[]{:S(2)}, u32[]{:S(2)}) %collective-permute-start.1) | collective-permute-done | bytes 2359328 | tf_op jit(solution)/shard_map/ppermute | solution.py:29
  116.0 2.8 %maximum_bitcast_fusion = f32[6,6,32,1024]{3,2,0,1:T(8,128)S(1)} fusion(f32[6,32,3,1024]{3,1,2,0:T(8,128)} %collective-permute-done.1, f32[6,32,3,1024]{3,1,2,0:T(8,128)} %collective-permute-done), kind=kLoop, calls=%fused_computation.28 | loop fusion | flops 1179648 | bytes 9437184 | tf_op jit(solution)/shard_map/transpose | solution.py:198
  118.8 2.9 %fusion.13 = f32[6,6,32,1024]{3,2,0,1:T(8,128)S(1)} fusion(f32[6,6,32,1024]{3,2,0,1:T(8,128)S(1)} %maximum_bitcast_fusion, f32[6,32]{1,0:T(8,128)S(1)} %get-tuple-element.39, f32[6,32]{1,0:T(8,128)S(1)} %copy-done.4, f32[6,32]{1,0:T(8,128)S(1)} %get-tuple-element.37, f32[6,32]{1,0:T(8,128)S(1)} %get-tuple-element.38, f32[6,32]{1,0:T(8,128)S(1)} %get-tuple-element.36), kind=kLoop, calls=%fused_computation.24 | loop fusion | flops 10616832 | bytes 9441024 | tf_op jit(solution)/shard_map/add | solution.py:151
  121.7 0.4 copy.33
  122.1 2.1 copy-done.1
  124.4 0.2 copy.35
  124.6 1.1 collective-permute-start.5
  125.8 0.2 copy.34
  126.1 2.7 %collective-permute-done.5 = f32[6,192,16]{1,2,0:T(8,128)S(1)} collective-permute-done((f32[6,192,16]{1,2,0:T(8,128)S(1)}, f32[6,192,16]{1,2,0:T(8,128)S(1)}, u32[]{:S(2)}, u32[]{:S(2)}) %collective-permute-start.5) | collective-permute-done | bytes 73760 | tf_op jit(solution)/shard_map/ppermute | solution.py:29
  129.0 1.1 collective-permute-done.4
  130.3 6.9 %concatenate.21 = f32[6,192,1056]{2,1,0:T(8,128)} concatenate(f32[6,192,16]{2,1,0:T(8,128)S(1)} %copy.36, f32[6,192,1024]{2,1,0:T(8,128)} %bitcast.66, f32[6,192,16]{2,1,0:T(8,128)S(1)} %copy.37), dimensions={2} | concatenate | bytes 9732096 | tf_op jit(solution)/shard_map/concatenate | solution.py:159
  137.2 3.6 %fusion.8 = (bf16[6,192,1152]{2,1,0:T(8,128)(2,1)S(1)}, bf16[6,192,1152]{2,1,0:T(8,128)(2,1)S(1)}) fusion(f32[6,192,1056]{2,1,0:T(8,128)} %concatenate.21), kind=kLoop, calls=%fused_computation.17 | loop fusion | flops 5308416 | bytes 10174464 | tf_op jit(solution)/shard_map/convert_element_type | solution.py:166
  140.7 10.1 %shard_map.60 = f32[4,192,1024]{2,1,0:T(8,128)} custom-call(bf16[6,192,1152]{2,1,0:T(8,128)(2,1)S(1)} %get-tuple-element.15.refs_0_, bf16[6,192,1152]{2,1,0:T(8,128)(2,1)S(1)} %get-tuple-element.14.refs_1_, f32[4,24,1024]{2,1,0:T(8,128)S(1)} %maximum_maximum_fusion.refs_2_, f32[4,192,1024]{2,1,0:T(8,128)} %shard_map.59.refs_3_), custom_call_target="tpu_custom_call" | custom-call | tf_op jit(solution)/shard_map/pallas_call | solution.py:133
  150.8 3.3 %constant_dynamic-slice_fusion.3 = (f32[4,48,1024]{2,1,0:T(8,128)S(1)}, f32[4,48,1024]{2,1,0:T(8,128)}, f32[4,48,1024]{2,1,0:T(8,128)}, f32[4,48,1024]{2,1,0:T(8,128)}) fusion(f32[4,192,1024]{2,1,0:T(8,128)} %shard_map.60, s32[]{:T(128)S(6)} %select_n.73, s32[]{:T(128)S(6)} %select_n.76, s32[]{:T(128)S(6)} %select_n.75, s32[]{:T(128)S(6)} %select_n.74), kind=kLoop, calls=%fused_computation.123 | loop fusion | bytes 6291472 | tf_op jit(solution)/shard_map/dynamic_slice | solution.py:209
  154.1 1.1 collective-permute-start.8
  155.2 0.3 collective-permute-start.7
  156.1 0.4 stack_reshape.12
  156.5 16.9 %collective-permute-done.8 = f32[4,48,1024]{2,1,0:T(8,128)} collective-permute-done((f32[4,48,1024]{2,1,0:T(8,128)}, f32[4,48,1024]{2,1,0:T(8,128)}, u32[]{:S(2)}, u32[]{:S(2)}) %collective-permute-start.8) | collective-permute-done | bytes 786464 | tf_op jit(solution)/shard_map/ppermute | solution.py:211
  173.5 2.7 %stack_reshape.15 = f32[1,192,16,64]{3,2,1,0:T(8,128)} reshape(f32[4,48,1024]{2,1,0:T(8,128)} %collective-permute-done.8) | data formatting | bytes 1572864 | tf_op jit(solution)/shard_map/stack;reshape | solution.py:43
  176.1 14.7 %collective-permute-done.7 = f32[4,48,1024]{2,1,0:T(8,128)} collective-permute-done((f32[4,48,1024]{2,1,0:T(8,128)}, f32[4,48,1024]{2,1,0:T(8,128)}, u32[]{:S(2)}, u32[]{:S(2)}) %collective-permute-start.7) | collective-permute-done | bytes 786464 | tf_op jit(solution)/shard_map/ppermute | solution.py:211
  190.8 2.6 %stack_reshape.14 = f32[1,192,16,64]{3,2,1,0:T(8,128)} reshape(f32[4,48,1024]{2,1,0:T(8,128)} %collective-permute-done.7) | data formatting | bytes 1572864 | tf_op jit(solution)/shard_map/stack;reshape | solution.py:43
  193.5 1.6 stack_reshape.13
  195.1 7.5 %fusion.19 = f32[192,64,128]{2,1,0:T(8,128)S(1)} fusion(f32[1,192,16,64]{3,2,0,1:T(8,128)} %bitcast.72, f32[1,192,16,64]{3,2,0,1:T(8,128)} %bitcast.73, f32[1,192,16,64]{3,2,0,1:T(8,128)} %bitcast.74, f32[1,192,16,64]{3,2,0,1:T(8,128)S(1)} %bitcast.71, f32[1,16,128]{2,1,0:T(8,128)S(1)} %get-tuple-element.33, f32[1,16,128]{2,1,0:T(8,128)S(1)} %get-tuple-element.32, ...), kind=kOutput, calls=%fused_computation.33 | convolution fusion | flops 606363648 | bytes 9469952 | tf_op jit(solution)/shard_map/prab,pac->rbc/dot_general | solution.py:47
  202.6 3.3 %multiply_add_fusion = (f32[192,64,64]{2,1,0:T(8,128)S(1)}, f32[192,64,64]{2,1,0:T(8,128)S(1)}) fusion(f32[192,64,128]{2,1,0:T(8,128)S(1)} %fusion.19, f32[64,64]{1,0:T(8,128)S(1)} %get-tuple-element.45, f32[64,64]{1,0:T(8,128)S(1)} %get-tuple-element.46), kind=kLoop, calls=%fused_computation.16 | loop fusion | flops 4718592 | bytes 12615680 | tf_op jit(solution)/shard_map/add | solution.py:59
  205.9 2.7 %fusion.27 = f32[192,20,128]{2,1,0:T(8,128)S(1)} fusion(f32[192,64,64]{2,1,0:T(8,128)S(1)} %get-tuple-element.13, f32[192,64,64]{2,1,0:T(8,128)S(1)} %get-tuple-element.12), kind=kOutput, calls=%fused_computation.41 | convolution fusion | flops 190334464 | bytes 8257536 | tf_op jit(solution)/shard_map/rbc,bq->rqc/dot_general | solution.py:66
  208.6 2.7 %fusion.26 = f32[192,20,128]{2,1,0:T(8,128)S(1)} fusion(f32[192,64,64]{2,1,0:T(8,128)S(1)} %get-tuple-element.13, f32[192,64,64]{2,1,0:T(8,128)S(1)} %get-tuple-element.12), kind=kOutput, calls=%fused_computation.40 | convolution fusion | flops 190334464 | bytes 8257536 | tf_op jit(solution)/shard_map/rbc,bq->rqc/dot_general | solution.py:65
  211.3 2.7 %fusion.22 = (f32[192,20,64]{2,1,0:T(8,128)}, f32[192,20,64]{2,1,0:T(8,128)S(1)}) fusion(f32[192,20,128]{2,1,0:T(8,128)S(1)} %fusion.27, f32[192,20,128]{2,1,0:T(8,128)S(1)} %fusion.26), kind=kLoop, calls=%fused_computation.35 | loop fusion | flops 983040 | bytes 5898240 | tf_op jit(solution)/shard_map/mul | solution.py:69
  214.0 2.0 reshape.171
  216.0 1.6 copy.43
  217.6 0.5 reshape.170
  218.1 1.6 copy.42
  (30 shorter events, 1.7 us)
Async XLA Ops:
  9.1 9.8 %copy-start.6 = (f32[6,5,32]{2,0,1:T(8,128)S(1)}, f32[6,5,32]{2,0,1:T(8,128)}, u32[]{:S(2)}) copy-start(f32[6,5,32]{2,0,1:T(8,128)} %param.7) | copy-start | bytes 11524
  9.1 9.9 %copy-start = (f32[6,32,4,1024]{3,2,1,0:T(4,128)S(1)}, f32[6,32,4,1024]{3,2,1,0:T(4,128)}, u32[]{:S(2)}) copy-start(f32[6,32,4,1024]{3,2,1,0:T(4,128)} %param.4) | copy-start | bytes 9437188
  9.1 56.5 %collective-permute-start = (f32[6,32,3,1024]{3,1,2,0:T(8,128)}, f32[6,32,3,1024]{3,1,2,0:T(8,128)}, u32[]{:S(2)}, u32[]{:S(2)}) collective-permute-start(f32[6,32,3,1024]{3,1,2,0:T(8,128)} %copy.45), channel_id=1, source_target_pairs={{0,4},{4,8},{8,12},{12,16},{16,20},{20,24},{24,28},{1,5},{5,9},{9,... | collective-permute-start | bytes 7077896 | tf_op jit(solution)/shard_map/ppermute | solution.py:26
  15.6 100.4 %collective-permute-start.1 = (f32[6,32,3,1024]{3,1,2,0:T(8,128)}, f32[6,32,3,1024]{3,1,2,0:T(8,128)}, u32[]{:S(2)}, u32[]{:S(2)}) collective-permute-start(f32[6,32,3,1024]{3,1,2,0:T(8,128)} %copy.46), channel_id=1, source_target_pairs={{4,0},{8,4},{12,8},{16,12},{20,16},{24,20},{28,24},{5,1},{9,5},{13... | collective-permute-start | bytes 7077896 | tf_op jit(solution)/shard_map/ppermute | solution.py:29
  19.0 4.7 %copy-start.3 = (f32[6,32]{1,0:T(8,128)}, f32[6,32]{1,0:T(8,128)S(1)}, u32[]{:S(2)}) copy-start(f32[6,32]{1,0:T(8,128)S(1)} %get-tuple-element.40) | copy-start | bytes 2308
  21.8 3.4 %copy-start.2 = (f32[16,4,1024]{2,1,0:T(4,128)S(1)}, f32[16,4,1024]{2,1,0:T(4,128)}, u32[]{:S(2)}) copy-start(f32[16,4,1024]{2,1,0:T(4,128)} %param.5) | copy-start | bytes 786436
  21.8 4.3 %copy-start.5 = (s32[2,4,1024]{2,1,0:T(4,128)S(1)}, s32[2,4,1024]{2,1,0:T(4,128)}, u32[]{:S(2)}) copy-start(s32[2,4,1024]{2,1,0:T(4,128)} %param.6) | copy-start | bytes 98308
  24.6 9.7 %collective-permute-start.3 = (f32[4,192,16]{2,1,0:T(8,128)}, f32[4,192,16]{2,1,0:T(8,128)}, u32[]{:S(2)}, u32[]{:S(2)}) collective-permute-start(f32[4,192,16]{2,1,0:T(8,128)} %get-tuple-element.26), channel_id=1, source_target_pairs={{1,0},{2,1},{3,2},{0,3},{5,4},{6,5},{7,6},{4,7},{9,8},{10,9},{11,1... | collective-permute-start | bytes 147464 | tf_op jit(solution)/shard_map/ppermute | solution.py:29
  25.0 11.4 %collective-permute-start.2 = (f32[4,192,16]{2,1,0:T(8,128)}, f32[4,192,16]{2,1,0:T(8,128)}, u32[]{:S(2)}, u32[]{:S(2)}) collective-permute-start(f32[4,192,16]{2,1,0:T(8,128)} %get-tuple-element.27), channel_id=1, source_target_pairs={{0,1},{1,2},{2,3},{3,0},{4,5},{5,6},{6,7},{7,4},{8,9},{9,10},{10,1... | collective-permute-start | bytes 147464 | tf_op jit(solution)/shard_map/ppermute | solution.py:26
  54.0 64.8 %copy-start.4 = (f32[6,32]{1,0:T(8,128)S(1)}, f32[6,32]{1,0:T(8,128)}, u32[]{:S(2)}) copy-start(f32[6,32]{1,0:T(8,128)} %copy-done.3) | copy-start | bytes 2308
  122.1 2.1 copy-start.1
  124.6 4.1 %collective-permute-start.5 = (f32[6,192,16]{1,2,0:T(8,128)S(1)}, f32[6,192,16]{1,2,0:T(8,128)S(1)}, u32[]{:S(2)}, u32[]{:S(2)}) collective-permute-start(f32[6,192,16]{1,2,0:T(8,128)S(1)} %copy.35), channel_id=1, source_target_pairs={{1,0},{2,1},{3,2},{0,3},{5,4},{6,5},{7,6},{4,7},{9,8},{10,9},{11,1... | collective-permute-start | bytes 221192 | tf_op jit(solution)/shard_map/ppermute | solution.py:29
  126.0 4.1 %collective-permute-start.4 = (f32[6,192,16]{1,2,0:T(8,128)S(1)}, f32[6,192,16]{1,2,0:T(8,128)S(1)}, u32[]{:S(2)}, u32[]{:S(2)}) collective-permute-start(f32[6,192,16]{1,2,0:T(8,128)S(1)} %copy.34), channel_id=1, source_target_pairs={{0,1},{1,2},{2,3},{3,0},{4,5},{5,6},{6,7},{7,4},{8,9},{9,10},{10,1... | collective-permute-start | bytes 221192 | tf_op jit(solution)/shard_map/ppermute | solution.py:26
  154.1 19.3 %collective-permute-start.8 = (f32[4,48,1024]{2,1,0:T(8,128)}, f32[4,48,1024]{2,1,0:T(8,128)}, u32[]{:S(2)}, u32[]{:S(2)}) collective-permute-start(f32[4,48,1024]{2,1,0:T(8,128)} %get-tuple-element.23), channel_id=1, source_target_pairs={{0,3},{1,0},{2,1},{3,2},{4,7},{5,4},{6,5},{7,6},{8,11},{9,8},{10,9... | collective-permute-start | bytes 2359304 | tf_op jit(solution)/shard_map/ppermute | solution.py:211
  155.2 35.6 %collective-permute-start.7 = (f32[4,48,1024]{2,1,0:T(8,128)}, f32[4,48,1024]{2,1,0:T(8,128)}, u32[]{:S(2)}, u32[]{:S(2)}) collective-permute-start(f32[4,48,1024]{2,1,0:T(8,128)} %get-tuple-element.24), channel_id=1, source_target_pairs={{0,2},{1,3},{2,0},{3,1},{4,6},{5,7},{6,4},{7,5},{8,10},{9,11},{10,... | collective-permute-start | bytes 2359304 | tf_op jit(solution)/shard_map/ppermute | solution.py:211
  155.5 38.0 %collective-permute-start.6 = (f32[4,48,1024]{2,1,0:T(8,128)}, f32[4,48,1024]{2,1,0:T(8,128)S(1)}, u32[]{:S(2)}, u32[]{:S(2)}) collective-permute-start(f32[4,48,1024]{2,1,0:T(8,128)} %get-tuple-element.25), channel_id=1, source_target_pairs={{0,1},{1,2},{2,3},{3,0},{4,5},{5,6},{6,7},{7,4},{8,9},{9,10},{10,1... | collective-permute-start | bytes 2359304 | tf_op jit(solution)/shard_map/ppermute | solution.py:211

commit v5 on v4

--- a/solution.py
+++ b/solution.py
@@ -169,7 +169,13 @@
 def on_device(fields, weights, stencil, bands):
     n_fields, n_levels, lat_rows, lon_cols = fields.shape
     n_items = n_fields * n_levels
-    below_raw, above_raw = shifted(fields, "lat", ROWS_OUT, 2, False)
+    count = lax.axis_size("lat")
+    forward = [(i, i + 1) for i in range(count - 1)]
+    backward = [(target, source) for source, target in forward]
+    edge_low = vertical_mix(jnp.transpose(fields[:, :, lat_rows - ROWS_OUT :, :], (2, 0, 1, 3)), bands)
+    edge_high = vertical_mix(jnp.transpose(fields[:, :, :ROWS_OUT, :], (2, 0, 1, 3)), bands)
+    below_raw = lax.ppermute(jnp.transpose(edge_low, (1, 2, 0, 3)), "lat", forward)
+    above_raw = lax.ppermute(jnp.transpose(edge_high, (1, 2, 0, 3)), "lat", backward)
 
     width = lon_cols + LANES
     local_rows = vertical_mix(jnp.transpose(fields, (2, 0, 1, 3)), bands)
@@ -195,7 +201,7 @@
 
     below_raw, above_raw, partial = lax.optimization_barrier((below_raw, above_raw, partial))
     halo_raw = jnp.concatenate([below_raw, above_raw], axis=2)
-    halo_rows = vertical_mix(jnp.transpose(halo_raw, (2, 0, 1, 3)), bands)
+    halo_rows = jnp.transpose(halo_raw, (2, 0, 1, 3))
     halo_hi, halo_lo = split_rows(widen(halo_rows.reshape(2 * ROWS_OUT, n_items, lon_cols)), width)
     departed = interpolate(halo_hi, halo_lo, info, lat_rows, lon_cols, base=partial)
 

time: 221 us -> 223 us (level)
    ppermute x0 -> x2, waiting for transfers between devices: none -> 63.4 us  [the longest x1 63.4 us: on_device(): lax.ppermute(jnp.transpose(edge_high, (1, 2, 0, 3)), 'lat', backward)]
    ppermute x3 -> x2, waiting for transfers between devices: 60.2 us -> 8.56 us  [shifted(): lax.ppermute(lax.slice_in_dim(block, 0, width, axis=dim), axis, backward)]
    ppermute x3 -> x2, waiting for transfers between devices: 14.8 us -> 4.71 us  [shifted(): lax.ppermute(lax.slice_in_dim(block, block.shape[dim] - width, None, axis...]
    ppermute x0 -> x2, starting transfers between devices: none -> 7.26 us  [the longest x1 3.96 us: on_device(): lax.ppermute(jnp.transpose(edge_low, (1, 2, 0, 3)), 'lat', forward)]
    slice x4 -> x3, local copies, waits for them, and re-layouts: 7.14 us -> 1.45 us  [shifted(): lax.slice_in_dim(block, 0, width, axis=dim)]
    slice x0 -> x1, local copies, waits for them, and re-layouts: none -> 5.69 us  [on_device(): fields[:, :, :ROWS_OUT, :]]
    unnamed x19 -> x11, local copies, waits for them, and re-layouts: 11.8 us -> 6.14 us
    ppermute x3 -> x2, starting transfers between devices: 4.82 us -> 0.46 us  [shifted(): lax.ppermute(lax.slice_in_dim(block, 0, width, axis=dim), axis, backward)]
  transfers between devices with their start and end apart: 9 -> 9, of which waited for: 8 -> 7; matrix products, arithmetic and copies ran while one was open for 11% -> 10% of each run, Pallas kernels for 5% -> 5%
where the time goes in v5:
time: 223 us; the launch traced here: 221 us
  waiting for transfers between devices  109 us (49%)
  local copies, waits for them, and re-layouts  44.6 us (20%)
  other arithmetic  23.6 us (11%)
  Pallas kernels  20.6 us (9%)
  matrix products  12.9 us (6%)
  starting transfers between devices  10.1 us (5%)
    ppermute x1, waiting for transfers between devices, on_device(): lax.ppermute(jnp.transpose(edge_high, (1, 2, 0, 3)), 'lat', backward)  63.4 us
    ppermute x3, waiting for transfers between devices, on_device(): lax.ppermute(piece, 'lon', [(i, (i + shift) % parts) for i in range(parts)])  31.9 us
    pallas_call x2, Pallas kernels, interpolate(): pl.pallas_call(functools.partial(interp_kernel, base is None, lat_rows),...  20.6 us
    concatenate x2, local copies, waits for them, and re-layouts, widen(): return jnp.concatenate([left, block, right], axis=block.ndim - 1)  11.2 us
    ppermute x2, waiting for transfers between devices, shifted(): lax.ppermute(lax.slice_in_dim(block, 0, width, axis=dim), axis, backward)  8.56 us
    dot_general x1, matrix products, spectrum(): jnp.einsum('prab,pac->rbc', folded, table, precision=highest)  7.48 us
    another operation x4, local copies, waits for them, and re-layouts, spectrum(): jnp.stack([piece.reshape(n_rows * n_items, per_piece, RADIX) for piece in...  7.32 us
    convert_element_type x2, other arithmetic, split_rows(): (padded - rounded).astype(jnp.bfloat16)  6.2 us
  transfers between devices with their start and end apart: 9, of which 7 were waited for; matrix products, arithmetic and copies ran while one was open for 10% of the time, Pallas kernels for 5%

profile of v5, /device:TPU:24, one launch (start us, length us, event | category | flops | bytes accessed | tf_op | source)
XLA Modules:
  0.0 221.3 jit_solution(17311049674868174403)
XLA Ops:
  0.6 0.8 slice_bitcast_fusion.4
  1.4 5.7 %fusion.98 = (f32[6,32,3,1024]{3,2,1,0:T(4,128)S(1)}, f32[6,32,3,1024]{3,2,1,0:T(4,128)S(1)}) fusion(f32[6,32,4,1024]{3,2,1,0:T(4,128)} %param.4), kind=kLoop, calls=%fused_computation.153 | loop fusion | bytes 9437184 | tf_op jit(solution)/shard_map/slice | solution.py:176
  7.1 3.3 %copy_bitcast_fusion = (f32[3,6,32,1024]{3,2,0,1:T(8,128)S(1)}, f32[3,6,32,1024]{3,2,0,1:T(8,128)S(1)}) fusion(f32[6,32,3,1024]{3,2,1,0:T(4,128)S(1)} %get-tuple-element.28, f32[6,32,3,1024]{3,2,1,0:T(4,128)S(1)} %get-tuple-element.29), kind=kLoop, calls=%fused_computation.52 | loop fusion | bytes 9437184 | tf_op jit(solution)/shard_map/transpose | solution.py:176
  10.4 4.3 %fusion.28 = (f32[6,32,3,1024]{3,1,2,0:T(8,128)}, f32[6,32,3,1024]{3,1,2,0:T(8,128)}) fusion(f32[3,6,32,1024]{3,2,0,1:T(8,128)S(1)} %get-tuple-element.43, f32[6,32]{1,0:T(8,128)S(1)} %get-tuple-element.41, f32[6,32]{1,0:T(8,128)S(1)} %get-tuple-element.42, f32[6,32]{1,0:T(8,128)S(1)} %get-tuple-element.39, f32[6,32]{1,0:T(8,128)S(1)} %get-tuple-element.40, ...), kind=kLoop, calls=%fused_computation.44 | loop fusion | flops 10616832 | bytes 9441024 | tf_op jit(solution)/shard_map/transpose | solution.py:178
  14.7 3.3 %collective-permute-start.1 = (f32[6,32,3,1024]{3,1,2,0:T(8,128)}, f32[6,32,3,1024]{3,1,2,0:T(8,128)}, u32[]{:S(2)}, u32[]{:S(2)}) collective-permute-start(f32[6,32,3,1024]{3,1,2,0:T(8,128)} %get-tuple-element.36), channel_id=1, source_target_pairs={{4,0},{8,4},{12,8},{16,12},{20,16},{24,20},{28,24},{5,1},{9,5},{13... | collective-permute-start | bytes 7077896 | tf_op jit(solution)/shard_map/ppermute | solution.py:178
  18.0 4.0 %collective-permute-start = (f32[6,32,3,1024]{3,1,2,0:T(8,128)}, f32[6,32,3,1024]{3,1,2,0:T(8,128)}, u32[]{:S(2)}, u32[]{:S(2)}) collective-permute-start(f32[6,32,3,1024]{3,1,2,0:T(8,128)} %get-tuple-element.37), channel_id=1, source_target_pairs={{0,4},{4,8},{8,12},{12,16},{16,20},{20,24},{24,28},{1,5},{5,9},{9,... | collective-permute-start | bytes 7077896 | tf_op jit(solution)/shard_map/ppermute | solution.py:177
  22.0 2.8 %multiply_add_fusion.1 = f32[4,6,32,1024]{3,0,2,1:T(4,128)S(1)} fusion(f32[4,6,32,1024]{3,0,2,1:T(4,128)S(1)} %bitcast.72, f32[6,32]{1,0:T(8,128)S(1)} %get-tuple-element.41, f32[6,32]{1,0:T(8,128)S(1)} %get-tuple-element.42, f32[6,32]{1,0:T(8,128)S(1)} %get-tuple-element.39, f32[6,32]{1,0:T(8,128)S(1)} %get-tuple-element.40, f32[6,32]{1,0:T(8,128)S(1)} %get-tuple-element.38), kind=kLoop, calls=%fused_computation.26 | loop fusion | flops 7077888 | bytes 6295296 | tf_op jit(solution)/shard_map/add | solution.py:151
  24.8 1.8 copy.29
  26.7 1.0 fusion.97
  27.7 0.4 collective-permute-start.3
  28.2 0.9 copy.66
  29.2 1.1 maximum_maximum_fusion.refs_2_
  30.3 7.1 %collective-permute-done.3 = f32[4,192,16]{2,1,0:T(8,128)} collective-permute-done((f32[4,192,16]{2,1,0:T(8,128)}, f32[4,192,16]{2,1,0:T(8,128)}, u32[]{:S(2)}, u32[]{:S(2)}) %collective-permute-start.3) | collective-permute-done | bytes 49184 | tf_op jit(solution)/shard_map/ppermute | solution.py:29
  37.4 2.1 collective-permute-done.2
  39.4 4.4 %concatenate.18 = f32[4,192,1056]{2,1,0:T(8,128)} concatenate(f32[4,192,16]{2,1,0:T(8,128)} %collective-permute-done.2, f32[4,192,1024]{2,1,0:T(8,128)S(1)} %bitcast.76, f32[4,192,16]{2,1,0:T(8,128)} %collective-permute-done.3), dimensions={2} | concatenate | bytes 6488064 | tf_op jit(solution)/shard_map/concatenate | solution.py:159
  43.8 2.6 %fusion.9 = (bf16[4,192,1152]{2,1,0:T(8,128)(2,1)S(1)}, bf16[4,192,1152]{2,1,0:T(8,128)(2,1)S(1)}) fusion(f32[4,192,1056]{2,1,0:T(8,128)} %concatenate.18), kind=kLoop, calls=%fused_computation.17 | loop fusion | flops 3538944 | bytes 6782976 | tf_op jit(solution)/shard_map/convert_element_type | solution.py:166
  46.4 10.5 %shard_map.59.refs_3_ = f32[4,192,1024]{2,1,0:T(8,128)} custom-call(bf16[4,192,1152]{2,1,0:T(8,128)(2,1)S(1)} %get-tuple-element.21.refs_0_, bf16[4,192,1152]{2,1,0:T(8,128)(2,1)S(1)} %get-tuple-element.20.refs_1_, f32[4,24,1024]{2,1,0:T(8,128)S(1)} %maximum_maximum_fusion.refs_2_), custom_call_target="tpu_custom_call" | custom-call | tf_op jit(solution)/shard_map/pallas_call | solution.py:133
  57.0 63.4 %collective-permute-done.1 = f32[6,32,3,1024]{3,1,2,0:T(8,128)} collective-permute-done((f32[6,32,3,1024]{3,1,2,0:T(8,128)}, f32[6,32,3,1024]{3,1,2,0:T(8,128)}, u32[]{:S(2)}, u32[]{:S(2)}) %collective-permute-start.1) | collective-permute-done | bytes 2359328 | tf_op jit(solution)/shard_map/ppermute | solution.py:178
  120.4 2.8 %maximum_bitcast_fusion = f32[6,6,32,1024]{3,2,0,1:T(8,128)S(1)} fusion(f32[6,32,3,1024]{3,1,2,0:T(8,128)} %collective-permute-done.1, f32[6,32,3,1024]{3,1,2,0:T(8,128)} %collective-permute-done), kind=kLoop, calls=%fused_computation.16 | loop fusion | flops 1179648 | bytes 9437184 | tf_op jit(solution)/shard_map/transpose | solution.py:204
  123.2 0.4 copy.33
  123.6 2.1 copy-done.1
  125.7 0.2 fusion.96
  125.9 0.2 copy.35
  126.2 0.2 copy.34
  126.4 0.5 collective-permute-start.4
  126.9 1.5 collective-permute-done.5
  128.7 2.6 %collective-permute-done.4 = f32[6,192,16]{1,2,0:T(8,128)S(1)} collective-permute-done((f32[6,192,16]{1,2,0:T(8,128)S(1)}, f32[6,192,16]{1,2,0:T(8,128)S(1)}, u32[]{:S(2)}, u32[]{:S(2)}) %collective-permute-start.4) | collective-permute-done | bytes 73760 | tf_op jit(solution)/shard_map/ppermute | solution.py:26
  131.3 0.2 copy.36
  131.5 6.9 %concatenate.21 = f32[6,192,1056]{2,1,0:T(8,128)} concatenate(f32[6,192,16]{2,1,0:T(8,128)S(1)} %copy.36, f32[6,192,1024]{2,1,0:T(8,128)} %bitcast.74, f32[6,192,16]{2,1,0:T(8,128)S(1)} %copy.37), dimensions={2} | concatenate | bytes 9732096 | tf_op jit(solution)/shard_map/concatenate | solution.py:159
  138.4 3.6 %fusion.8 = (bf16[6,192,1152]{2,1,0:T(8,128)(2,1)S(1)}, bf16[6,192,1152]{2,1,0:T(8,128)(2,1)S(1)}) fusion(f32[6,192,1056]{2,1,0:T(8,128)} %concatenate.21), kind=kLoop, calls=%fused_computation.13 | loop fusion | flops 5308416 | bytes 10174464 | tf_op jit(solution)/shard_map/convert_element_type | solution.py:166
  142.0 10.1 %shard_map.60 = f32[4,192,1024]{2,1,0:T(8,128)} custom-call(bf16[6,192,1152]{2,1,0:T(8,128)(2,1)S(1)} %get-tuple-element.15.refs_0_, bf16[6,192,1152]{2,1,0:T(8,128)(2,1)S(1)} %get-tuple-element.14.refs_1_, f32[4,24,1024]{2,1,0:T(8,128)S(1)} %maximum_maximum_fusion.refs_2_, f32[4,192,1024]{2,1,0:T(8,128)} %shard_map.59.refs_3_), custom_call_target="tpu_custom_call" | custom-call | tf_op jit(solution)/shard_map/pallas_call | solution.py:133
  152.0 3.3 %constant_dynamic-slice_fusion.3 = (f32[4,48,1024]{2,1,0:T(8,128)S(1)}, f32[4,48,1024]{2,1,0:T(8,128)}, f32[4,48,1024]{2,1,0:T(8,128)}, f32[4,48,1024]{2,1,0:T(8,128)}) fusion(f32[4,192,1024]{2,1,0:T(8,128)} %shard_map.60, s32[]{:T(128)S(6)} %select_n.73, s32[]{:T(128)S(6)} %select_n.76, s32[]{:T(128)S(6)} %select_n.75, s32[]{:T(128)S(6)} %select_n.74), kind=kLoop, calls=%fused_computation.139 | loop fusion | bytes 6291472 | tf_op jit(solution)/shard_map/dynamic_slice | solution.py:215
  155.4 1.7 collective-permute-start.7
  157.5 0.4 stack_reshape.12
  157.9 15.5 %collective-permute-done.8 = f32[4,48,1024]{2,1,0:T(8,128)} collective-permute-done((f32[4,48,1024]{2,1,0:T(8,128)}, f32[4,48,1024]{2,1,0:T(8,128)}, u32[]{:S(2)}, u32[]{:S(2)}) %collective-permute-start.8) | collective-permute-done | bytes 786464 | tf_op jit(solution)/shard_map/ppermute | solution.py:217
  173.4 2.7 %stack_reshape.15 = f32[1,192,16,64]{3,2,1,0:T(8,128)} reshape(f32[4,48,1024]{2,1,0:T(8,128)} %collective-permute-done.8) | data formatting | bytes 1572864 | tf_op jit(solution)/shard_map/stack;reshape | solution.py:43
  176.1 16.4 %collective-permute-done.7 = f32[4,48,1024]{2,1,0:T(8,128)} collective-permute-done((f32[4,48,1024]{2,1,0:T(8,128)}, f32[4,48,1024]{2,1,0:T(8,128)}, u32[]{:S(2)}, u32[]{:S(2)}) %collective-permute-start.7) | collective-permute-done | bytes 786464 | tf_op jit(solution)/shard_map/ppermute | solution.py:217
  192.5 2.7 %stack_reshape.14 = f32[1,192,16,64]{3,2,1,0:T(8,128)} reshape(f32[4,48,1024]{2,1,0:T(8,128)} %collective-permute-done.7) | data formatting | bytes 1572864 | tf_op jit(solution)/shard_map/stack;reshape | solution.py:43
  195.1 1.6 stack_reshape.13
  196.7 7.5 %fusion.11 = f32[192,64,128]{2,1,0:T(8,128)S(1)} fusion(f32[1,192,16,64]{3,2,0,1:T(8,128)} %bitcast.80, f32[1,192,16,64]{3,2,0,1:T(8,128)} %bitcast.81, f32[1,192,16,64]{3,2,0,1:T(8,128)} %bitcast.82, f32[1,192,16,64]{3,2,0,1:T(8,128)S(1)} %bitcast.79, f32[1,16,128]{2,1,0:T(8,128)S(1)} %get-tuple-element.33, f32[1,16,128]{2,1,0:T(8,128)S(1)} %get-tuple-element.32, ...), kind=kOutput, calls=%fused_computation.29 | convolution fusion | flops 606363648 | bytes 9469952 | tf_op jit(solution)/shard_map/prab,pac->rbc/dot_general | solution.py:47
  204.2 3.3 %multiply_add_fusion = (f32[192,64,64]{2,1,0:T(8,128)S(1)}, f32[192,64,64]{2,1,0:T(8,128)S(1)}) fusion(f32[192,64,128]{2,1,0:T(8,128)S(1)} %fusion.11, f32[64,64]{1,0:T(8,128)S(1)} %get-tuple-element.49, f32[64,64]{1,0:T(8,128)S(1)} %get-tuple-element.50), kind=kLoop, calls=%fused_computation.12 | loop fusion | flops 4718592 | bytes 12615680 | tf_op jit(solution)/shard_map/add | solution.py:59
  207.5 2.7 %fusion.37 = f32[192,20,128]{2,1,0:T(8,128)S(1)} fusion(f32[192,64,64]{2,1,0:T(8,128)S(1)} %get-tuple-element.13, f32[192,64,64]{2,1,0:T(8,128)S(1)} %get-tuple-element.12), kind=kOutput, calls=%fused_computation.57 | convolution fusion | flops 190334464 | bytes 8257536 | tf_op jit(solution)/shard_map/rbc,bq->rqc/dot_general | solution.py:66
  210.2 2.7 %fusion.36 = f32[192,20,128]{2,1,0:T(8,128)S(1)} fusion(f32[192,64,64]{2,1,0:T(8,128)S(1)} %get-tuple-element.13, f32[192,64,64]{2,1,0:T(8,128)S(1)} %get-tuple-element.12), kind=kOutput, calls=%fused_computation.56 | convolution fusion | flops 190334464 | bytes 8257536 | tf_op jit(solution)/shard_map/rbc,bq->rqc/dot_general | solution.py:65
  212.9 2.7 %fusion.32 = (f32[192,20,64]{2,1,0:T(8,128)}, f32[192,20,64]{2,1,0:T(8,128)S(1)}) fusion(f32[192,20,128]{2,1,0:T(8,128)S(1)} %fusion.37, f32[192,20,128]{2,1,0:T(8,128)S(1)} %fusion.36), kind=kLoop, calls=%fused_computation.49 | loop fusion | flops 983040 | bytes 5898240 | tf_op jit(solution)/shard_map/mul | solution.py:69
  215.6 2.0 reshape.171
  217.6 1.6 copy.43
  219.2 0.5 reshape.170
  219.7 1.6 copy.42
  (23 shorter events, 1.0 us)
Async XLA Ops:
  10.3 11.6 %copy-start = (f32[6,32,4,1024]{3,2,1,0:T(4,128)S(1)}, f32[6,32,4,1024]{3,2,1,0:T(4,128)}, u32[]{:S(2)}) copy-start(f32[6,32,4,1024]{3,2,1,0:T(4,128)} %param.4) | copy-start | bytes 9437188
  14.7 105.7 %collective-permute-start.1 = (f32[6,32,3,1024]{3,1,2,0:T(8,128)}, f32[6,32,3,1024]{3,1,2,0:T(8,128)}, u32[]{:S(2)}, u32[]{:S(2)}) collective-permute-start(f32[6,32,3,1024]{3,1,2,0:T(8,128)} %get-tuple-element.36), channel_id=1, source_target_pairs={{4,0},{8,4},{12,8},{16,12},{20,16},{24,20},{28,24},{5,1},{9,5},{13... | collective-permute-start | bytes 7077896 | tf_op jit(solution)/shard_map/ppermute | solution.py:178
  18.0 102.4 %collective-permute-start = (f32[6,32,3,1024]{3,1,2,0:T(8,128)}, f32[6,32,3,1024]{3,1,2,0:T(8,128)}, u32[]{:S(2)}, u32[]{:S(2)}) collective-permute-start(f32[6,32,3,1024]{3,1,2,0:T(8,128)} %get-tuple-element.37), channel_id=1, source_target_pairs={{0,4},{4,8},{8,12},{12,16},{16,20},{20,24},{24,28},{1,5},{5,9},{9,... | collective-permute-start | bytes 7077896 | tf_op jit(solution)/shard_map/ppermute | solution.py:177
  24.8 3.4 %copy-start.2 = (f32[16,4,1024]{2,1,0:T(4,128)S(1)}, f32[16,4,1024]{2,1,0:T(4,128)}, u32[]{:S(2)}) copy-start(f32[16,4,1024]{2,1,0:T(4,128)} %param.5) | copy-start | bytes 786436
  24.8 4.3 %copy-start.3 = (s32[2,4,1024]{2,1,0:T(4,128)S(1)}, s32[2,4,1024]{2,1,0:T(4,128)}, u32[]{:S(2)}) copy-start(s32[2,4,1024]{2,1,0:T(4,128)} %param.6) | copy-start | bytes 98308
  27.7 9.7 %collective-permute-start.3 = (f32[4,192,16]{2,1,0:T(8,128)}, f32[4,192,16]{2,1,0:T(8,128)}, u32[]{:S(2)}, u32[]{:S(2)}) collective-permute-start(f32[4,192,16]{2,1,0:T(8,128)} %get-tuple-element.26), channel_id=1, source_target_pairs={{1,0},{2,1},{3,2},{0,3},{5,4},{6,5},{7,6},{4,7},{9,8},{10,9},{11,1... | collective-permute-start | bytes 147464 | tf_op jit(solution)/shard_map/ppermute | solution.py:29
  28.0 11.4 %collective-permute-start.2 = (f32[4,192,16]{2,1,0:T(8,128)}, f32[4,192,16]{2,1,0:T(8,128)}, u32[]{:S(2)}, u32[]{:S(2)}) collective-permute-start(f32[4,192,16]{2,1,0:T(8,128)} %get-tuple-element.27), channel_id=1, source_target_pairs={{0,1},{1,2},{2,3},{3,0},{4,5},{5,6},{6,7},{7,4},{8,9},{9,10},{10,1... | collective-permute-start | bytes 147464 | tf_op jit(solution)/shard_map/ppermute | solution.py:26
  123.6 2.1 copy-start.1
  126.1 2.3 %collective-permute-start.5 = (f32[6,192,16]{1,2,0:T(8,128)S(1)}, f32[6,192,16]{1,2,0:T(8,128)S(1)}, u32[]{:S(2)}, u32[]{:S(2)}) collective-permute-start(f32[6,192,16]{1,2,0:T(8,128)S(1)} %copy.35), channel_id=1, source_target_pairs={{1,0},{2,1},{3,2},{0,3},{5,4},{6,5},{7,6},{4,7},{9,8},{10,9},{11,1... | collective-permute-start | bytes 221192 | tf_op jit(solution)/shard_map/ppermute | solution.py:29
  126.4 4.9 %collective-permute-start.4 = (f32[6,192,16]{1,2,0:T(8,128)S(1)}, f32[6,192,16]{1,2,0:T(8,128)S(1)}, u32[]{:S(2)}, u32[]{:S(2)}) collective-permute-start(f32[6,192,16]{1,2,0:T(8,128)S(1)} %copy.34), channel_id=1, source_target_pairs={{0,1},{1,2},{2,3},{3,0},{4,5},{5,6},{6,7},{7,4},{8,9},{9,10},{10,1... | collective-permute-start | bytes 221192 | tf_op jit(solution)/shard_map/ppermute | solution.py:26
  155.4 18.0 %collective-permute-start.8 = (f32[4,48,1024]{2,1,0:T(8,128)}, f32[4,48,1024]{2,1,0:T(8,128)}, u32[]{:S(2)}, u32[]{:S(2)}) collective-permute-start(f32[4,48,1024]{2,1,0:T(8,128)} %get-tuple-element.23), channel_id=1, source_target_pairs={{0,3},{1,0},{2,1},{3,2},{4,7},{5,4},{6,5},{7,6},{8,11},{9,8},{10,9... | collective-permute-start | bytes 2359304 | tf_op jit(solution)/shard_map/ppermute | solution.py:217
  155.4 37.1 %collective-permute-start.7 = (f32[4,48,1024]{2,1,0:T(8,128)}, f32[4,48,1024]{2,1,0:T(8,128)}, u32[]{:S(2)}, u32[]{:S(2)}) collective-permute-start(f32[4,48,1024]{2,1,0:T(8,128)} %get-tuple-element.24), channel_id=1, source_target_pairs={{0,2},{1,3},{2,0},{3,1},{4,6},{5,7},{6,4},{7,5},{8,10},{9,11},{10,... | collective-permute-start | bytes 2359304 | tf_op jit(solution)/shard_map/ppermute | solution.py:217
  157.1 38.1 %collective-permute-start.6 = (f32[4,48,1024]{2,1,0:T(8,128)}, f32[4,48,1024]{2,1,0:T(8,128)S(1)}, u32[]{:S(2)}, u32[]{:S(2)}) collective-permute-start(f32[4,48,1024]{2,1,0:T(8,128)} %get-tuple-element.25), channel_id=1, source_target_pairs={{0,1},{1,2},{2,3},{3,0},{4,5},{5,6},{6,7},{7,4},{8,9},{9,10},{10,1... | collective-permute-start | bytes 2359304 | tf_op jit(solution)/shard_map/ppermute | solution.py:217

commit v6 on v4

--- a/solution.py
+++ b/solution.py
@@ -196,7 +196,17 @@
     below_raw, above_raw, partial = lax.optimization_barrier((below_raw, above_raw, partial))
     halo_raw = jnp.concatenate([below_raw, above_raw], axis=2)
     halo_rows = vertical_mix(jnp.transpose(halo_raw, (2, 0, 1, 3)), bands)
-    halo_hi, halo_lo = split_rows(widen(halo_rows.reshape(2 * ROWS_OUT, n_items, lon_cols)), width)
+    halo_main = halo_rows.reshape(2 * ROWS_OUT, n_items, lon_cols)
+    left, right = shifted(halo_main, "lon", HALO, 2, True)
+    parts_hi = []
+    parts_lo = []
+    for piece in (left, halo_main, right):
+        piece_hi, piece_lo = split_rows(piece, piece.shape[-1])
+        parts_hi.append(piece_hi)
+        parts_lo.append(piece_lo)
+    filler = jnp.zeros((2 * ROWS_OUT, n_items, width - lon_cols - 2 * HALO), jnp.bfloat16)
+    halo_hi = jnp.concatenate(parts_hi + [filler], axis=2)
+    halo_lo = jnp.concatenate(parts_lo + [filler], axis=2)
     departed = interpolate(halo_hi, halo_lo, info, lat_rows, lon_cols, base=partial)
 
     parts = lax.axis_size("lon")

time: 221 us -> 232 us (1.050)
  local copies, waits for them, and re-layouts: 46.2 us -> 54.3 us
  other arithmetic: 22.1 us -> 25.7 us
  waiting for transfers between devices: 107 us -> 104 us
    concatenate x0 -> x2, local copies, waits for them, and re-layouts: none -> 10.8 us  [the longest x1 6.01 us: on_device(): halo_hi = jnp.concatenate(parts_hi + [filler], axis=2)]
    concatenate x2 -> x1, local copies, waits for them, and re-layouts: 11.2 us -> 4.43 us  [widen(): return jnp.concatenate([left, block, right], axis=block.ndim - 1)]
    convert_element_type x2 -> x4, other arithmetic: 6.2 us -> 9.77 us  [split_rows(): (padded - rounded).astype(jnp.bfloat16)]
    unnamed x19 -> x21, local copies, waits for them, and re-layouts: 11.8 us -> 13.6 us
  transfers between devices with their start and end apart: 9 -> 9, of which waited for: 8 -> 7; matrix products, arithmetic and copies ran while one was open for 11% -> 13% of each run, Pallas kernels for 5% -> 5%
where the time goes in v6:
time: 232 us; the launch traced here: 231 us
  waiting for transfers between devices  104 us (45%)
  local copies, waits for them, and re-layouts  54.3 us (23%)
  other arithmetic  25.7 us (11%)
  Pallas kernels  20.6 us (9%)
  matrix products  12.9 us (6%)
  starting transfers between devices  12.6 us (5%)
    ppermute x3, waiting for transfers between devices, shifted(): lax.ppermute(lax.slice_in_dim(block, 0, width, axis=dim), axis, backward)  58.8 us
    ppermute x3, waiting for transfers between devices, on_device(): lax.ppermute(piece, 'lon', [(i, (i + shift) % parts) for i in range(parts)])  31.5 us
    pallas_call x2, Pallas kernels, interpolate(): pl.pallas_call(functools.partial(interp_kernel, base is None, lat_rows),...  20.6 us
    ppermute x3, waiting for transfers between devices, shifted(): lax.ppermute(lax.slice_in_dim(block, block.shape[dim] - width, None, axis...  13.7 us
    unnamed x21, local copies, waits for them, and re-layouts  13.6 us
    convert_element_type x4, other arithmetic, split_rows(): (padded - rounded).astype(jnp.bfloat16)  9.77 us
    dot_general x1, matrix products, spectrum(): jnp.einsum('prab,pac->rbc', folded, table, precision=highest)  7.48 us
    another operation x4, local copies, waits for them, and re-layouts, spectrum(): jnp.stack([piece.reshape(n_rows * n_items, per_piece, RADIX) for piece in...  7.34 us
  transfers between devices with their start and end apart: 9, of which 7 were waited for; matrix products, arithmetic and copies ran while one was open for 13% of the time, Pallas kernels for 5%

profile of v6, /device:TPU:24, one launch (start us, length us, event | category | flops | bytes accessed | tf_op | source)
XLA Modules:
  0.0 231.1 jit_solution(16617929146991196348)
XLA Ops:
  0.6 5.7 %fusion.88 = (f32[6,32,3,1024]{3,2,1,0:T(4,128)S(1)}, f32[6,32,3,1024]{3,2,1,0:T(4,128)S(1)}) fusion(f32[6,32,4,1024]{3,2,1,0:T(4,128)} %param.4), kind=kLoop, calls=%fused_computation.141 | loop fusion | bytes 9437184 | tf_op jit(solution)/shard_map/slice | solution.py:29
  6.3 2.8 %copy.68 = f32[6,32,3,1024]{3,1,2,0:T(8,128)} copy(f32[6,32,3,1024]{3,2,1,0:T(4,128)S(1)} %get-tuple-element.31) | data formatting | bytes 4718592
  9.1 3.7 %collective-permute-start = (f32[6,32,3,1024]{3,1,2,0:T(8,128)}, f32[6,32,3,1024]{3,1,2,0:T(8,128)}, u32[]{:S(2)}, u32[]{:S(2)}) collective-permute-start(f32[6,32,3,1024]{3,1,2,0:T(8,128)} %copy.68), channel_id=1, source_target_pairs={{0,4},{4,8},{8,12},{12,16},{16,20},{20,24},{24,28},{1,5},{5,9},{9,... | collective-permute-start | bytes 7077896 | tf_op jit(solution)/shard_map/ppermute | solution.py:26
  12.8 2.8 %copy.69 = f32[6,32,3,1024]{3,1,2,0:T(8,128)} copy(f32[6,32,3,1024]{3,2,1,0:T(4,128)S(1)} %get-tuple-element.30) | data formatting | bytes 4718592
  15.6 3.3 %collective-permute-start.1 = (f32[6,32,3,1024]{3,1,2,0:T(8,128)}, f32[6,32,3,1024]{3,1,2,0:T(8,128)}, u32[]{:S(2)}, u32[]{:S(2)}) collective-permute-start(f32[6,32,3,1024]{3,1,2,0:T(8,128)} %copy.69), channel_id=1, source_target_pairs={{4,0},{8,4},{12,8},{16,12},{20,16},{24,20},{28,24},{5,1},{9,5},{13... | collective-permute-start | bytes 7077896 | tf_op jit(solution)/shard_map/ppermute | solution.py:29
  19.0 2.8 %multiply_add_fusion.1 = f32[4,6,32,1024]{3,0,2,1:T(4,128)S(1)} fusion(f32[4,6,32,1024]{3,0,2,1:T(4,128)S(1)} %bitcast.66, f32[6,32]{1,0:T(8,128)S(1)} %get-tuple-element.45, f32[6,32]{1,0:T(8,128)S(1)} %get-tuple-element.46, f32[6,32]{1,0:T(8,128)S(1)} %get-tuple-element.43, f32[6,32]{1,0:T(8,128)S(1)} %get-tuple-element.44, f32[6,32]{1,0:T(8,128)S(1)} %get-tuple-element.42), kind=kLoop, calls=%fused_computation.30 | loop fusion | flops 7077888 | bytes 6295296 | tf_op jit(solution)/shard_map/add | solution.py:151
  21.8 1.8 copy.48
  23.6 1.0 fusion.87
  25.1 0.9 copy.87
  26.2 1.1 maximum_maximum_fusion.refs_2_
  27.3 7.0 %collective-permute-done.3 = f32[4,192,16]{2,1,0:T(8,128)} collective-permute-done((f32[4,192,16]{2,1,0:T(8,128)}, f32[4,192,16]{2,1,0:T(8,128)}, u32[]{:S(2)}, u32[]{:S(2)}) %collective-permute-start.3) | collective-permute-done | bytes 49184 | tf_op jit(solution)/shard_map/ppermute | solution.py:29
  34.3 2.1 collective-permute-done.2
  36.4 4.4 %concatenate.21 = f32[4,192,1056]{2,1,0:T(8,128)} concatenate(f32[4,192,16]{2,1,0:T(8,128)} %collective-permute-done.2, f32[4,192,1024]{2,1,0:T(8,128)S(1)} %bitcast.69, f32[4,192,16]{2,1,0:T(8,128)} %collective-permute-done.3), dimensions={2} | concatenate | bytes 6488064 | tf_op jit(solution)/shard_map/concatenate | solution.py:159
  40.8 2.6 %fusion.17 = (bf16[4,192,1152]{2,1,0:T(8,128)(2,1)S(1)}, bf16[4,192,1152]{2,1,0:T(8,128)(2,1)S(1)}) fusion(f32[4,192,1056]{2,1,0:T(8,128)} %concatenate.21), kind=kLoop, calls=%fused_computation.29 | loop fusion | flops 3538944 | bytes 6782976 | tf_op jit(solution)/shard_map/convert_element_type | solution.py:166
  43.5 10.5 %shard_map.59.refs_3_ = f32[4,192,1024]{2,1,0:T(8,128)} custom-call(bf16[4,192,1152]{2,1,0:T(8,128)(2,1)S(1)} %get-tuple-element.23.refs_0_, bf16[4,192,1152]{2,1,0:T(8,128)(2,1)S(1)} %get-tuple-element.22.refs_1_, f32[4,24,1024]{2,1,0:T(8,128)S(1)} %maximum_maximum_fusion.refs_2_), custom_call_target="tpu_custom_call" | custom-call | tf_op jit(solution)/shard_map/pallas_call | solution.py:133
  54.0 11.6 %collective-permute-done = f32[6,32,3,1024]{3,1,2,0:T(8,128)} collective-permute-done((f32[6,32,3,1024]{3,1,2,0:T(8,128)}, f32[6,32,3,1024]{3,1,2,0:T(8,128)}, u32[]{:S(2)}, u32[]{:S(2)}) %collective-permute-start) | collective-permute-done | bytes 2359328 | tf_op jit(solution)/shard_map/ppermute | solution.py:26
  65.6 50.5 %collective-permute-done.1 = f32[6,32,3,1024]{3,1,2,0:T(8,128)} collective-permute-done((f32[6,32,3,1024]{3,1,2,0:T(8,128)}, f32[6,32,3,1024]{3,1,2,0:T(8,128)}, u32[]{:S(2)}, u32[]{:S(2)}) %collective-permute-start.1) | collective-permute-done | bytes 2359328 | tf_op jit(solution)/shard_map/ppermute | solution.py:29
  116.1 2.8 %maximum_bitcast_fusion = f32[6,6,32,1024]{3,2,0,1:T(8,128)S(1)} fusion(f32[6,32,3,1024]{3,1,2,0:T(8,128)} %collective-permute-done.1, f32[6,32,3,1024]{3,1,2,0:T(8,128)} %collective-permute-done), kind=kLoop, calls=%fused_computation.28 | loop fusion | flops 1179648 | bytes 9437184 | tf_op jit(solution)/shard_map/transpose | solution.py:198
  118.8 2.9 %fusion.12 = f32[6,6,32,1024]{3,2,0,1:T(8,128)S(1)} fusion(f32[6,6,32,1024]{3,2,0,1:T(8,128)S(1)} %maximum_bitcast_fusion, f32[6,32]{1,0:T(8,128)S(1)} %get-tuple-element.45, f32[6,32]{1,0:T(8,128)S(1)} %copy-done.5, f32[6,32]{1,0:T(8,128)S(1)} %get-tuple-element.43, f32[6,32]{1,0:T(8,128)S(1)} %get-tuple-element.44, f32[6,32]{1,0:T(8,128)S(1)} %get-tuple-element.42), kind=kLoop, calls=%fused_computation.23 | loop fusion | flops 10616832 | bytes 9441024 | tf_op jit(solution)/shard_map/add | solution.py:151
  122.1 2.2 copy-done.2
  124.8 5.5 %fusion.16 = (bf16[6,192,1024]{2,1,0:T(8,128)(2,1)}, bf16[6,192,1024]{2,1,0:T(8,128)(2,1)}) fusion(f32[6,6,32,1024]{3,2,1,0:T(8,128)} %copy-done.2), kind=kLoop, calls=%fused_computation.27 | loop fusion | flops 4718592 | bytes 9437184 | tf_op jit(solution)/shard_map/convert_element_type | solution.py:166
  130.5 1.8 collective-permute-start.5
  132.3 0.9 copy.55
  133.2 1.3 collective-permute-done.5
  134.5 0.9 copy.56
  136.1 0.8 subtract_convert_fusion.1
  137.1 0.8 subtract_convert_fusion
  137.9 4.8 %concatenate.25.refs_1_ = bf16[6,192,1152]{2,1,0:T(8,128)(2,1)S(1)} concatenate(bf16[6,192,16]{2,1,0:T(8,128)(2,1)} %subtract_convert_fusion.1, bf16[6,192,1024]{2,1,0:T(8,128)(2,1)} %get-tuple-element.18, bf16[6,192,16]{2,1,0:T(8,128)(2,1)} %subtract_convert_fusion, bf16[6,192,96]{2,1,0:T(8,128)(2,1)S(1)} %broadcast_in_dim.5), dimensions={2} | concatenate | bytes 5308416 | tf_op jit(solution)/shard_map/concatenate | solution.py:209
  142.7 6.0 %concatenate.24.refs_0_ = bf16[6,192,1152]{2,1,0:T(8,128)(2,1)} concatenate(bf16[6,192,16]{2,1,0:T(8,128)(2,1)} %copy.55, bf16[6,192,1024]{2,1,0:T(8,128)(2,1)} %get-tuple-element.19, bf16[6,192,16]{2,1,0:T(8,128)(2,1)} %copy.56, bf16[6,192,96]{2,1,0:T(8,128)(2,1)S(1)} %broadcast_in_dim.5), dimensions={2} | concatenate | bytes 5308416 | tf_op jit(solution)/shard_map/concatenate | solution.py:208
  148.8 1.7 copy-done
  150.5 10.1 %shard_map.60 = f32[4,192,1024]{2,1,0:T(8,128)} custom-call(bf16[6,192,1152]{2,1,0:T(8,128)(2,1)S(1)} %copy-done, bf16[6,192,1152]{2,1,0:T(8,128)(2,1)S(1)} %concatenate.25.refs_1_, f32[4,24,1024]{2,1,0:T(8,128)S(1)} %maximum_maximum_fusion.refs_2_, f32[4,192,1024]{2,1,0:T(8,128)} %shard_map.59.refs_3_), custom_call_target="tpu_custom_call" | custom-call | tf_op jit(solution)/shard_map/pallas_call | solution.py:133
  160.6 3.3 %constant_dynamic-slice_fusion.3 = (f32[4,48,1024]{2,1,0:T(8,128)S(1)}, f32[4,48,1024]{2,1,0:T(8,128)}, f32[4,48,1024]{2,1,0:T(8,128)}, f32[4,48,1024]{2,1,0:T(8,128)}) fusion(f32[4,192,1024]{2,1,0:T(8,128)} %shard_map.60, s32[]{:T(128)S(6)} %select_n.73, s32[]{:T(128)S(6)} %select_n.76, s32[]{:T(128)S(6)} %select_n.75, s32[]{:T(128)S(6)} %select_n.74), kind=kLoop, calls=%fused_computation.125 | loop fusion | bytes 6291472 | tf_op jit(solution)/shard_map/dynamic_slice | solution.py:219
  163.9 1.8 collective-permute-start.8
  165.8 1.5 collective-permute-start.7
  168.1 15.9 %collective-permute-done.8 = f32[4,48,1024]{2,1,0:T(8,128)} collective-permute-done((f32[4,48,1024]{2,1,0:T(8,128)}, f32[4,48,1024]{2,1,0:T(8,128)}, u32[]{:S(2)}, u32[]{:S(2)}) %collective-permute-start.8) | collective-permute-done | bytes 786464 | tf_op jit(solution)/shard_map/ppermute | solution.py:221
  183.9 2.7 %stack_reshape.15 = f32[1,192,16,64]{3,2,1,0:T(8,128)} reshape(f32[4,48,1024]{2,1,0:T(8,128)} %collective-permute-done.8) | data formatting | bytes 1572864 | tf_op jit(solution)/shard_map/stack;reshape | solution.py:43
  186.6 15.7 %collective-permute-done.7 = f32[4,48,1024]{2,1,0:T(8,128)} collective-permute-done((f32[4,48,1024]{2,1,0:T(8,128)}, f32[4,48,1024]{2,1,0:T(8,128)}, u32[]{:S(2)}, u32[]{:S(2)}) %collective-permute-start.7) | collective-permute-done | bytes 786464 | tf_op jit(solution)/shard_map/ppermute | solution.py:221
  202.3 2.7 %stack_reshape.14 = f32[1,192,16,64]{3,2,1,0:T(8,128)} reshape(f32[4,48,1024]{2,1,0:T(8,128)} %collective-permute-done.7) | data formatting | bytes 1572864 | tf_op jit(solution)/shard_map/stack;reshape | solution.py:43
  204.9 1.6 stack_reshape.13
  206.5 7.5 %fusion.19 = f32[192,64,128]{2,1,0:T(8,128)S(1)} fusion(f32[1,192,16,64]{3,2,0,1:T(8,128)} %bitcast.73, f32[1,192,16,64]{3,2,0,1:T(8,128)} %bitcast.74, f32[1,192,16,64]{3,2,0,1:T(8,128)} %bitcast.75, f32[1,192,16,64]{3,2,0,1:T(8,128)S(1)} %bitcast.72, f32[1,16,128]{2,1,0:T(8,128)S(1)} %get-tuple-element.39, f32[1,16,128]{2,1,0:T(8,128)S(1)} %get-tuple-element.38, ...), kind=kOutput, calls=%fused_computation.33 | convolution fusion | flops 606363648 | bytes 9469952 | tf_op jit(solution)/shard_map/prab,pac->rbc/dot_general | solution.py:47
  214.0 3.3 %multiply_add_fusion = (f32[192,64,64]{2,1,0:T(8,128)S(1)}, f32[192,64,64]{2,1,0:T(8,128)S(1)}) fusion(f32[192,64,128]{2,1,0:T(8,128)S(1)} %fusion.19, f32[64,64]{1,0:T(8,128)S(1)} %get-tuple-element.51, f32[64,64]{1,0:T(8,128)S(1)} %get-tuple-element.52), kind=kLoop, calls=%fused_computation.16 | loop fusion | flops 4718592 | bytes 12615680 | tf_op jit(solution)/shard_map/add | solution.py:59
  217.3 2.7 %fusion.27 = f32[192,20,128]{2,1,0:T(8,128)S(1)} fusion(f32[192,64,64]{2,1,0:T(8,128)S(1)} %get-tuple-element.15, f32[192,64,64]{2,1,0:T(8,128)S(1)} %get-tuple-element.14), kind=kOutput, calls=%fused_computation.41 | convolution fusion | flops 190334464 | bytes 8257536 | tf_op jit(solution)/shard_map/rbc,bq->rqc/dot_general | solution.py:66
  220.0 2.7 %fusion.26 = f32[192,20,128]{2,1,0:T(8,128)S(1)} fusion(f32[192,64,64]{2,1,0:T(8,128)S(1)} %get-tuple-element.15, f32[192,64,64]{2,1,0:T(8,128)S(1)} %get-tuple-element.14), kind=kOutput, calls=%fused_computation.40 | convolution fusion | flops 190334464 | bytes 8257536 | tf_op jit(solution)/shard_map/rbc,bq->rqc/dot_general | solution.py:65
  222.7 2.7 %fusion.22 = (f32[192,20,64]{2,1,0:T(8,128)}, f32[192,20,64]{2,1,0:T(8,128)S(1)}) fusion(f32[192,20,128]{2,1,0:T(8,128)S(1)} %fusion.27, f32[192,20,128]{2,1,0:T(8,128)S(1)} %fusion.26), kind=kLoop, calls=%fused_computation.35 | loop fusion | flops 983040 | bytes 5898240 | tf_op jit(solution)/shard_map/mul | solution.py:69
  225.4 2.0 reshape.171
  227.4 1.6 copy.66
  229.0 0.5 reshape.170
  229.5 1.6 copy.65
  (42 shorter events, 3.6 us)
Async XLA Ops:
  9.1 9.8 %copy-start.7 = (f32[6,5,32]{2,0,1:T(8,128)S(1)}, f32[6,5,32]{2,0,1:T(8,128)}, u32[]{:S(2)}) copy-start(f32[6,5,32]{2,0,1:T(8,128)} %param.7) | copy-start | bytes 11524
  9.1 9.8 %copy-start.1 = (f32[6,32,4,1024]{3,2,1,0:T(4,128)S(1)}, f32[6,32,4,1024]{3,2,1,0:T(4,128)}, u32[]{:S(2)}) copy-start(f32[6,32,4,1024]{3,2,1,0:T(4,128)} %param.4) | copy-start | bytes 9437188
  9.1 56.5 %collective-permute-start = (f32[6,32,3,1024]{3,1,2,0:T(8,128)}, f32[6,32,3,1024]{3,1,2,0:T(8,128)}, u32[]{:S(2)}, u32[]{:S(2)}) collective-permute-start(f32[6,32,3,1024]{3,1,2,0:T(8,128)} %copy.68), channel_id=1, source_target_pairs={{0,4},{4,8},{8,12},{12,16},{16,20},{20,24},{24,28},{1,5},{5,9},{9,... | collective-permute-start | bytes 7077896 | tf_op jit(solution)/shard_map/ppermute | solution.py:26
  15.6 100.4 %collective-permute-start.1 = (f32[6,32,3,1024]{3,1,2,0:T(8,128)}, f32[6,32,3,1024]{3,1,2,0:T(8,128)}, u32[]{:S(2)}, u32[]{:S(2)}) collective-permute-start(f32[6,32,3,1024]{3,1,2,0:T(8,128)} %copy.69), channel_id=1, source_target_pairs={{4,0},{8,4},{12,8},{16,12},{20,16},{24,20},{28,24},{5,1},{9,5},{13... | collective-permute-start | bytes 7077896 | tf_op jit(solution)/shard_map/ppermute | solution.py:29
  19.0 2.8 %copy-start.4 = (f32[6,32]{1,0:T(8,128)}, f32[6,32]{1,0:T(8,128)S(1)}, u32[]{:S(2)}) copy-start(f32[6,32]{1,0:T(8,128)S(1)} %get-tuple-element.46) | copy-start | bytes 2308
  21.8 3.4 %copy-start.3 = (f32[16,4,1024]{2,1,0:T(4,128)S(1)}, f32[16,4,1024]{2,1,0:T(4,128)}, u32[]{:S(2)}) copy-start(f32[16,4,1024]{2,1,0:T(4,128)} %param.5) | copy-start | bytes 786436
  21.8 4.3 %copy-start.6 = (s32[2,4,1024]{2,1,0:T(4,128)S(1)}, s32[2,4,1024]{2,1,0:T(4,128)}, u32[]{:S(2)}) copy-start(s32[2,4,1024]{2,1,0:T(4,128)} %param.6) | copy-start | bytes 98308
  24.6 9.7 %collective-permute-start.3 = (f32[4,192,16]{2,1,0:T(8,128)}, f32[4,192,16]{2,1,0:T(8,128)}, u32[]{:S(2)}, u32[]{:S(2)}) collective-permute-start(f32[4,192,16]{2,1,0:T(8,128)} %get-tuple-element.28), channel_id=1, source_target_pairs={{1,0},{2,1},{3,2},{0,3},{5,4},{6,5},{7,6},{4,7},{9,8},{10,9},{11,1... | collective-permute-start | bytes 147464 | tf_op jit(solution)/shard_map/ppermute | solution.py:29
  25.0 11.4 %collective-permute-start.2 = (f32[4,192,16]{2,1,0:T(8,128)}, f32[4,192,16]{2,1,0:T(8,128)}, u32[]{:S(2)}, u32[]{:S(2)}) collective-permute-start(f32[4,192,16]{2,1,0:T(8,128)} %get-tuple-element.29), channel_id=1, source_target_pairs={{0,1},{1,2},{2,3},{3,0},{4,5},{5,6},{6,7},{7,4},{8,9},{9,10},{10,1... | collective-permute-start | bytes 147464 | tf_op jit(solution)/shard_map/ppermute | solution.py:26
  54.0 64.8 %copy-start.5 = (f32[6,32]{1,0:T(8,128)S(1)}, f32[6,32]{1,0:T(8,128)}, u32[]{:S(2)}) copy-start(f32[6,32]{1,0:T(8,128)} %copy-done.4) | copy-start | bytes 2308
  122.1 2.2 copy-start.2
  124.7 7.6 %collective-permute-start.4 = (f32[6,192,16]{1,2,0:T(8,128)S(1)}, f32[6,192,16]{1,2,0:T(8,128)S(1)}, u32[]{:S(2)}, u32[]{:S(2)}) collective-permute-start(f32[6,192,16]{1,2,0:T(8,128)S(1)} %copy.53), channel_id=1, source_target_pairs={{0,1},{1,2},{2,3},{3,0},{4,5},{5,6},{6,7},{7,4},{8,9},{9,10},{10,1... | collective-permute-start | bytes 221192 | tf_op jit(solution)/shard_map/ppermute | solution.py:26
  130.5 4.0 %collective-permute-start.5 = (f32[6,192,16]{1,2,0:T(8,128)S(1)}, f32[6,192,16]{1,2,0:T(8,128)S(1)}, u32[]{:S(2)}, u32[]{:S(2)}) collective-permute-start(f32[6,192,16]{1,2,0:T(8,128)S(1)} %copy.54), channel_id=1, source_target_pairs={{1,0},{2,1},{3,2},{0,3},{5,4},{6,5},{7,6},{4,7},{9,8},{10,9},{11,1... | collective-permute-start | bytes 221192 | tf_op jit(solution)/shard_map/ppermute | solution.py:29
  148.8 1.7 copy-start
  163.9 20.0 %collective-permute-start.8 = (f32[4,48,1024]{2,1,0:T(8,128)}, f32[4,48,1024]{2,1,0:T(8,128)}, u32[]{:S(2)}, u32[]{:S(2)}) collective-permute-start(f32[4,48,1024]{2,1,0:T(8,128)} %get-tuple-element.25), channel_id=1, source_target_pairs={{0,3},{1,0},{2,1},{3,2},{4,7},{5,4},{6,5},{7,6},{8,11},{9,8},{10,9... | collective-permute-start | bytes 2359304 | tf_op jit(solution)/shard_map/ppermute | solution.py:221
  165.8 36.5 %collective-permute-start.7 = (f32[4,48,1024]{2,1,0:T(8,128)}, f32[4,48,1024]{2,1,0:T(8,128)}, u32[]{:S(2)}, u32[]{:S(2)}) collective-permute-start(f32[4,48,1024]{2,1,0:T(8,128)} %get-tuple-element.26), channel_id=1, source_target_pairs={{0,2},{1,3},{2,0},{3,1},{4,6},{5,7},{6,4},{7,5},{8,10},{9,11},{10,... | collective-permute-start | bytes 2359304 | tf_op jit(solution)/shard_map/ppermute | solution.py:221
  167.2 37.7 %collective-permute-start.6 = (f32[4,48,1024]{2,1,0:T(8,128)}, f32[4,48,1024]{2,1,0:T(8,128)S(1)}, u32[]{:S(2)}, u32[]{:S(2)}) collective-permute-start(f32[4,48,1024]{2,1,0:T(8,128)} %get-tuple-element.27), channel_id=1, source_target_pairs={{0,1},{1,2},{2,3},{3,0},{4,5},{5,6},{6,7},{7,4},{8,9},{9,10},{10,1... | collective-permute-start | bytes 2359304 | tf_op jit(solution)/shard_map/ppermute | solution.py:221

commit v7 on v4

--- a/solution.py
+++ b/solution.py
@@ -169,7 +169,15 @@
 def on_device(fields, weights, stencil, bands):
     n_fields, n_levels, lat_rows, lon_cols = fields.shape
     n_items = n_fields * n_levels
-    below_raw, above_raw = shifted(fields, "lat", ROWS_OUT, 2, False)
+    split_at = n_fields // 2
+    lows = []
+    highs = []
+    for group in (fields[:split_at], fields[split_at:]):
+        low, high = shifted(group, "lat", ROWS_OUT, 2, False)
+        lows.append(low)
+        highs.append(high)
+    below_raw = jnp.concatenate(lows, axis=0)
+    above_raw = jnp.concatenate(highs, axis=0)
 
     width = lon_cols + LANES
     local_rows = vertical_mix(jnp.transpose(fields, (2, 0, 1, 3)), bands)

time: 221 us -> 230 us (1.041); the launches traced: 220 us -> 225 us
  waiting for transfers between devices: 107 us -> 98.7 us
  starting transfers between devices: 10.3 us -> 17.3 us
  other arithmetic: 22.1 us -> 28.7 us
    ppermute x3 -> x4, waiting for transfers between devices: 60.2 us -> 45.5 us  [shifted(): lax.ppermute(lax.slice_in_dim(block, 0, width, axis=dim), axis, backward)]
    ppermute x3 -> x4, waiting for transfers between devices: 14.8 us -> 21.5 us  [shifted(): lax.ppermute(lax.slice_in_dim(block, block.shape[dim] - width, None, axis...]
    ppermute x3 -> x4, starting transfers between devices: 4.82 us -> 9.9 us  [shifted(): lax.ppermute(lax.slice_in_dim(block, 0, width, axis=dim), axis, backward)]
    add x2, other arithmetic: 5.68 us -> 10.5 us  [vertical_mix(): mixed + bands[lead + (slice(None), shift_k, slice(None), None)] * stacked...]
    slice x4, local copies, waits for them, and re-layouts: 7.14 us -> 3.38 us  [shifted(): lax.slice_in_dim(block, 0, width, axis=dim)]
    concatenate x0 -> x2, other arithmetic: none -> 3.57 us  [the longest x1 1.78 us: on_device(): below_raw = jnp.concatenate(lows, axis=0)]
    unnamed x19 -> x35, local copies, waits for them, and re-layouts: 11.8 us -> 13.9 us
    ppermute x3 -> x4, starting transfers between devices: 3.86 us -> 5.82 us  [shifted(): lax.ppermute(lax.slice_in_dim(block, block.shape[dim] - width, None, axis...]
  transfers between devices with their start and end apart: 9 -> 11, of which waited for: 8 -> 8; matrix products, arithmetic and copies ran while one was open for 11% -> 12% of each run, Pallas kernels for 5% -> 5%
where the time goes in v7:
time: 230 us; the launch traced here: 225 us
  waiting for transfers between devices  98.7 us (43%)
  local copies, waits for them, and re-layouts  46 us (20%)
  other arithmetic  28.7 us (12%)
  Pallas kernels  20.6 us (9%)
  starting transfers between devices  17.3 us (8%)
  matrix products  12.9 us (6%)
    ppermute x4, waiting for transfers between devices, shifted(): lax.ppermute(lax.slice_in_dim(block, 0, width, axis=dim), axis, backward)  45.5 us
    ppermute x3, waiting for transfers between devices, on_device(): lax.ppermute(piece, 'lon', [(i, (i + shift) % parts) for i in range(parts)])  31.7 us
    ppermute x4, waiting for transfers between devices, shifted(): lax.ppermute(lax.slice_in_dim(block, block.shape[dim] - width, None, axis...  21.5 us
    pallas_call x2, Pallas kernels, interpolate(): pl.pallas_call(functools.partial(interp_kernel, base is None, lat_rows),...  20.6 us
    unnamed x35, local copies, waits for them, and re-layouts  13.9 us
    concatenate x2, local copies, waits for them, and re-layouts, widen(): return jnp.concatenate([left, block, right], axis=block.ndim - 1)  11.3 us
    add x2, other arithmetic, vertical_mix(): mixed + bands[lead + (slice(None), shift_k, slice(None), None)] * stacked...  10.5 us
    ppermute x4, starting transfers between devices, shifted(): lax.ppermute(lax.slice_in_dim(block, 0, width, axis=dim), axis, backward)  9.9 us
  transfers between devices with their start and end apart: 11, of which 8 were waited for; matrix products, arithmetic and copies ran while one was open for 12% of the time, Pallas kernels for 5%

profile of v7, /device:TPU:24, one launch (start us, length us, event | category | flops | bytes accessed | tf_op | source)
XLA Modules:
  0.0 225.2 jit_solution(17643232403267544691)
XLA Ops:
  0.6 0.8 slice_bitcast_fusion.4
  1.4 7.6 %multiply_add_fusion.1 = f32[4,6,32,1024]{3,0,2,1:T(4,128)S(1)} fusion(f32[4,6,32,1024]{3,0,2,1:T(4,128)} %bitcast.64, f32[6,32]{1,0:T(8,128)S(1)} %get-tuple-element.41, f32[6,32]{1,0:T(8,128)S(1)} %get-tuple-element.42, f32[6,32]{1,0:T(8,128)S(1)} %get-tuple-element.39, f32[6,32]{1,0:T(8,128)S(1)} %get-tuple-element.40, f32[6,32]{1,0:T(8,128)S(1)} %get-tuple-element.38), kind=kLoop, calls=%fused_computation.30 | loop fusion | flops 7077888 | bytes 6295296 | tf_op jit(solution)/shard_map/add | solution.py:151
  9.1 1.8 copy.31
  10.9 1.0 fusion.87
  11.9 0.9 collective-permute-start.5
  12.8 1.9 fusion.88
  14.8 1.7 copy.50
  16.5 3.3 %collective-permute-start.3 = (f32[3,32,3,1024]{3,1,2,0:T(8,128)}, f32[3,32,3,1024]{3,1,2,0:T(8,128)}, u32[]{:S(2)}, u32[]{:S(2)}) collective-permute-start(f32[3,32,3,1024]{3,1,2,0:T(8,128)} %copy.50), channel_id=1, source_target_pairs={{4,0},{8,4},{12,8},{16,12},{20,16},{24,20},{28,24},{5,1},{9,5},{13... | collective-permute-start | bytes 3538952 | tf_op jit(solution)/shard_map/ppermute | solution.py:29
  19.8 1.7 copy.47
  21.5 3.7 %collective-permute-start = (f32[3,32,3,1024]{3,1,2,0:T(8,128)}, f32[3,32,3,1024]{3,1,2,0:T(8,128)}, u32[]{:S(2)}, u32[]{:S(2)}) collective-permute-start(f32[3,32,3,1024]{3,1,2,0:T(8,128)} %copy.47), channel_id=1, source_target_pairs={{0,4},{4,8},{8,12},{12,16},{16,20},{20,24},{24,28},{1,5},{5,9},{9,... | collective-permute-start | bytes 3538952 | tf_op jit(solution)/shard_map/ppermute | solution.py:26
  25.2 1.7 copy.48
  26.9 1.9 collective-permute-start.1
  28.9 1.7 copy.49
  30.6 4.8 %collective-permute-start.2 = (f32[3,32,3,1024]{3,1,2,0:T(8,128)}, f32[3,32,3,1024]{3,1,2,0:T(8,128)}, u32[]{:S(2)}, u32[]{:S(2)}) collective-permute-start(f32[3,32,3,1024]{3,1,2,0:T(8,128)} %copy.49), channel_id=1, source_target_pairs={{4,0},{8,4},{12,8},{16,12},{20,16},{24,20},{28,24},{5,1},{9,5},{13... | collective-permute-start | bytes 3538952 | tf_op jit(solution)/shard_map/ppermute | solution.py:29
  36.6 0.8 fusion.45
  37.4 1.1 copy.68
  39.5 6.9 %collective-permute-done.4 = f32[4,192,16]{2,1,0:T(8,128)} collective-permute-done((f32[4,192,16]{2,1,0:T(8,128)}, f32[4,192,16]{2,1,0:T(8,128)}, u32[]{:S(2)}, u32[]{:S(2)}) %collective-permute-start.4) | collective-permute-done | bytes 49184 | tf_op jit(solution)/shard_map/ppermute | solution.py:26
  46.3 4.4 %concatenate.26 = f32[4,192,1056]{2,1,0:T(8,128)} concatenate(f32[4,192,16]{2,1,0:T(8,128)} %collective-permute-done.4, f32[4,192,1024]{2,1,0:T(8,128)S(1)} %bitcast.68, f32[4,192,16]{2,1,0:T(8,128)} %copy-done.2), dimensions={2} | concatenate | bytes 6488064 | tf_op jit(solution)/shard_map/concatenate | solution.py:159
  50.7 2.6 %fusion.17 = (bf16[4,192,1152]{2,1,0:T(8,128)(2,1)S(1)}, bf16[4,192,1152]{2,1,0:T(8,128)(2,1)S(1)}) fusion(f32[4,192,1056]{2,1,0:T(8,128)} %concatenate.26), kind=kLoop, calls=%fused_computation.29 | loop fusion | flops 3538944 | bytes 6782976 | tf_op jit(solution)/shard_map/convert_element_type | solution.py:166
  53.4 10.5 %shard_map.59.refs_3_ = f32[4,192,1024]{2,1,0:T(8,128)} custom-call(bf16[4,192,1152]{2,1,0:T(8,128)(2,1)S(1)} %get-tuple-element.21.refs_0_, bf16[4,192,1152]{2,1,0:T(8,128)(2,1)S(1)} %get-tuple-element.20.refs_1_, f32[4,24,1024]{2,1,0:T(8,128)S(1)} %maximum_maximum_fusion.refs_2_), custom_call_target="tpu_custom_call" | custom-call | tf_op jit(solution)/shard_map/pallas_call | solution.py:133
  63.8 13.4 %collective-permute-done.1 = f32[3,32,3,1024]{3,1,2,0:T(8,128)} collective-permute-done((f32[3,32,3,1024]{3,1,2,0:T(8,128)}, f32[3,32,3,1024]{3,1,2,0:T(8,128)}, u32[]{:S(2)}, u32[]{:S(2)}) %collective-permute-start.1) | collective-permute-done | bytes 1179680 | tf_op jit(solution)/shard_map/ppermute | solution.py:26
  77.3 1.8 pad_maximum_fusion.1
  79.1 19.1 %collective-permute-done.3 = f32[3,32,3,1024]{3,1,2,0:T(8,128)} collective-permute-done((f32[3,32,3,1024]{3,1,2,0:T(8,128)}, f32[3,32,3,1024]{3,1,2,0:T(8,128)}, u32[]{:S(2)}, u32[]{:S(2)}) %collective-permute-start.3) | collective-permute-done | bytes 1179680 | tf_op jit(solution)/shard_map/ppermute | solution.py:29
  98.1 23.8 %collective-permute-done.2 = f32[3,32,3,1024]{3,1,2,0:T(8,128)} collective-permute-done((f32[3,32,3,1024]{3,1,2,0:T(8,128)}, f32[3,32,3,1024]{3,1,2,0:T(8,128)}, u32[]{:S(2)}, u32[]{:S(2)}) %collective-permute-start.2) | collective-permute-done | bytes 1179680 | tf_op jit(solution)/shard_map/ppermute | solution.py:29
  122.0 1.8 pad_maximum_fusion.2
  124.5 2.9 %fusion.13 = f32[6,6,32,1024]{3,2,0,1:T(8,128)S(1)} fusion(f32[6,6,32,1024]{3,2,0,1:T(8,128)S(1)} %maximum_bitcast_fusion, f32[6,32]{1,0:T(8,128)S(1)} %copy-done.10, f32[6,32]{1,0:T(8,128)S(1)} %copy-done.12, f32[6,32]{1,0:T(8,128)S(1)} %copy-done.6, f32[6,32]{1,0:T(8,128)S(1)} %copy-done.8, f32[6,32]{1,0:T(8,128)S(1)} %copy-done.4), kind=kLoop, calls=%fused_computation.24 | loop fusion | flops 10616832 | bytes 9441024 | tf_op jit(solution)/shard_map/add | solution.py:151
  127.8 2.1 copy-done.1
  130.4 0.9 collective-permute-start.7
  131.6 2.6 %collective-permute-done.7 = f32[6,192,16]{1,2,0:T(8,128)S(1)} collective-permute-done((f32[6,192,16]{1,2,0:T(8,128)S(1)}, f32[6,192,16]{1,2,0:T(8,128)S(1)}, u32[]{:S(2)}, u32[]{:S(2)}) %collective-permute-start.7) | collective-permute-done | bytes 73760 | tf_op jit(solution)/shard_map/ppermute | solution.py:29
  134.4 1.2 collective-permute-done.6
  135.8 6.9 %concatenate.29 = f32[6,192,1056]{2,1,0:T(8,128)} concatenate(f32[6,192,16]{2,1,0:T(8,128)S(1)} %copy.38, f32[6,192,1024]{2,1,0:T(8,128)} %bitcast.66, f32[6,192,16]{2,1,0:T(8,128)S(1)} %copy.39), dimensions={2} | concatenate | bytes 9732096 | tf_op jit(solution)/shard_map/concatenate | solution.py:159
  142.7 3.6 %fusion.8 = (bf16[6,192,1152]{2,1,0:T(8,128)(2,1)S(1)}, bf16[6,192,1152]{2,1,0:T(8,128)(2,1)S(1)}) fusion(f32[6,192,1056]{2,1,0:T(8,128)} %concatenate.29), kind=kLoop, calls=%fused_computation.17 | loop fusion | flops 5308416 | bytes 10174464 | tf_op jit(solution)/shard_map/convert_element_type | solution.py:166
  146.3 10.1 %shard_map.60 = f32[4,192,1024]{2,1,0:T(8,128)} custom-call(bf16[6,192,1152]{2,1,0:T(8,128)(2,1)S(1)} %get-tuple-element.15.refs_0_, bf16[6,192,1152]{2,1,0:T(8,128)(2,1)S(1)} %get-tuple-element.14.refs_1_, f32[4,24,1024]{2,1,0:T(8,128)S(1)} %maximum_maximum_fusion.refs_2_, f32[4,192,1024]{2,1,0:T(8,128)} %shard_map.59.refs_3_), custom_call_target="tpu_custom_call" | custom-call | tf_op jit(solution)/shard_map/pallas_call | solution.py:133
  156.4 3.3 %constant_dynamic-slice_fusion.3 = (f32[4,48,1024]{2,1,0:T(8,128)S(1)}, f32[4,48,1024]{2,1,0:T(8,128)}, f32[4,48,1024]{2,1,0:T(8,128)}, f32[4,48,1024]{2,1,0:T(8,128)}) fusion(f32[4,192,1024]{2,1,0:T(8,128)} %shard_map.60, s32[]{:T(128)S(6)} %select_n.73, s32[]{:T(128)S(6)} %select_n.76, s32[]{:T(128)S(6)} %select_n.75, s32[]{:T(128)S(6)} %select_n.74), kind=kLoop, calls=%fused_computation.125 | loop fusion | bytes 6291472 | tf_op jit(solution)/shard_map/dynamic_slice | solution.py:217
  159.7 1.0 collective-permute-start.10
  162.1 16.9 %collective-permute-done.10 = f32[4,48,1024]{2,1,0:T(8,128)} collective-permute-done((f32[4,48,1024]{2,1,0:T(8,128)}, f32[4,48,1024]{2,1,0:T(8,128)}, u32[]{:S(2)}, u32[]{:S(2)}) %collective-permute-start.10) | collective-permute-done | bytes 786464 | tf_op jit(solution)/shard_map/ppermute | solution.py:219
  179.0 2.6 %stack_reshape.15 = f32[1,192,16,64]{3,2,1,0:T(8,128)} reshape(f32[4,48,1024]{2,1,0:T(8,128)} %collective-permute-done.10) | data formatting | bytes 1572864 | tf_op jit(solution)/shard_map/stack;reshape | solution.py:43
  181.6 14.8 %collective-permute-done.9 = f32[4,48,1024]{2,1,0:T(8,128)} collective-permute-done((f32[4,48,1024]{2,1,0:T(8,128)}, f32[4,48,1024]{2,1,0:T(8,128)}, u32[]{:S(2)}, u32[]{:S(2)}) %collective-permute-start.9) | collective-permute-done | bytes 786464 | tf_op jit(solution)/shard_map/ppermute | solution.py:219
  196.4 2.6 %stack_reshape.14 = f32[1,192,16,64]{3,2,1,0:T(8,128)} reshape(f32[4,48,1024]{2,1,0:T(8,128)} %collective-permute-done.9) | data formatting | bytes 1572864 | tf_op jit(solution)/shard_map/stack;reshape | solution.py:43
  199.0 1.6 stack_reshape.13
  200.7 7.5 %fusion.19 = f32[192,64,128]{2,1,0:T(8,128)S(1)} fusion(f32[1,192,16,64]{3,2,0,1:T(8,128)} %bitcast.72, f32[1,192,16,64]{3,2,0,1:T(8,128)} %bitcast.73, f32[1,192,16,64]{3,2,0,1:T(8,128)} %bitcast.74, f32[1,192,16,64]{3,2,0,1:T(8,128)S(1)} %bitcast.71, f32[1,16,128]{2,1,0:T(8,128)S(1)} %get-tuple-element.35, f32[1,16,128]{2,1,0:T(8,128)S(1)} %get-tuple-element.34, ...), kind=kOutput, calls=%fused_computation.33 | convolution fusion | flops 606363648 | bytes 9469952 | tf_op jit(solution)/shard_map/prab,pac->rbc/dot_general | solution.py:47
  208.1 3.3 %multiply_add_fusion = (f32[192,64,64]{2,1,0:T(8,128)S(1)}, f32[192,64,64]{2,1,0:T(8,128)S(1)}) fusion(f32[192,64,128]{2,1,0:T(8,128)S(1)} %fusion.19, f32[64,64]{1,0:T(8,128)S(1)} %get-tuple-element.47, f32[64,64]{1,0:T(8,128)S(1)} %get-tuple-element.48), kind=kLoop, calls=%fused_computation.16 | loop fusion | flops 4718592 | bytes 12615680 | tf_op jit(solution)/shard_map/add | solution.py:59
  211.4 2.7 %fusion.27 = f32[192,20,128]{2,1,0:T(8,128)S(1)} fusion(f32[192,64,64]{2,1,0:T(8,128)S(1)} %get-tuple-element.13, f32[192,64,64]{2,1,0:T(8,128)S(1)} %get-tuple-element.12), kind=kOutput, calls=%fused_computation.43 | convolution fusion | flops 190334464 | bytes 8257536 | tf_op jit(solution)/shard_map/rbc,bq->rqc/dot_general | solution.py:66
  214.2 2.7 %fusion.26 = f32[192,20,128]{2,1,0:T(8,128)S(1)} fusion(f32[192,64,64]{2,1,0:T(8,128)S(1)} %get-tuple-element.13, f32[192,64,64]{2,1,0:T(8,128)S(1)} %get-tuple-element.12), kind=kOutput, calls=%fused_computation.42 | convolution fusion | flops 190334464 | bytes 8257536 | tf_op jit(solution)/shard_map/rbc,bq->rqc/dot_general | solution.py:65
  216.9 2.7 %fusion.22 = (f32[192,20,64]{2,1,0:T(8,128)}, f32[192,20,64]{2,1,0:T(8,128)S(1)}) fusion(f32[192,20,128]{2,1,0:T(8,128)S(1)} %fusion.27, f32[192,20,128]{2,1,0:T(8,128)S(1)} %fusion.26), kind=kLoop, calls=%fused_computation.35 | loop fusion | flops 983040 | bytes 5898240 | tf_op jit(solution)/shard_map/mul | solution.py:69
  219.6 2.0 reshape.171
  221.5 1.6 copy.45
  223.6 1.6 copy.44
  (52 shorter events, 6.2 us)
Async XLA Ops:
  1.4 7.6 %copy-start.3 = (f32[6,32]{1,0:T(8,128)}, f32[6,32]{1,0:T(8,128)S(1)}, u32[]{:S(2)}) copy-start(f32[6,32]{1,0:T(8,128)S(1)} %get-tuple-element.38) | copy-start | bytes 2308
  1.4 7.6 %copy-start.5 = (f32[6,32]{1,0:T(8,128)}, f32[6,32]{1,0:T(8,128)S(1)}, u32[]{:S(2)}) copy-start(f32[6,32]{1,0:T(8,128)S(1)} %get-tuple-element.39) | copy-start | bytes 2308
  1.4 7.7 %copy-start.7 = (f32[6,32]{1,0:T(8,128)}, f32[6,32]{1,0:T(8,128)S(1)}, u32[]{:S(2)}) copy-start(f32[6,32]{1,0:T(8,128)S(1)} %get-tuple-element.40) | copy-start | bytes 2308
  1.4 7.7 %copy-start.9 = (f32[6,32]{1,0:T(8,128)}, f32[6,32]{1,0:T(8,128)S(1)}, u32[]{:S(2)}) copy-start(f32[6,32]{1,0:T(8,128)S(1)} %get-tuple-element.41) | copy-start | bytes 2308
  1.4 7.7 %copy-start.11 = (f32[6,32]{1,0:T(8,128)}, f32[6,32]{1,0:T(8,128)S(1)}, u32[]{:S(2)}) copy-start(f32[6,32]{1,0:T(8,128)S(1)} %get-tuple-element.42) | copy-start | bytes 2308
  9.1 3.8 %copy-start = (f32[6,32,4,1024]{3,2,1,0:T(4,128)S(1)}, f32[6,32,4,1024]{3,2,1,0:T(4,128)}, u32[]{:S(2)}) copy-start(f32[6,32,4,1024]{3,2,1,0:T(4,128)} %param.4) | copy-start | bytes 9437188
  11.9 26.7 %collective-permute-start.5 = (f32[4,192,16]{2,1,0:T(8,128)}, f32[4,192,16]{2,1,0:T(8,128)S(1)}, u32[]{:S(2)}, u32[]{:S(2)}) collective-permute-start(f32[4,192,16]{2,1,0:T(8,128)} %get-tuple-element.26), channel_id=1, source_target_pairs={{1,0},{2,1},{3,2},{0,3},{5,4},{6,5},{7,6},{4,7},{9,8},{10,9},{11,1... | collective-permute-start | bytes 147464 | tf_op jit(solution)/shard_map/ppermute | solution.py:29
  16.5 81.7 %collective-permute-start.3 = (f32[3,32,3,1024]{3,1,2,0:T(8,128)}, f32[3,32,3,1024]{3,1,2,0:T(8,128)}, u32[]{:S(2)}, u32[]{:S(2)}) collective-permute-start(f32[3,32,3,1024]{3,1,2,0:T(8,128)} %copy.50), channel_id=1, source_target_pairs={{4,0},{8,4},{12,8},{16,12},{20,16},{24,20},{28,24},{5,1},{9,5},{13... | collective-permute-start | bytes 3538952 | tf_op jit(solution)/shard_map/ppermute | solution.py:29
  21.5 13.9 %copy-start.13 = (s32[2,4,1024]{2,1,0:T(4,128)S(1)}, s32[2,4,1024]{2,1,0:T(4,128)}, u32[]{:S(2)}) copy-start(s32[2,4,1024]{2,1,0:T(4,128)} %param.6) | copy-start | bytes 98308
  21.5 42.3 %collective-permute-start = (f32[3,32,3,1024]{3,1,2,0:T(8,128)}, f32[3,32,3,1024]{3,1,2,0:T(8,128)}, u32[]{:S(2)}, u32[]{:S(2)}) collective-permute-start(f32[3,32,3,1024]{3,1,2,0:T(8,128)} %copy.47), channel_id=1, source_target_pairs={{0,4},{4,8},{8,12},{12,16},{16,20},{20,24},{24,28},{1,5},{5,9},{9,... | collective-permute-start | bytes 3538952 | tf_op jit(solution)/shard_map/ppermute | solution.py:26
  26.9 50.4 %collective-permute-start.1 = (f32[3,32,3,1024]{3,1,2,0:T(8,128)}, f32[3,32,3,1024]{3,1,2,0:T(8,128)}, u32[]{:S(2)}, u32[]{:S(2)}) collective-permute-start(f32[3,32,3,1024]{3,1,2,0:T(8,128)} %copy.48), channel_id=1, source_target_pairs={{0,4},{4,8},{8,12},{12,16},{16,20},{20,24},{24,28},{1,5},{5,9},{9,... | collective-permute-start | bytes 3538952 | tf_op jit(solution)/shard_map/ppermute | solution.py:26
  30.6 91.4 %collective-permute-start.2 = (f32[3,32,3,1024]{3,1,2,0:T(8,128)}, f32[3,32,3,1024]{3,1,2,0:T(8,128)}, u32[]{:S(2)}, u32[]{:S(2)}) collective-permute-start(f32[3,32,3,1024]{3,1,2,0:T(8,128)} %copy.49), channel_id=1, source_target_pairs={{4,0},{8,4},{12,8},{16,12},{20,16},{24,20},{28,24},{5,1},{9,5},{13... | collective-permute-start | bytes 3538952 | tf_op jit(solution)/shard_map/ppermute | solution.py:29
  38.6 0.7 copy-start.2
  38.6 7.7 %collective-permute-start.4 = (f32[4,192,16]{2,1,0:T(8,128)}, f32[4,192,16]{2,1,0:T(8,128)}, u32[]{:S(2)}, u32[]{:S(2)}) collective-permute-start(f32[4,192,16]{2,1,0:T(8,128)} %get-tuple-element.27), channel_id=1, source_target_pairs={{0,1},{1,2},{2,3},{3,0},{4,5},{5,6},{6,7},{7,4},{8,9},{9,10},{10,1... | collective-permute-start | bytes 147464 | tf_op jit(solution)/shard_map/ppermute | solution.py:26
  123.8 0.7 copy-start.4
  123.8 0.7 copy-start.6
  123.8 0.7 copy-start.8
  123.8 0.7 copy-start.10
  123.8 0.7 copy-start.12
  127.8 2.2 copy-start.1
  130.4 3.8 %collective-permute-start.7 = (f32[6,192,16]{1,2,0:T(8,128)S(1)}, f32[6,192,16]{1,2,0:T(8,128)S(1)}, u32[]{:S(2)}, u32[]{:S(2)}) collective-permute-start(f32[6,192,16]{1,2,0:T(8,128)S(1)} %copy.37), channel_id=1, source_target_pairs={{1,0},{2,1},{3,2},{0,3},{5,4},{6,5},{7,6},{4,7},{9,8},{10,9},{11,1... | collective-permute-start | bytes 221192 | tf_op jit(solution)/shard_map/ppermute | solution.py:29
  131.5 4.1 %collective-permute-start.6 = (f32[6,192,16]{1,2,0:T(8,128)S(1)}, f32[6,192,16]{1,2,0:T(8,128)S(1)}, u32[]{:S(2)}, u32[]{:S(2)}) collective-permute-start(f32[6,192,16]{1,2,0:T(8,128)S(1)} %copy.36), channel_id=1, source_target_pairs={{0,1},{1,2},{2,3},{3,0},{4,5},{5,6},{6,7},{7,4},{8,9},{9,10},{10,1... | collective-permute-start | bytes 221192 | tf_op jit(solution)/shard_map/ppermute | solution.py:26
  159.7 19.3 %collective-permute-start.10 = (f32[4,48,1024]{2,1,0:T(8,128)}, f32[4,48,1024]{2,1,0:T(8,128)}, u32[]{:S(2)}, u32[]{:S(2)}) collective-permute-start(f32[4,48,1024]{2,1,0:T(8,128)} %get-tuple-element.23), channel_id=1, source_target_pairs={{0,3},{1,0},{2,1},{3,2},{4,7},{5,4},{6,5},{7,6},{8,11},{9,8},{10,9... | collective-permute-start | bytes 2359304 | tf_op jit(solution)/shard_map/ppermute | solution.py:219
  160.7 35.7 %collective-permute-start.9 = (f32[4,48,1024]{2,1,0:T(8,128)}, f32[4,48,1024]{2,1,0:T(8,128)}, u32[]{:S(2)}, u32[]{:S(2)}) collective-permute-start(f32[4,48,1024]{2,1,0:T(8,128)} %get-tuple-element.24), channel_id=1, source_target_pairs={{0,2},{1,3},{2,0},{3,1},{4,6},{5,7},{6,4},{7,5},{8,10},{9,11},{10,... | collective-permute-start | bytes 2359304 | tf_op jit(solution)/shard_map/ppermute | solution.py:219
  161.1 38.0 %collective-permute-start.8 = (f32[4,48,1024]{2,1,0:T(8,128)}, f32[4,48,1024]{2,1,0:T(8,128)S(1)}, u32[]{:S(2)}, u32[]{:S(2)}) collective-permute-start(f32[4,48,1024]{2,1,0:T(8,128)} %get-tuple-element.25), channel_id=1, source_target_pairs={{0,1},{1,2},{2,3},{3,0},{4,5},{5,6},{6,7},{7,4},{8,9},{9,10},{10,1... | collective-permute-start | bytes 2359304 | tf_op jit(solution)/shard_map/ppermute | solution.py:219

commit v8 on v4

--- a/solution.py
+++ b/solution.py
@@ -114,9 +114,13 @@
             m_lo = (matrix - m_hi.astype(jnp.float32)).astype(jnp.bfloat16)
             x_hi = hi_ref[index, :, pl.ds(start, WINDOW)]
             x_lo = lo_ref[index, :, pl.ds(start, WINDOW)]
-            both = jnp.dot(x_hi, jnp.concatenate([m_hi, m_lo], axis=1), preferred_element_type=jnp.float32)
-            acc = acc + both[:, :LANES] + both[:, LANES:]
-            acc = acc + jnp.dot(x_lo, m_hi, preferred_element_type=jnp.float32)
+            rows_hi = x_hi.shape[0]
+            both = jnp.dot(
+                jnp.concatenate([x_hi, x_lo], axis=0),
+                jnp.concatenate([m_hi, m_lo], axis=1),
+                preferred_element_type=jnp.float32,
+            )
+            acc = acc + both[:rows_hi, :LANES] + both[:rows_hi, LANES:] + both[rows_hi:, :LANES]
         out_ref[row] = acc
 
 

time: 221 us -> 221 us (level)
  no operation moved by 1% of the time
where the time goes in v8:
time: 221 us; the launch traced here: 220 us
  waiting for transfers between devices  107 us (48%)
  local copies, waits for them, and re-layouts  46.2 us (21%)
  other arithmetic  22.1 us (10%)
  Pallas kernels  20.2 us (9%)
  matrix products  12.9 us (6%)
  starting transfers between devices  10.3 us (5%)
    ppermute x3, waiting for transfers between devices, shifted(): lax.ppermute(lax.slice_in_dim(block, 0, width, axis=dim), axis, backward)  60.2 us
    ppermute x3, waiting for transfers between devices, on_device(): lax.ppermute(piece, 'lon', [(i, (i + shift) % parts) for i in range(parts)])  31.6 us
    pallas_call x2, Pallas kernels, interpolate(): pl.pallas_call(functools.partial(interp_kernel, base is None, lat_rows),...  20.2 us
    ppermute x3, waiting for transfers between devices, shifted(): lax.ppermute(lax.slice_in_dim(block, block.shape[dim] - width, None, axis...  15.2 us
    unnamed x19, local copies, waits for them, and re-layouts  11.8 us
    concatenate x2, local copies, waits for them, and re-layouts, widen(): return jnp.concatenate([left, block, right], axis=block.ndim - 1)  11.2 us
    dot_general x1, matrix products, spectrum(): jnp.einsum('prab,pac->rbc', folded, table, precision=highest)  7.48 us
    another operation x4, local copies, waits for them, and re-layouts, spectrum(): jnp.stack([piece.reshape(n_rows * n_items, per_piece, RADIX) for piece in...  7.33 us
  transfers between devices with their start and end apart: 9, of which 8 were waited for; matrix products, arithmetic and copies ran while one was open for 11% of the time, Pallas kernels for 5%

profile of v8, /device:TPU:24, one launch (start us, length us, event | category | flops | bytes accessed | tf_op | source)
XLA Modules:
  0.0 219.7 jit_solution(5159820949810918774)
XLA Ops:
  0.6 5.7 %fusion.88 = (f32[6,32,3,1024]{3,2,1,0:T(4,128)S(1)}, f32[6,32,3,1024]{3,2,1,0:T(4,128)S(1)}) fusion(f32[6,32,4,1024]{3,2,1,0:T(4,128)} %param.4), kind=kLoop, calls=%fused_computation.137 | loop fusion | bytes 9437184 | tf_op jit(solution)/shard_map/slice | solution.py:29
  6.3 2.8 %copy.45 = f32[6,32,3,1024]{3,1,2,0:T(8,128)} copy(f32[6,32,3,1024]{3,2,1,0:T(4,128)S(1)} %get-tuple-element.29) | data formatting | bytes 4718592
  9.1 3.7 %collective-permute-start = (f32[6,32,3,1024]{3,1,2,0:T(8,128)}, f32[6,32,3,1024]{3,1,2,0:T(8,128)}, u32[]{:S(2)}, u32[]{:S(2)}) collective-permute-start(f32[6,32,3,1024]{3,1,2,0:T(8,128)} %copy.45), channel_id=1, source_target_pairs={{0,4},{4,8},{8,12},{12,16},{16,20},{20,24},{24,28},{1,5},{5,9},{9,... | collective-permute-start | bytes 7077896 | tf_op jit(solution)/shard_map/ppermute | solution.py:26
  12.8 2.8 %copy.46 = f32[6,32,3,1024]{3,1,2,0:T(8,128)} copy(f32[6,32,3,1024]{3,2,1,0:T(4,128)S(1)} %get-tuple-element.28) | data formatting | bytes 4718592
  15.6 3.3 %collective-permute-start.1 = (f32[6,32,3,1024]{3,1,2,0:T(8,128)}, f32[6,32,3,1024]{3,1,2,0:T(8,128)}, u32[]{:S(2)}, u32[]{:S(2)}) collective-permute-start(f32[6,32,3,1024]{3,1,2,0:T(8,128)} %copy.46), channel_id=1, source_target_pairs={{4,0},{8,4},{12,8},{16,12},{20,16},{24,20},{28,24},{5,1},{9,5},{13... | collective-permute-start | bytes 7077896 | tf_op jit(solution)/shard_map/ppermute | solution.py:29
  19.0 2.8 %multiply_add_fusion.1 = f32[4,6,32,1024]{3,0,2,1:T(4,128)S(1)} fusion(f32[4,6,32,1024]{3,0,2,1:T(4,128)S(1)} %bitcast.64, f32[6,32]{1,0:T(8,128)S(1)} %get-tuple-element.39, f32[6,32]{1,0:T(8,128)S(1)} %get-tuple-element.40, f32[6,32]{1,0:T(8,128)S(1)} %get-tuple-element.37, f32[6,32]{1,0:T(8,128)S(1)} %get-tuple-element.38, f32[6,32]{1,0:T(8,128)S(1)} %get-tuple-element.36), kind=kLoop, calls=%fused_computation.30 | loop fusion | flops 7077888 | bytes 6295296 | tf_op jit(solution)/shard_map/add | solution.py:155
  21.8 1.8 copy.29
  23.6 1.0 fusion.87
  24.6 0.4 collective-permute-start.3
  25.2 0.9 copy.64
  26.2 1.1 maximum_maximum_fusion.refs_2_
  27.3 7.1 %collective-permute-done.3 = f32[4,192,16]{2,1,0:T(8,128)} collective-permute-done((f32[4,192,16]{2,1,0:T(8,128)}, f32[4,192,16]{2,1,0:T(8,128)}, u32[]{:S(2)}, u32[]{:S(2)}) %collective-permute-start.3) | collective-permute-done | bytes 49184 | tf_op jit(solution)/shard_map/ppermute | solution.py:29
  34.4 2.1 collective-permute-done.2
  36.4 4.4 %concatenate.18 = f32[4,192,1056]{2,1,0:T(8,128)} concatenate(f32[4,192,16]{2,1,0:T(8,128)} %collective-permute-done.2, f32[4,192,1024]{2,1,0:T(8,128)S(1)} %bitcast.68, f32[4,192,16]{2,1,0:T(8,128)} %collective-permute-done.3), dimensions={2} | concatenate | bytes 6488064 | tf_op jit(solution)/shard_map/concatenate | solution.py:163
  40.8 2.6 %fusion.17 = (bf16[4,192,1152]{2,1,0:T(8,128)(2,1)S(1)}, bf16[4,192,1152]{2,1,0:T(8,128)(2,1)S(1)}) fusion(f32[4,192,1056]{2,1,0:T(8,128)} %concatenate.18), kind=kLoop, calls=%fused_computation.29 | loop fusion | flops 3538944 | bytes 6782976 | tf_op jit(solution)/shard_map/convert_element_type | solution.py:170
  43.4 10.1 %shard_map.59.refs_3_ = f32[4,192,1024]{2,1,0:T(8,128)} custom-call(bf16[4,192,1152]{2,1,0:T(8,128)(2,1)S(1)} %get-tuple-element.21.refs_0_, bf16[4,192,1152]{2,1,0:T(8,128)(2,1)S(1)} %get-tuple-element.20.refs_1_, f32[4,24,1024]{2,1,0:T(8,128)S(1)} %maximum_maximum_fusion.refs_2_), custom_call_target="tpu_custom_call" | custom-call | tf_op jit(solution)/shard_map/pallas_call | solution.py:137
  53.6 12.0 %collective-permute-done = f32[6,32,3,1024]{3,1,2,0:T(8,128)} collective-permute-done((f32[6,32,3,1024]{3,1,2,0:T(8,128)}, f32[6,32,3,1024]{3,1,2,0:T(8,128)}, u32[]{:S(2)}, u32[]{:S(2)}) %collective-permute-start) | collective-permute-done | bytes 2359328 | tf_op jit(solution)/shard_map/ppermute | solution.py:26
  65.6 50.5 %collective-permute-done.1 = f32[6,32,3,1024]{3,1,2,0:T(8,128)} collective-permute-done((f32[6,32,3,1024]{3,1,2,0:T(8,128)}, f32[6,32,3,1024]{3,1,2,0:T(8,128)}, u32[]{:S(2)}, u32[]{:S(2)}) %collective-permute-start.1) | collective-permute-done | bytes 2359328 | tf_op jit(solution)/shard_map/ppermute | solution.py:29
  116.0 2.8 %maximum_bitcast_fusion = f32[6,6,32,1024]{3,2,0,1:T(8,128)S(1)} fusion(f32[6,32,3,1024]{3,1,2,0:T(8,128)} %collective-permute-done.1, f32[6,32,3,1024]{3,1,2,0:T(8,128)} %collective-permute-done), kind=kLoop, calls=%fused_computation.28 | loop fusion | flops 1179648 | bytes 9437184 | tf_op jit(solution)/shard_map/transpose | solution.py:202
  118.8 2.9 %fusion.13 = f32[6,6,32,1024]{3,2,0,1:T(8,128)S(1)} fusion(f32[6,6,32,1024]{3,2,0,1:T(8,128)S(1)} %maximum_bitcast_fusion, f32[6,32]{1,0:T(8,128)S(1)} %get-tuple-element.39, f32[6,32]{1,0:T(8,128)S(1)} %copy-done.4, f32[6,32]{1,0:T(8,128)S(1)} %get-tuple-element.37, f32[6,32]{1,0:T(8,128)S(1)} %get-tuple-element.38, f32[6,32]{1,0:T(8,128)S(1)} %get-tuple-element.36), kind=kLoop, calls=%fused_computation.24 | loop fusion | flops 10616832 | bytes 9441024 | tf_op jit(solution)/shard_map/add | solution.py:155
  121.7 0.4 copy.33
  122.1 2.1 copy-done.1
  124.4 0.2 copy.35
  124.6 1.1 collective-permute-start.5
  125.8 0.2 copy.34
  126.1 2.7 %collective-permute-done.5 = f32[6,192,16]{1,2,0:T(8,128)S(1)} collective-permute-done((f32[6,192,16]{1,2,0:T(8,128)S(1)}, f32[6,192,16]{1,2,0:T(8,128)S(1)}, u32[]{:S(2)}, u32[]{:S(2)}) %collective-permute-start.5) | collective-permute-done | bytes 73760 | tf_op jit(solution)/shard_map/ppermute | solution.py:29
  129.0 1.1 collective-permute-done.4
  130.3 6.9 %concatenate.21 = f32[6,192,1056]{2,1,0:T(8,128)} concatenate(f32[6,192,16]{2,1,0:T(8,128)S(1)} %copy.36, f32[6,192,1024]{2,1,0:T(8,128)} %bitcast.66, f32[6,192,16]{2,1,0:T(8,128)S(1)} %copy.37), dimensions={2} | concatenate | bytes 9732096 | tf_op jit(solution)/shard_map/concatenate | solution.py:163
  137.2 3.6 %fusion.8 = (bf16[6,192,1152]{2,1,0:T(8,128)(2,1)S(1)}, bf16[6,192,1152]{2,1,0:T(8,128)(2,1)S(1)}) fusion(f32[6,192,1056]{2,1,0:T(8,128)} %concatenate.21), kind=kLoop, calls=%fused_computation.17 | loop fusion | flops 5308416 | bytes 10174464 | tf_op jit(solution)/shard_map/convert_element_type | solution.py:170
  140.7 10.1 %shard_map.60 = f32[4,192,1024]{2,1,0:T(8,128)} custom-call(bf16[6,192,1152]{2,1,0:T(8,128)(2,1)S(1)} %get-tuple-element.15.refs_0_, bf16[6,192,1152]{2,1,0:T(8,128)(2,1)S(1)} %get-tuple-element.14.refs_1_, f32[4,24,1024]{2,1,0:T(8,128)S(1)} %maximum_maximum_fusion.refs_2_, f32[4,192,1024]{2,1,0:T(8,128)} %shard_map.59.refs_3_), custom_call_target="tpu_custom_call" | custom-call | tf_op jit(solution)/shard_map/pallas_call | solution.py:137
  150.8 3.3 %constant_dynamic-slice_fusion.3 = (f32[4,48,1024]{2,1,0:T(8,128)S(1)}, f32[4,48,1024]{2,1,0:T(8,128)}, f32[4,48,1024]{2,1,0:T(8,128)}, f32[4,48,1024]{2,1,0:T(8,128)}) fusion(f32[4,192,1024]{2,1,0:T(8,128)} %shard_map.60, s32[]{:T(128)S(6)} %select_n.73, s32[]{:T(128)S(6)} %select_n.76, s32[]{:T(128)S(6)} %select_n.75, s32[]{:T(128)S(6)} %select_n.74), kind=kLoop, calls=%fused_computation.123 | loop fusion | bytes 6291472 | tf_op jit(solution)/shard_map/dynamic_slice | solution.py:213
  154.1 1.1 collective-permute-start.8
  155.2 0.3 collective-permute-start.7
  156.1 0.4 stack_reshape.12
  156.6 16.9 %collective-permute-done.8 = f32[4,48,1024]{2,1,0:T(8,128)} collective-permute-done((f32[4,48,1024]{2,1,0:T(8,128)}, f32[4,48,1024]{2,1,0:T(8,128)}, u32[]{:S(2)}, u32[]{:S(2)}) %collective-permute-start.8) | collective-permute-done | bytes 786464 | tf_op jit(solution)/shard_map/ppermute | solution.py:215
  173.5 2.7 %stack_reshape.15 = f32[1,192,16,64]{3,2,1,0:T(8,128)} reshape(f32[4,48,1024]{2,1,0:T(8,128)} %collective-permute-done.8) | data formatting | bytes 1572864 | tf_op jit(solution)/shard_map/stack;reshape | solution.py:43
  176.1 14.7 %collective-permute-done.7 = f32[4,48,1024]{2,1,0:T(8,128)} collective-permute-done((f32[4,48,1024]{2,1,0:T(8,128)}, f32[4,48,1024]{2,1,0:T(8,128)}, u32[]{:S(2)}, u32[]{:S(2)}) %collective-permute-start.7) | collective-permute-done | bytes 786464 | tf_op jit(solution)/shard_map/ppermute | solution.py:215
  190.9 2.6 %stack_reshape.14 = f32[1,192,16,64]{3,2,1,0:T(8,128)} reshape(f32[4,48,1024]{2,1,0:T(8,128)} %collective-permute-done.7) | data formatting | bytes 1572864 | tf_op jit(solution)/shard_map/stack;reshape | solution.py:43
  193.5 1.6 stack_reshape.13
  195.1 7.5 %fusion.19 = f32[192,64,128]{2,1,0:T(8,128)S(1)} fusion(f32[1,192,16,64]{3,2,0,1:T(8,128)} %bitcast.72, f32[1,192,16,64]{3,2,0,1:T(8,128)} %bitcast.73, f32[1,192,16,64]{3,2,0,1:T(8,128)} %bitcast.74, f32[1,192,16,64]{3,2,0,1:T(8,128)S(1)} %bitcast.71, f32[1,16,128]{2,1,0:T(8,128)S(1)} %get-tuple-element.33, f32[1,16,128]{2,1,0:T(8,128)S(1)} %get-tuple-element.32, ...), kind=kOutput, calls=%fused_computation.33 | convolution fusion | flops 606363648 | bytes 9469952 | tf_op jit(solution)/shard_map/prab,pac->rbc/dot_general | solution.py:47
  202.6 3.3 %multiply_add_fusion = (f32[192,64,64]{2,1,0:T(8,128)S(1)}, f32[192,64,64]{2,1,0:T(8,128)S(1)}) fusion(f32[192,64,128]{2,1,0:T(8,128)S(1)} %fusion.19, f32[64,64]{1,0:T(8,128)S(1)} %get-tuple-element.45, f32[64,64]{1,0:T(8,128)S(1)} %get-tuple-element.46), kind=kLoop, calls=%fused_computation.16 | loop fusion | flops 4718592 | bytes 12615680 | tf_op jit(solution)/shard_map/add | solution.py:59
  205.9 2.7 %fusion.27 = f32[192,20,128]{2,1,0:T(8,128)S(1)} fusion(f32[192,64,64]{2,1,0:T(8,128)S(1)} %get-tuple-element.13, f32[192,64,64]{2,1,0:T(8,128)S(1)} %get-tuple-element.12), kind=kOutput, calls=%fused_computation.41 | convolution fusion | flops 190334464 | bytes 8257536 | tf_op jit(solution)/shard_map/rbc,bq->rqc/dot_general | solution.py:66
  208.6 2.7 %fusion.26 = f32[192,20,128]{2,1,0:T(8,128)S(1)} fusion(f32[192,64,64]{2,1,0:T(8,128)S(1)} %get-tuple-element.13, f32[192,64,64]{2,1,0:T(8,128)S(1)} %get-tuple-element.12), kind=kOutput, calls=%fused_computation.40 | convolution fusion | flops 190334464 | bytes 8257536 | tf_op jit(solution)/shard_map/rbc,bq->rqc/dot_general | solution.py:65
  211.3 2.7 %fusion.22 = (f32[192,20,64]{2,1,0:T(8,128)}, f32[192,20,64]{2,1,0:T(8,128)S(1)}) fusion(f32[192,20,128]{2,1,0:T(8,128)S(1)} %fusion.27, f32[192,20,128]{2,1,0:T(8,128)S(1)} %fusion.26), kind=kLoop, calls=%fused_computation.35 | loop fusion | flops 983040 | bytes 5898240 | tf_op jit(solution)/shard_map/mul | solution.py:69
  214.0 2.0 reshape.171
  216.0 1.6 copy.43
  217.6 0.5 reshape.170
  218.1 1.6 copy.42
  (30 shorter events, 1.7 us)
Async XLA Ops:
  9.1 9.8 %copy-start.6 = (f32[6,5,32]{2,0,1:T(8,128)S(1)}, f32[6,5,32]{2,0,1:T(8,128)}, u32[]{:S(2)}) copy-start(f32[6,5,32]{2,0,1:T(8,128)} %param.7) | copy-start | bytes 11524
  9.1 9.9 %copy-start = (f32[6,32,4,1024]{3,2,1,0:T(4,128)S(1)}, f32[6,32,4,1024]{3,2,1,0:T(4,128)}, u32[]{:S(2)}) copy-start(f32[6,32,4,1024]{3,2,1,0:T(4,128)} %param.4) | copy-start | bytes 9437188
  9.1 56.5 %collective-permute-start = (f32[6,32,3,1024]{3,1,2,0:T(8,128)}, f32[6,32,3,1024]{3,1,2,0:T(8,128)}, u32[]{:S(2)}, u32[]{:S(2)}) collective-permute-start(f32[6,32,3,1024]{3,1,2,0:T(8,128)} %copy.45), channel_id=1, source_target_pairs={{0,4},{4,8},{8,12},{12,16},{16,20},{20,24},{24,28},{1,5},{5,9},{9,... | collective-permute-start | bytes 7077896 | tf_op jit(solution)/shard_map/ppermute | solution.py:26
  15.6 100.4 %collective-permute-start.1 = (f32[6,32,3,1024]{3,1,2,0:T(8,128)}, f32[6,32,3,1024]{3,1,2,0:T(8,128)}, u32[]{:S(2)}, u32[]{:S(2)}) collective-permute-start(f32[6,32,3,1024]{3,1,2,0:T(8,128)} %copy.46), channel_id=1, source_target_pairs={{4,0},{8,4},{12,8},{16,12},{20,16},{24,20},{28,24},{5,1},{9,5},{13... | collective-permute-start | bytes 7077896 | tf_op jit(solution)/shard_map/ppermute | solution.py:29
  19.0 4.7 %copy-start.3 = (f32[6,32]{1,0:T(8,128)}, f32[6,32]{1,0:T(8,128)S(1)}, u32[]{:S(2)}) copy-start(f32[6,32]{1,0:T(8,128)S(1)} %get-tuple-element.40) | copy-start | bytes 2308
  21.8 3.4 %copy-start.2 = (f32[16,4,1024]{2,1,0:T(4,128)S(1)}, f32[16,4,1024]{2,1,0:T(4,128)}, u32[]{:S(2)}) copy-start(f32[16,4,1024]{2,1,0:T(4,128)} %param.5) | copy-start | bytes 786436
  21.8 4.3 %copy-start.5 = (s32[2,4,1024]{2,1,0:T(4,128)S(1)}, s32[2,4,1024]{2,1,0:T(4,128)}, u32[]{:S(2)}) copy-start(s32[2,4,1024]{2,1,0:T(4,128)} %param.6) | copy-start | bytes 98308
  24.6 9.7 %collective-permute-start.3 = (f32[4,192,16]{2,1,0:T(8,128)}, f32[4,192,16]{2,1,0:T(8,128)}, u32[]{:S(2)}, u32[]{:S(2)}) collective-permute-start(f32[4,192,16]{2,1,0:T(8,128)} %get-tuple-element.26), channel_id=1, source_target_pairs={{1,0},{2,1},{3,2},{0,3},{5,4},{6,5},{7,6},{4,7},{9,8},{10,9},{11,1... | collective-permute-start | bytes 147464 | tf_op jit(solution)/shard_map/ppermute | solution.py:29
  25.0 11.4 %collective-permute-start.2 = (f32[4,192,16]{2,1,0:T(8,128)}, f32[4,192,16]{2,1,0:T(8,128)}, u32[]{:S(2)}, u32[]{:S(2)}) collective-permute-start(f32[4,192,16]{2,1,0:T(8,128)} %get-tuple-element.27), channel_id=1, source_target_pairs={{0,1},{1,2},{2,3},{3,0},{4,5},{5,6},{6,7},{7,4},{8,9},{9,10},{10,1... | collective-permute-start | bytes 147464 | tf_op jit(solution)/shard_map/ppermute | solution.py:26
  53.6 65.2 %copy-start.4 = (f32[6,32]{1,0:T(8,128)S(1)}, f32[6,32]{1,0:T(8,128)}, u32[]{:S(2)}) copy-start(f32[6,32]{1,0:T(8,128)} %copy-done.3) | copy-start | bytes 2308
  122.1 2.1 copy-start.1
  124.6 4.1 %collective-permute-start.5 = (f32[6,192,16]{1,2,0:T(8,128)S(1)}, f32[6,192,16]{1,2,0:T(8,128)S(1)}, u32[]{:S(2)}, u32[]{:S(2)}) collective-permute-start(f32[6,192,16]{1,2,0:T(8,128)S(1)} %copy.35), channel_id=1, source_target_pairs={{1,0},{2,1},{3,2},{0,3},{5,4},{6,5},{7,6},{4,7},{9,8},{10,9},{11,1... | collective-permute-start | bytes 221192 | tf_op jit(solution)/shard_map/ppermute | solution.py:29
  126.0 4.1 %collective-permute-start.4 = (f32[6,192,16]{1,2,0:T(8,128)S(1)}, f32[6,192,16]{1,2,0:T(8,128)S(1)}, u32[]{:S(2)}, u32[]{:S(2)}) collective-permute-start(f32[6,192,16]{1,2,0:T(8,128)S(1)} %copy.34), channel_id=1, source_target_pairs={{0,1},{1,2},{2,3},{3,0},{4,5},{5,6},{6,7},{7,4},{8,9},{9,10},{10,1... | collective-permute-start | bytes 221192 | tf_op jit(solution)/shard_map/ppermute | solution.py:26
  154.1 19.3 %collective-permute-start.8 = (f32[4,48,1024]{2,1,0:T(8,128)}, f32[4,48,1024]{2,1,0:T(8,128)}, u32[]{:S(2)}, u32[]{:S(2)}) collective-permute-start(f32[4,48,1024]{2,1,0:T(8,128)} %get-tuple-element.23), channel_id=1, source_target_pairs={{0,3},{1,0},{2,1},{3,2},{4,7},{5,4},{6,5},{7,6},{8,11},{9,8},{10,9... | collective-permute-start | bytes 2359304 | tf_op jit(solution)/shard_map/ppermute | solution.py:215
  155.2 35.6 %collective-permute-start.7 = (f32[4,48,1024]{2,1,0:T(8,128)}, f32[4,48,1024]{2,1,0:T(8,128)}, u32[]{:S(2)}, u32[]{:S(2)}) collective-permute-start(f32[4,48,1024]{2,1,0:T(8,128)} %get-tuple-element.24), channel_id=1, source_target_pairs={{0,2},{1,3},{2,0},{3,1},{4,6},{5,7},{6,4},{7,5},{8,10},{9,11},{10,... | collective-permute-start | bytes 2359304 | tf_op jit(solution)/shard_map/ppermute | solution.py:215
  155.5 38.0 %collective-permute-start.6 = (f32[4,48,1024]{2,1,0:T(8,128)}, f32[4,48,1024]{2,1,0:T(8,128)S(1)}, u32[]{:S(2)}, u32[]{:S(2)}) collective-permute-start(f32[4,48,1024]{2,1,0:T(8,128)} %get-tuple-element.25), channel_id=1, source_target_pairs={{0,1},{1,2},{2,3},{3,0},{4,5},{5,6},{6,7},{7,4},{8,9},{9,10},{10,1... | collective-permute-start | bytes 2359304 | tf_op jit(solution)/shard_map/ppermute | solution.py:215

commit v9 on v8

--- a/solution.py
+++ b/solution.py
@@ -70,11 +70,11 @@
     return (real_part.reshape(n_rows, n_items, NK), imag_part.reshape(n_rows, n_items, NK))
 
 
-def interp_kernel(local, lat_rows, *refs):
+def interp_kernel(local, lat_rows, parts, *refs):
     if local:
         hi_ref, lo_ref, info_ref, out_ref = refs
     else:
-        hi_ref, lo_ref, info_ref, base_ref, out_ref = refs
+        me_ref, hi_ref, lo_ref, info_ref, base_ref, out_ref = refs
     block = pl.program_id(0)
     start = pl.multiple_of(block * LANES, LANES)
     c_index = lax.broadcasted_iota(jnp.int32, (WINDOW, LANES), 0).astype(jnp.float32)
@@ -121,7 +121,13 @@
                 preferred_element_type=jnp.float32,
             )
             acc = acc + both[:rows_hi, :LANES] + both[:rows_hi, LANES:] + both[rows_hi:, :LANES]
-        out_ref[row] = acc
+        if local:
+            out_ref[row] = acc
+        else:
+            chunk = acc.shape[0] // parts
+            for c in range(parts):
+                slot = lax.rem(c - me_ref[0] + parts, parts)
+                out_ref[slot, row] = acc[c * chunk : (c + 1) * chunk]
 
 
 def interpolate(x_hi, x_lo, info, lat_rows, lon_cols, base=None):
@@ -131,15 +137,23 @@
     tile = pl.BlockSpec((lat_rows, n_items, LANES), lambda jb: (0, 0, jb))
     specs = [whole, whole, pl.BlockSpec((lat_rows, info.shape[1], LANES), lambda jb: (0, 0, jb))]
     operands = [x_hi, x_lo, info]
+    parts = 1
+    out_shape = jax.ShapeDtypeStruct((lat_rows, n_items, lon_cols), jnp.float32)
+    out_spec = tile
     if base is not None:
-        specs.append(tile)
-        operands.append(base)
+        parts = lax.axis_size("lon")
+        me = jnp.reshape(lax.axis_index("lon"), (1,)).astype(jnp.int32)
+        specs = [pl.BlockSpec(memory_space=pltpu.SMEM)] + specs + [tile]
+        operands = [me] + operands + [base]
+        chunk = n_items // parts
+        out_shape = jax.ShapeDtypeStruct((parts, lat_rows, chunk, lon_cols), jnp.float32)
+        out_spec = pl.BlockSpec((parts, lat_rows, chunk, LANES), lambda jb: (0, 0, 0, jb))
     return pl.pallas_call(
-        functools.partial(interp_kernel, base is None, lat_rows),
-        out_shape=jax.ShapeDtypeStruct((lat_rows, n_items, lon_cols), jnp.float32),
+        functools.partial(interp_kernel, base is None, lat_rows, parts),
+        out_shape=out_shape,
         grid=(blocks,),
         in_specs=specs,
-        out_specs=tile,
+        out_specs=out_spec,
         compiler_params=pltpu.CompilerParams(vmem_limit_bytes=48 * 1024 * 1024),
     )(*operands)
 
@@ -209,8 +223,7 @@
     pieces = []
     owners = []
     for shift in range(parts):
-        target = lax.rem(me + shift, parts)
-        piece = lax.dynamic_slice_in_dim(departed, target * chunk, chunk, axis=1)
+        piece = departed[shift]
         if shift:
             piece = lax.ppermute(piece, "lon", [(i, (i + shift) % parts) for i in range(parts)])
         pieces.append(piece)

time: 221 us -> 222 us (level)
    dynamic_slice x1 -> x0, local copies, waits for them, and re-layouts: 3.33 us -> none  [on_device(): piece = lax.dynamic_slice_in_dim(departed, target * chunk, chunk, axis=1)]
    slice x0 -> x1, local copies, waits for them, and re-layouts: none -> 3.3 us  [on_device(): piece = departed[shift]]
where the time goes in v9:
time: 222 us; the launch traced here: 221 us
  waiting for transfers between devices  107 us (48%)
  local copies, waits for them, and re-layouts  47.3 us (21%)
  other arithmetic  22.1 us (10%)
  Pallas kernels  20.2 us (9%)
  matrix products  12.9 us (6%)
  starting transfers between devices  10.3 us (5%)
    ppermute x3, waiting for transfers between devices, shifted(): lax.ppermute(lax.slice_in_dim(block, 0, width, axis=dim), axis, backward)  60.2 us
    ppermute x3, waiting for transfers between devices, on_device(): lax.ppermute(piece, 'lon', [(i, (i + shift) % parts) for i in range(parts)])  31.7 us
    pallas_call x2, Pallas kernels, interpolate(): pl.pallas_call(functools.partial(interp_kernel, base is None, lat_rows, p...  20.2 us
    ppermute x3, waiting for transfers between devices, shifted(): lax.ppermute(lax.slice_in_dim(block, block.shape[dim] - width, None, axis...  15.2 us
    unnamed x19, local copies, waits for them, and re-layouts  11.8 us
    concatenate x2, local copies, waits for them, and re-layouts, widen(): return jnp.concatenate([left, block, right], axis=block.ndim - 1)  11.3 us
    another operation x4, local copies, waits for them, and re-layouts, spectrum(): jnp.stack([piece.reshape(n_rows * n_items, per_piece, RADIX) for piece in...  8.44 us
    dot_general x1, matrix products, spectrum(): jnp.einsum('prab,pac->rbc', folded, table, precision=highest)  7.48 us
  transfers between devices with their start and end apart: 9, of which 8 were waited for; matrix products, arithmetic and copies ran while one was open for 11% of the time, Pallas kernels for 5%

profile of v9, /device:TPU:24, one launch (start us, length us, event | category | flops | bytes accessed | tf_op | source)
XLA Modules:
  0.0 220.8 jit_solution(12133643795641876172)
XLA Ops:
  0.6 5.7 %fusion.89 = (f32[6,32,3,1024]{3,2,1,0:T(4,128)S(1)}, f32[6,32,3,1024]{3,2,1,0:T(4,128)S(1)}) fusion(f32[6,32,4,1024]{3,2,1,0:T(4,128)} %param.4), kind=kLoop, calls=%fused_computation.137 | loop fusion | bytes 9437184 | tf_op jit(solution)/shard_map/slice | solution.py:29
  6.3 2.8 %copy.46 = f32[6,32,3,1024]{3,1,2,0:T(8,128)} copy(f32[6,32,3,1024]{3,2,1,0:T(4,128)S(1)} %get-tuple-element.29) | data formatting | bytes 4718592
  9.1 3.7 %collective-permute-start = (f32[6,32,3,1024]{3,1,2,0:T(8,128)}, f32[6,32,3,1024]{3,1,2,0:T(8,128)}, u32[]{:S(2)}, u32[]{:S(2)}) collective-permute-start(f32[6,32,3,1024]{3,1,2,0:T(8,128)} %copy.46), channel_id=1, source_target_pairs={{0,4},{4,8},{8,12},{12,16},{16,20},{20,24},{24,28},{1,5},{5,9},{9,... | collective-permute-start | bytes 7077896 | tf_op jit(solution)/shard_map/ppermute | solution.py:26
  12.8 2.8 %copy.47 = f32[6,32,3,1024]{3,1,2,0:T(8,128)} copy(f32[6,32,3,1024]{3,2,1,0:T(4,128)S(1)} %get-tuple-element.28) | data formatting | bytes 4718592
  15.6 3.3 %collective-permute-start.1 = (f32[6,32,3,1024]{3,1,2,0:T(8,128)}, f32[6,32,3,1024]{3,1,2,0:T(8,128)}, u32[]{:S(2)}, u32[]{:S(2)}) collective-permute-start(f32[6,32,3,1024]{3,1,2,0:T(8,128)} %copy.47), channel_id=1, source_target_pairs={{4,0},{8,4},{12,8},{16,12},{20,16},{24,20},{28,24},{5,1},{9,5},{13... | collective-permute-start | bytes 7077896 | tf_op jit(solution)/shard_map/ppermute | solution.py:29
  19.0 2.8 %multiply_add_fusion.1 = f32[4,6,32,1024]{3,0,2,1:T(4,128)S(1)} fusion(f32[4,6,32,1024]{3,0,2,1:T(4,128)S(1)} %bitcast.73, f32[6,32]{1,0:T(8,128)S(1)} %get-tuple-element.39, f32[6,32]{1,0:T(8,128)S(1)} %get-tuple-element.40, f32[6,32]{1,0:T(8,128)S(1)} %get-tuple-element.37, f32[6,32]{1,0:T(8,128)S(1)} %get-tuple-element.38, f32[6,32]{1,0:T(8,128)S(1)} %get-tuple-element.36), kind=kLoop, calls=%fused_computation.30 | loop fusion | flops 7077888 | bytes 6295296 | tf_op jit(solution)/shard_map/add | solution.py:169
  21.8 1.8 copy.30
  23.7 1.0 fusion.88
  24.7 0.4 collective-permute-start.3
  25.2 0.9 copy.65
  26.2 1.1 maximum_maximum_fusion.refs_2_.refs_3_
  27.3 7.1 %collective-permute-done.3 = f32[4,192,16]{2,1,0:T(8,128)} collective-permute-done((f32[4,192,16]{2,1,0:T(8,128)}, f32[4,192,16]{2,1,0:T(8,128)}, u32[]{:S(2)}, u32[]{:S(2)}) %collective-permute-start.3) | collective-permute-done | bytes 49184 | tf_op jit(solution)/shard_map/ppermute | solution.py:29
  34.4 2.1 collective-permute-done.2
  36.4 4.4 %concatenate.18 = f32[4,192,1056]{2,1,0:T(8,128)} concatenate(f32[4,192,16]{2,1,0:T(8,128)} %collective-permute-done.2, f32[4,192,1024]{2,1,0:T(8,128)S(1)} %bitcast.77, f32[4,192,16]{2,1,0:T(8,128)} %collective-permute-done.3), dimensions={2} | concatenate | bytes 6488064 | tf_op jit(solution)/shard_map/concatenate | solution.py:177
  40.8 2.6 %fusion.17 = (bf16[4,192,1152]{2,1,0:T(8,128)(2,1)S(1)}, bf16[4,192,1152]{2,1,0:T(8,128)(2,1)S(1)}) fusion(f32[4,192,1056]{2,1,0:T(8,128)} %concatenate.18), kind=kLoop, calls=%fused_computation.29 | loop fusion | flops 3538944 | bytes 6782976 | tf_op jit(solution)/shard_map/convert_element_type | solution.py:184
  43.4 10.1 %shard_map.59.refs_4_ = f32[4,192,1024]{2,1,0:T(8,128)} custom-call(bf16[4,192,1152]{2,1,0:T(8,128)(2,1)S(1)} %get-tuple-element.21.refs_0_, bf16[4,192,1152]{2,1,0:T(8,128)(2,1)S(1)} %get-tuple-element.20.refs_1_, f32[4,24,1024]{2,1,0:T(8,128)S(1)} %maximum_maximum_fusion.refs_2_.refs_3_), custom_call_target="tpu_custom_call" | custom-call | tf_op jit(solution)/shard_map/pallas_call | solution.py:151
  53.5 12.1 %collective-permute-done = f32[6,32,3,1024]{3,1,2,0:T(8,128)} collective-permute-done((f32[6,32,3,1024]{3,1,2,0:T(8,128)}, f32[6,32,3,1024]{3,1,2,0:T(8,128)}, u32[]{:S(2)}, u32[]{:S(2)}) %collective-permute-start) | collective-permute-done | bytes 2359328 | tf_op jit(solution)/shard_map/ppermute | solution.py:26
  65.6 50.5 %collective-permute-done.1 = f32[6,32,3,1024]{3,1,2,0:T(8,128)} collective-permute-done((f32[6,32,3,1024]{3,1,2,0:T(8,128)}, f32[6,32,3,1024]{3,1,2,0:T(8,128)}, u32[]{:S(2)}, u32[]{:S(2)}) %collective-permute-start.1) | collective-permute-done | bytes 2359328 | tf_op jit(solution)/shard_map/ppermute | solution.py:29
  116.0 2.8 %maximum_bitcast_fusion = f32[6,6,32,1024]{3,2,0,1:T(8,128)S(1)} fusion(f32[6,32,3,1024]{3,1,2,0:T(8,128)} %collective-permute-done.1, f32[6,32,3,1024]{3,1,2,0:T(8,128)} %collective-permute-done), kind=kLoop, calls=%fused_computation.28 | loop fusion | flops 1179648 | bytes 9437184 | tf_op jit(solution)/shard_map/transpose | solution.py:216
  118.8 2.9 %fusion.13 = f32[6,6,32,1024]{3,2,0,1:T(8,128)S(1)} fusion(f32[6,6,32,1024]{3,2,0,1:T(8,128)S(1)} %maximum_bitcast_fusion, f32[6,32]{1,0:T(8,128)S(1)} %get-tuple-element.39, f32[6,32]{1,0:T(8,128)S(1)} %copy-done.4, f32[6,32]{1,0:T(8,128)S(1)} %get-tuple-element.37, f32[6,32]{1,0:T(8,128)S(1)} %get-tuple-element.38, f32[6,32]{1,0:T(8,128)S(1)} %get-tuple-element.36), kind=kLoop, calls=%fused_computation.24 | loop fusion | flops 10616832 | bytes 9441024 | tf_op jit(solution)/shard_map/add | solution.py:169
  121.7 0.4 copy.34
  122.1 2.1 copy-done.1
  124.4 0.2 copy.36
  124.7 1.1 collective-permute-start.5
  125.8 0.2 copy.35
  126.1 2.7 %collective-permute-done.5 = f32[6,192,16]{1,2,0:T(8,128)S(1)} collective-permute-done((f32[6,192,16]{1,2,0:T(8,128)S(1)}, f32[6,192,16]{1,2,0:T(8,128)S(1)}, u32[]{:S(2)}, u32[]{:S(2)}) %collective-permute-start.5) | collective-permute-done | bytes 73760 | tf_op jit(solution)/shard_map/ppermute | solution.py:29
  129.0 1.1 collective-permute-done.4
  130.3 6.9 %concatenate.21 = f32[6,192,1056]{2,1,0:T(8,128)} concatenate(f32[6,192,16]{2,1,0:T(8,128)S(1)} %copy.37, f32[6,192,1024]{2,1,0:T(8,128)} %bitcast.75, f32[6,192,16]{2,1,0:T(8,128)S(1)} %copy.38), dimensions={2} | concatenate | bytes 9732096 | tf_op jit(solution)/shard_map/concatenate | solution.py:177
  137.2 3.6 %fusion.8 = (bf16[6,192,1152]{2,1,0:T(8,128)(2,1)S(1)}, bf16[6,192,1152]{2,1,0:T(8,128)(2,1)S(1)}) fusion(f32[6,192,1056]{2,1,0:T(8,128)} %concatenate.21), kind=kLoop, calls=%fused_computation.17 | loop fusion | flops 5308416 | bytes 10174464 | tf_op jit(solution)/shard_map/convert_element_type | solution.py:184
  140.8 10.1 %shard_map.60 = f32[4,4,48,1024]{3,2,1,0:T(8,128)} custom-call(s32[1]{0:T(128)} %bitcast.1.refs_0_, bf16[6,192,1152]{2,1,0:T(8,128)(2,1)S(1)} %get-tuple-element.15.refs_1_, bf16[6,192,1152]{2,1,0:T(8,128)(2,1)S(1)} %get-tuple-element.14.refs_2_, f32[4,24,1024]{2,1,0:T(8,128)S(1)} %maximum_maximum_fusion.refs_2_.refs_3_, f32[4,192,1024]{2,1,0:T(8,128)} %shard_map.59.refs_4_), custom_call_target="tpu_custom_call" | custom-call | tf_op jit(solution)/shard_map/pallas_call | solution.py:151
  150.9 3.3 %fusion.87 = (f32[1,4,48,1024]{3,2,1,0:T(8,128)S(1)}, f32[4,48,1024]{2,1,0:T(8,128)}, f32[4,48,1024]{2,1,0:T(8,128)}, f32[4,48,1024]{2,1,0:T(8,128)S(1)}) fusion(f32[4,4,48,1024]{3,2,1,0:T(8,128)} %shard_map.60), kind=kLoop, calls=%fused_computation.135 | loop fusion | bytes 6291456 | tf_op jit(solution)/shard_map/slice | solution.py:226
  154.2 1.1 collective-permute-start.8
  155.3 0.3 collective-permute-start.7
  156.2 0.4 stack_reshape_squeeze.3
  156.6 16.9 %collective-permute-done.8 = f32[4,48,1024]{2,1,0:T(8,128)} collective-permute-done((f32[4,48,1024]{2,1,0:T(8,128)}, f32[4,48,1024]{2,1,0:T(8,128)}, u32[]{:S(2)}, u32[]{:S(2)}) %collective-permute-start.8) | collective-permute-done | bytes 786464 | tf_op jit(solution)/shard_map/ppermute | solution.py:228
  173.5 2.7 %stack_reshape.11 = f32[1,192,16,64]{3,2,1,0:T(8,128)} reshape(f32[4,48,1024]{2,1,0:T(8,128)} %collective-permute-done.8) | data formatting | bytes 1572864 | tf_op jit(solution)/shard_map/stack;reshape | solution.py:43
  176.2 14.7 %collective-permute-done.7 = f32[4,48,1024]{2,1,0:T(8,128)} collective-permute-done((f32[4,48,1024]{2,1,0:T(8,128)}, f32[4,48,1024]{2,1,0:T(8,128)}, u32[]{:S(2)}, u32[]{:S(2)}) %collective-permute-start.7) | collective-permute-done | bytes 786464 | tf_op jit(solution)/shard_map/ppermute | solution.py:228
  190.9 2.7 %stack_reshape.10 = f32[1,192,16,64]{3,2,1,0:T(8,128)} reshape(f32[4,48,1024]{2,1,0:T(8,128)} %collective-permute-done.7) | data formatting | bytes 1572864 | tf_op jit(solution)/shard_map/stack;reshape | solution.py:43
  193.6 2.7 %stack_reshape.9 = f32[1,192,16,64]{3,2,1,0:T(8,128)} reshape(f32[4,48,1024]{2,1,0:T(8,128)} %collective-permute-done.6) | data formatting | bytes 1572864 | tf_op jit(solution)/shard_map/stack;reshape | solution.py:43
  196.3 7.5 %fusion.19 = f32[192,64,128]{2,1,0:T(8,128)S(1)} fusion(f32[1,192,16,64]{3,2,0,1:T(8,128)} %bitcast.81, f32[1,192,16,64]{3,2,0,1:T(8,128)} %bitcast.82, f32[1,192,16,64]{3,2,0,1:T(8,128)} %bitcast.83, f32[1,192,16,64]{3,2,0,1:T(8,128)S(1)} %bitcast.80, f32[1,16,128]{2,1,0:T(8,128)S(1)} %get-tuple-element.33, f32[1,16,128]{2,1,0:T(8,128)S(1)} %get-tuple-element.32, ...), kind=kOutput, calls=%fused_computation.33 | convolution fusion | flops 606363648 | bytes 9469952 | tf_op jit(solution)/shard_map/prab,pac->rbc/dot_general | solution.py:47
  203.8 3.3 %multiply_add_fusion = (f32[192,64,64]{2,1,0:T(8,128)S(1)}, f32[192,64,64]{2,1,0:T(8,128)S(1)}) fusion(f32[192,64,128]{2,1,0:T(8,128)S(1)} %fusion.19, f32[64,64]{1,0:T(8,128)S(1)} %get-tuple-element.45, f32[64,64]{1,0:T(8,128)S(1)} %get-tuple-element.46), kind=kLoop, calls=%fused_computation.16 | loop fusion | flops 4718592 | bytes 12615680 | tf_op jit(solution)/shard_map/add | solution.py:59
  207.1 2.7 %fusion.27 = f32[192,20,128]{2,1,0:T(8,128)S(1)} fusion(f32[192,64,64]{2,1,0:T(8,128)S(1)} %get-tuple-element.13, f32[192,64,64]{2,1,0:T(8,128)S(1)} %get-tuple-element.12), kind=kOutput, calls=%fused_computation.41 | convolution fusion | flops 190334464 | bytes 8257536 | tf_op jit(solution)/shard_map/rbc,bq->rqc/dot_general | solution.py:66
  209.8 2.7 %fusion.26 = f32[192,20,128]{2,1,0:T(8,128)S(1)} fusion(f32[192,64,64]{2,1,0:T(8,128)S(1)} %get-tuple-element.13, f32[192,64,64]{2,1,0:T(8,128)S(1)} %get-tuple-element.12), kind=kOutput, calls=%fused_computation.40 | convolution fusion | flops 190334464 | bytes 8257536 | tf_op jit(solution)/shard_map/rbc,bq->rqc/dot_general | solution.py:65
  212.5 2.7 %fusion.22 = (f32[192,20,64]{2,1,0:T(8,128)}, f32[192,20,64]{2,1,0:T(8,128)S(1)}) fusion(f32[192,20,128]{2,1,0:T(8,128)S(1)} %fusion.27, f32[192,20,128]{2,1,0:T(8,128)S(1)} %fusion.26), kind=kLoop, calls=%fused_computation.35 | loop fusion | flops 983040 | bytes 5898240 | tf_op jit(solution)/shard_map/mul | solution.py:69
  215.2 2.0 reshape.175
  217.2 1.6 copy.44
  218.8 0.5 reshape.174
  219.3 1.6 copy.43
  (30 shorter events, 1.7 us)
Async XLA Ops:
  9.1 9.8 %copy-start.6 = (f32[6,5,32]{2,0,1:T(8,128)S(1)}, f32[6,5,32]{2,0,1:T(8,128)}, u32[]{:S(2)}) copy-start(f32[6,5,32]{2,0,1:T(8,128)} %param.7) | copy-start | bytes 11524
  9.1 9.9 %copy-start = (f32[6,32,4,1024]{3,2,1,0:T(4,128)S(1)}, f32[6,32,4,1024]{3,2,1,0:T(4,128)}, u32[]{:S(2)}) copy-start(f32[6,32,4,1024]{3,2,1,0:T(4,128)} %param.4) | copy-start | bytes 9437188
  9.1 56.5 %collective-permute-start = (f32[6,32,3,1024]{3,1,2,0:T(8,128)}, f32[6,32,3,1024]{3,1,2,0:T(8,128)}, u32[]{:S(2)}, u32[]{:S(2)}) collective-permute-start(f32[6,32,3,1024]{3,1,2,0:T(8,128)} %copy.46), channel_id=1, source_target_pairs={{0,4},{4,8},{8,12},{12,16},{16,20},{20,24},{24,28},{1,5},{5,9},{9,... | collective-permute-start | bytes 7077896 | tf_op jit(solution)/shard_map/ppermute | solution.py:26
  15.6 100.4 %collective-permute-start.1 = (f32[6,32,3,1024]{3,1,2,0:T(8,128)}, f32[6,32,3,1024]{3,1,2,0:T(8,128)}, u32[]{:S(2)}, u32[]{:S(2)}) collective-permute-start(f32[6,32,3,1024]{3,1,2,0:T(8,128)} %copy.47), channel_id=1, source_target_pairs={{4,0},{8,4},{12,8},{16,12},{20,16},{24,20},{28,24},{5,1},{9,5},{13... | collective-permute-start | bytes 7077896 | tf_op jit(solution)/shard_map/ppermute | solution.py:29
  19.0 4.7 %copy-start.3 = (f32[6,32]{1,0:T(8,128)}, f32[6,32]{1,0:T(8,128)S(1)}, u32[]{:S(2)}) copy-start(f32[6,32]{1,0:T(8,128)S(1)} %get-tuple-element.40) | copy-start | bytes 2308
  21.8 3.4 %copy-start.2 = (f32[16,4,1024]{2,1,0:T(4,128)S(1)}, f32[16,4,1024]{2,1,0:T(4,128)}, u32[]{:S(2)}) copy-start(f32[16,4,1024]{2,1,0:T(4,128)} %param.5) | copy-start | bytes 786436
  21.8 4.3 %copy-start.5 = (s32[2,4,1024]{2,1,0:T(4,128)S(1)}, s32[2,4,1024]{2,1,0:T(4,128)}, u32[]{:S(2)}) copy-start(s32[2,4,1024]{2,1,0:T(4,128)} %param.6) | copy-start | bytes 98308
  24.7 9.7 %collective-permute-start.3 = (f32[4,192,16]{2,1,0:T(8,128)}, f32[4,192,16]{2,1,0:T(8,128)}, u32[]{:S(2)}, u32[]{:S(2)}) collective-permute-start(f32[4,192,16]{2,1,0:T(8,128)} %get-tuple-element.26), channel_id=1, source_target_pairs={{1,0},{2,1},{3,2},{0,3},{5,4},{6,5},{7,6},{4,7},{9,8},{10,9},{11,1... | collective-permute-start | bytes 147464 | tf_op jit(solution)/shard_map/ppermute | solution.py:29
  25.0 11.4 %collective-permute-start.2 = (f32[4,192,16]{2,1,0:T(8,128)}, f32[4,192,16]{2,1,0:T(8,128)}, u32[]{:S(2)}, u32[]{:S(2)}) collective-permute-start(f32[4,192,16]{2,1,0:T(8,128)} %get-tuple-element.27), channel_id=1, source_target_pairs={{0,1},{1,2},{2,3},{3,0},{4,5},{5,6},{6,7},{7,4},{8,9},{9,10},{10,1... | collective-permute-start | bytes 147464 | tf_op jit(solution)/shard_map/ppermute | solution.py:26
  53.5 65.3 %copy-start.4 = (f32[6,32]{1,0:T(8,128)S(1)}, f32[6,32]{1,0:T(8,128)}, u32[]{:S(2)}) copy-start(f32[6,32]{1,0:T(8,128)} %copy-done.3) | copy-start | bytes 2308
  122.1 2.1 copy-start.1
  124.7 4.1 %collective-permute-start.5 = (f32[6,192,16]{1,2,0:T(8,128)S(1)}, f32[6,192,16]{1,2,0:T(8,128)S(1)}, u32[]{:S(2)}, u32[]{:S(2)}) collective-permute-start(f32[6,192,16]{1,2,0:T(8,128)S(1)} %copy.36), channel_id=1, source_target_pairs={{1,0},{2,1},{3,2},{0,3},{5,4},{6,5},{7,6},{4,7},{9,8},{10,9},{11,1... | collective-permute-start | bytes 221192 | tf_op jit(solution)/shard_map/ppermute | solution.py:29
  126.0 4.1 %collective-permute-start.4 = (f32[6,192,16]{1,2,0:T(8,128)S(1)}, f32[6,192,16]{1,2,0:T(8,128)S(1)}, u32[]{:S(2)}, u32[]{:S(2)}) collective-permute-start(f32[6,192,16]{1,2,0:T(8,128)S(1)} %copy.35), channel_id=1, source_target_pairs={{0,1},{1,2},{2,3},{3,0},{4,5},{5,6},{6,7},{7,4},{8,9},{9,10},{10,1... | collective-permute-start | bytes 221192 | tf_op jit(solution)/shard_map/ppermute | solution.py:26
  154.2 19.3 %collective-permute-start.8 = (f32[4,48,1024]{2,1,0:T(8,128)}, f32[4,48,1024]{2,1,0:T(8,128)}, u32[]{:S(2)}, u32[]{:S(2)}) collective-permute-start(f32[4,48,1024]{2,1,0:T(8,128)} %get-tuple-element.23), channel_id=1, source_target_pairs={{0,3},{1,0},{2,1},{3,2},{4,7},{5,4},{6,5},{7,6},{8,11},{9,8},{10,9... | collective-permute-start | bytes 2359304 | tf_op jit(solution)/shard_map/ppermute | solution.py:228
  155.3 35.6 %collective-permute-start.7 = (f32[4,48,1024]{2,1,0:T(8,128)}, f32[4,48,1024]{2,1,0:T(8,128)}, u32[]{:S(2)}, u32[]{:S(2)}) collective-permute-start(f32[4,48,1024]{2,1,0:T(8,128)} %get-tuple-element.24), channel_id=1, source_target_pairs={{0,2},{1,3},{2,0},{3,1},{4,6},{5,7},{6,4},{7,5},{8,10},{9,11},{10,... | collective-permute-start | bytes 2359304 | tf_op jit(solution)/shard_map/ppermute | solution.py:228
  155.6 38.0 %collective-permute-start.6 = (f32[4,48,1024]{2,1,0:T(8,128)S(1)}, f32[4,48,1024]{2,1,0:T(8,128)}, u32[]{:S(2)}, u32[]{:S(2)}) collective-permute-start(f32[4,48,1024]{2,1,0:T(8,128)S(1)} %get-tuple-element.25), channel_id=1, source_target_pairs={{0,1},{1,2},{2,3},{3,0},{4,5},{5,6},{6,7},{7,4},{8,9},{9,10},{10,1... | collective-permute-start | bytes 2359304 | tf_op jit(solution)/shard_map/ppermute | solution.py:228

commit v10 on v8

--- a/solution.py
+++ b/solution.py
@@ -62,8 +62,15 @@
     angle_three = (
         2.0 * math.pi / RADIX * (digits[:, None] * quotients[None, :] % RADIX).astype(jnp.float32)
     )
-    with_cos = jnp.einsum("rbc,bq->rqc", twisted, jnp.cos(angle_three), precision=highest)
-    with_sin = jnp.einsum("rbc,bq->rqc", twisted, jnp.sin(angle_three), precision=highest)
+    modes = NK // RADIX
+    both = jnp.einsum(
+        "rbc,bq->rqc",
+        twisted,
+        jnp.concatenate([jnp.cos(angle_three), jnp.sin(angle_three)], axis=1),
+        precision=highest,
+    )
+    with_cos = both[:, :modes]
+    with_sin = both[:, modes:]
     scale = 1.0 / math.sqrt(line_len)
     real_part = (with_cos[..., :RADIX] + with_sin[..., RADIX:]) * scale
     imag_part = (with_cos[..., RADIX:] - with_sin[..., :RADIX]) * scale

time: 221 us -> 216 us (0.977)
  waiting for transfers between devices: 107 us -> 99.2 us
  starting transfers between devices: 10.3 us -> 13.5 us
    ppermute x3, waiting for transfers between devices: 60.2 us -> 51.3 us  [shifted(): lax.ppermute(lax.slice_in_dim(block, 0, width, axis=dim), axis, backward)]
    ppermute x3, waiting for transfers between devices: 15.2 us -> 21.1 us  [shifted(): lax.ppermute(lax.slice_in_dim(block, block.shape[dim] - width, None, axis...]
    ppermute x3, waiting for transfers between devices: 31.6 us -> 26.8 us  [on_device(): lax.ppermute(piece, 'lon', [(i, (i + shift) % parts) for i in range(parts)])]
    dot_general x2 -> x1, matrix products: 5.42 us -> 3.45 us  [spectrum(): jnp.einsum('rbc,bq->rqc', twisted, jnp.concatenate([jnp.cos(angle_three),...]
where the time goes in v10:
time: 216 us; the launch traced here: 213 us
  waiting for transfers between devices  99.2 us (46%)
  local copies, waits for them, and re-layouts  46.3 us (21%)
  other arithmetic  21.9 us (10%)
  Pallas kernels  20.2 us (9%)
  starting transfers between devices  13.5 us (6%)
  matrix products  10.9 us (5%)
    ppermute x3, waiting for transfers between devices, shifted(): lax.ppermute(lax.slice_in_dim(block, 0, width, axis=dim), axis, backward)  51.3 us
    ppermute x3, waiting for transfers between devices, on_device(): lax.ppermute(piece, 'lon', [(i, (i + shift) % parts) for i in range(parts)])  26.8 us
    ppermute x3, waiting for transfers between devices, shifted(): lax.ppermute(lax.slice_in_dim(block, block.shape[dim] - width, None, axis...  21.1 us
    pallas_call x2, Pallas kernels, interpolate(): pl.pallas_call(functools.partial(interp_kernel, base is None, lat_rows),...  20.2 us
    unnamed x19, local copies, waits for them, and re-layouts  11.8 us
    concatenate x2, local copies, waits for them, and re-layouts, widen(): return jnp.concatenate([left, block, right], axis=block.ndim - 1)  11.3 us
    dot_general x1, matrix products, spectrum(): jnp.einsum('prab,pac->rbc', folded, table, precision=highest)  7.48 us
    another operation x4, local copies, waits for them, and re-layouts, spectrum(): jnp.stack([piece.reshape(n_rows * n_items, per_piece, RADIX) for piece in...  7.38 us
  transfers between devices with their start and end apart: 9, of which 8 were waited for; matrix products, arithmetic and copies ran while one was open for 11% of the time, Pallas kernels for 5%

profile of v10, /device:TPU:24, one launch (start us, length us, event | category | flops | bytes accessed | tf_op | source)
XLA Modules:
  0.0 213.0 jit_solution(4334643425382832941)
XLA Ops:
  0.6 5.7 %fusion.80 = (f32[6,32,3,1024]{3,2,1,0:T(4,128)S(1)}, f32[6,32,3,1024]{3,2,1,0:T(4,128)S(1)}) fusion(f32[6,32,4,1024]{3,2,1,0:T(4,128)} %param.4), kind=kLoop, calls=%fused_computation.129 | loop fusion | bytes 9437184 | tf_op jit(solution)/shard_map/slice | solution.py:29
  6.3 2.8 %copy.45 = f32[6,32,3,1024]{3,1,2,0:T(8,128)} copy(f32[6,32,3,1024]{3,2,1,0:T(4,128)S(1)} %get-tuple-element.29) | data formatting | bytes 4718592
  9.1 3.7 %collective-permute-start = (f32[6,32,3,1024]{3,1,2,0:T(8,128)}, f32[6,32,3,1024]{3,1,2,0:T(8,128)}, u32[]{:S(2)}, u32[]{:S(2)}) collective-permute-start(f32[6,32,3,1024]{3,1,2,0:T(8,128)} %copy.45), channel_id=1, source_target_pairs={{0,4},{4,8},{8,12},{12,16},{16,20},{20,24},{24,28},{1,5},{5,9},{9,... | collective-permute-start | bytes 7077896 | tf_op jit(solution)/shard_map/ppermute | solution.py:26
  12.8 2.8 %copy.46 = f32[6,32,3,1024]{3,1,2,0:T(8,128)} copy(f32[6,32,3,1024]{3,2,1,0:T(4,128)S(1)} %get-tuple-element.28) | data formatting | bytes 4718592
  15.6 3.3 %collective-permute-start.1 = (f32[6,32,3,1024]{3,1,2,0:T(8,128)}, f32[6,32,3,1024]{3,1,2,0:T(8,128)}, u32[]{:S(2)}, u32[]{:S(2)}) collective-permute-start(f32[6,32,3,1024]{3,1,2,0:T(8,128)} %copy.46), channel_id=1, source_target_pairs={{4,0},{8,4},{12,8},{16,12},{20,16},{24,20},{28,24},{5,1},{9,5},{13... | collective-permute-start | bytes 7077896 | tf_op jit(solution)/shard_map/ppermute | solution.py:29
  19.0 2.8 %multiply_add_fusion.1 = f32[4,6,32,1024]{3,0,2,1:T(4,128)S(1)} fusion(f32[4,6,32,1024]{3,0,2,1:T(4,128)S(1)} %bitcast.59, f32[6,32]{1,0:T(8,128)S(1)} %get-tuple-element.39, f32[6,32]{1,0:T(8,128)S(1)} %get-tuple-element.40, f32[6,32]{1,0:T(8,128)S(1)} %get-tuple-element.37, f32[6,32]{1,0:T(8,128)S(1)} %get-tuple-element.38, f32[6,32]{1,0:T(8,128)S(1)} %get-tuple-element.36), kind=kLoop, calls=%fused_computation.33 | loop fusion | flops 7077888 | bytes 6295296 | tf_op jit(solution)/shard_map/add | solution.py:162
  21.8 1.8 copy.29
  23.7 1.0 fusion.79
  24.7 1.7 collective-permute-start.3
  26.4 0.9 copy.64
  27.5 1.1 maximum_maximum_fusion.refs_2_
  28.5 6.0 %collective-permute-done.2 = f32[4,192,16]{2,1,0:T(8,128)} collective-permute-done((f32[4,192,16]{2,1,0:T(8,128)}, f32[4,192,16]{2,1,0:T(8,128)}, u32[]{:S(2)}, u32[]{:S(2)}) %collective-permute-start.2) | collective-permute-done | bytes 49184 | tf_op jit(solution)/shard_map/ppermute | solution.py:26
  34.5 0.9 collective-permute-done.3
  35.4 4.4 %concatenate.22 = f32[4,192,1056]{2,1,0:T(8,128)} concatenate(f32[4,192,16]{2,1,0:T(8,128)} %collective-permute-done.2, f32[4,192,1024]{2,1,0:T(8,128)S(1)} %bitcast.63, f32[4,192,16]{2,1,0:T(8,128)} %collective-permute-done.3), dimensions={2} | concatenate | bytes 6488064 | tf_op jit(solution)/shard_map/concatenate | solution.py:170
  39.8 2.6 %fusion.21 = (bf16[4,192,1152]{2,1,0:T(8,128)(2,1)S(1)}, bf16[4,192,1152]{2,1,0:T(8,128)(2,1)S(1)}) fusion(f32[4,192,1056]{2,1,0:T(8,128)} %concatenate.22), kind=kLoop, calls=%fused_computation.32 | loop fusion | flops 3538944 | bytes 6782976 | tf_op jit(solution)/shard_map/convert_element_type | solution.py:177
  42.4 10.1 %shard_map.59.refs_3_ = f32[4,192,1024]{2,1,0:T(8,128)} custom-call(bf16[4,192,1152]{2,1,0:T(8,128)(2,1)S(1)} %get-tuple-element.21.refs_0_, bf16[4,192,1152]{2,1,0:T(8,128)(2,1)S(1)} %get-tuple-element.20.refs_1_, f32[4,24,1024]{2,1,0:T(8,128)S(1)} %maximum_maximum_fusion.refs_2_), custom_call_target="tpu_custom_call" | custom-call | tf_op jit(solution)/shard_map/pallas_call | solution.py:144
  52.5 13.1 %collective-permute-done = f32[6,32,3,1024]{3,1,2,0:T(8,128)} collective-permute-done((f32[6,32,3,1024]{3,1,2,0:T(8,128)}, f32[6,32,3,1024]{3,1,2,0:T(8,128)}, u32[]{:S(2)}, u32[]{:S(2)}) %collective-permute-start) | collective-permute-done | bytes 2359328 | tf_op jit(solution)/shard_map/ppermute | solution.py:26
  65.6 50.5 %collective-permute-done.1 = f32[6,32,3,1024]{3,1,2,0:T(8,128)} collective-permute-done((f32[6,32,3,1024]{3,1,2,0:T(8,128)}, f32[6,32,3,1024]{3,1,2,0:T(8,128)}, u32[]{:S(2)}, u32[]{:S(2)}) %collective-permute-start.1) | collective-permute-done | bytes 2359328 | tf_op jit(solution)/shard_map/ppermute | solution.py:29
  116.0 2.8 %maximum_bitcast_fusion = f32[6,6,32,1024]{3,2,0,1:T(8,128)S(1)} fusion(f32[6,32,3,1024]{3,1,2,0:T(8,128)} %collective-permute-done.1, f32[6,32,3,1024]{3,1,2,0:T(8,128)} %collective-permute-done), kind=kLoop, calls=%fused_computation.31 | loop fusion | flops 1179648 | bytes 9437184 | tf_op jit(solution)/shard_map/transpose | solution.py:209
  118.8 2.9 %fusion.17 = f32[6,6,32,1024]{3,2,0,1:T(8,128)S(1)} fusion(f32[6,6,32,1024]{3,2,0,1:T(8,128)S(1)} %maximum_bitcast_fusion, f32[6,32]{1,0:T(8,128)S(1)} %get-tuple-element.39, f32[6,32]{1,0:T(8,128)S(1)} %copy-done.4, f32[6,32]{1,0:T(8,128)S(1)} %get-tuple-element.37, f32[6,32]{1,0:T(8,128)S(1)} %get-tuple-element.38, f32[6,32]{1,0:T(8,128)S(1)} %get-tuple-element.36), kind=kLoop, calls=%fused_computation.27 | loop fusion | flops 10616832 | bytes 9441024 | tf_op jit(solution)/shard_map/add | solution.py:162
  121.7 0.4 copy.33
  122.1 2.1 copy-done.1
  124.4 0.2 copy.34
  124.7 0.2 copy.35
  124.9 1.8 collective-permute-start.5
  126.7 2.0 collective-permute-done.4
  129.2 6.9 %concatenate.25 = f32[6,192,1056]{2,1,0:T(8,128)} concatenate(f32[6,192,16]{2,1,0:T(8,128)S(1)} %copy.36, f32[6,192,1024]{2,1,0:T(8,128)} %bitcast.61, f32[6,192,16]{2,1,0:T(8,128)S(1)} %copy.37), dimensions={2} | concatenate | bytes 9732096 | tf_op jit(solution)/shard_map/concatenate | solution.py:170
  136.1 3.6 %fusion.12 = (bf16[6,192,1152]{2,1,0:T(8,128)(2,1)S(1)}, bf16[6,192,1152]{2,1,0:T(8,128)(2,1)S(1)}) fusion(f32[6,192,1056]{2,1,0:T(8,128)} %concatenate.25), kind=kLoop, calls=%fused_computation.20 | loop fusion | flops 5308416 | bytes 10174464 | tf_op jit(solution)/shard_map/convert_element_type | solution.py:177
  139.6 10.1 %shard_map.60 = f32[4,192,1024]{2,1,0:T(8,128)} custom-call(bf16[6,192,1152]{2,1,0:T(8,128)(2,1)S(1)} %get-tuple-element.15.refs_0_, bf16[6,192,1152]{2,1,0:T(8,128)(2,1)S(1)} %get-tuple-element.14.refs_1_, f32[4,24,1024]{2,1,0:T(8,128)S(1)} %maximum_maximum_fusion.refs_2_, f32[4,192,1024]{2,1,0:T(8,128)} %shard_map.59.refs_3_), custom_call_target="tpu_custom_call" | custom-call | tf_op jit(solution)/shard_map/pallas_call | solution.py:144
  149.7 3.3 %constant_dynamic-slice_fusion.3 = (f32[4,48,1024]{2,1,0:T(8,128)S(1)}, f32[4,48,1024]{2,1,0:T(8,128)}, f32[4,48,1024]{2,1,0:T(8,128)}, f32[4,48,1024]{2,1,0:T(8,128)}) fusion(f32[4,192,1024]{2,1,0:T(8,128)} %shard_map.60, s32[]{:T(128)S(6)} %select_n.73, s32[]{:T(128)S(6)} %select_n.76, s32[]{:T(128)S(6)} %select_n.75, s32[]{:T(128)S(6)} %select_n.74), kind=kLoop, calls=%fused_computation.123 | loop fusion | bytes 6291472 | tf_op jit(solution)/shard_map/dynamic_slice | solution.py:220
  153.1 1.6 collective-permute-start.6
  154.7 0.5 collective-permute-start.7
  155.2 0.8 collective-permute-start.8
  156.5 0.4 stack_reshape.12
  156.9 14.1 %collective-permute-done.6 = f32[4,48,1024]{2,1,0:T(8,128)} collective-permute-done((f32[4,48,1024]{2,1,0:T(8,128)}, f32[4,48,1024]{2,1,0:T(8,128)}, u32[]{:S(2)}, u32[]{:S(2)}) %collective-permute-start.6) | collective-permute-done | bytes 786464 | tf_op jit(solution)/shard_map/ppermute | solution.py:222
  171.0 2.7 %stack_reshape.13 = f32[1,192,16,64]{3,2,1,0:T(8,128)} reshape(f32[4,48,1024]{2,1,0:T(8,128)} %collective-permute-done.6) | data formatting | bytes 1572864 | tf_op jit(solution)/shard_map/stack;reshape | solution.py:43
  173.7 1.8 collective-permute-done.7
  175.5 2.7 %stack_reshape.14 = f32[1,192,16,64]{3,2,1,0:T(8,128)} reshape(f32[4,48,1024]{2,1,0:T(8,128)} %collective-permute-done.7) | data formatting | bytes 1572864 | tf_op jit(solution)/shard_map/stack;reshape | solution.py:43
  178.2 11.0 %collective-permute-done.8 = f32[4,48,1024]{2,1,0:T(8,128)S(1)} collective-permute-done((f32[4,48,1024]{2,1,0:T(8,128)}, f32[4,48,1024]{2,1,0:T(8,128)S(1)}, u32[]{:S(2)}, u32[]{:S(2)}) %collective-permute-start.8) | collective-permute-done | bytes 786464 | tf_op jit(solution)/shard_map/ppermute | solution.py:222
  189.1 1.6 stack_reshape.15
  190.7 7.5 %fusion.23 = f32[192,64,128]{2,1,0:T(8,128)S(1)} fusion(f32[1,192,16,64]{3,2,0,1:T(8,128)} %bitcast.69, f32[1,192,16,64]{3,2,0,1:T(8,128)} %bitcast.68, f32[1,192,16,64]{3,2,0,1:T(8,128)} %bitcast.67, f32[1,192,16,64]{3,2,0,1:T(8,128)S(1)} %bitcast.66, f32[1,16,128]{2,1,0:T(8,128)S(1)} %get-tuple-element.33, f32[1,16,128]{2,1,0:T(8,128)S(1)} %get-tuple-element.32, ...), kind=kOutput, calls=%fused_computation.36 | convolution fusion | flops 606363648 | bytes 9469952 | tf_op jit(solution)/shard_map/prab,pac->rbc/dot_general | solution.py:47
  198.2 3.0 %multiply_add_fusion = (f32[192,64,64]{2,1,0:T(8,128)S(1)}, f32[192,64,64]{2,1,0:T(8,128)S(1)}) fusion(f32[192,64,128]{2,1,0:T(8,128)S(1)} %fusion.23, f32[64,64]{1,0:T(8,128)S(1)} %get-tuple-element.45, f32[64,64]{1,0:T(8,128)S(1)} %get-tuple-element.46), kind=kLoop, calls=%fused_computation.19 | loop fusion | flops 4718592 | bytes 12615680 | tf_op jit(solution)/shard_map/add | solution.py:59
  201.2 3.5 %fusion.28 = f32[192,40,128]{2,1,0:T(8,128)S(1)} fusion(f32[192,64,64]{2,1,0:T(8,128)S(1)} %get-tuple-element.13, f32[192,64,64]{2,1,0:T(8,128)S(1)} %get-tuple-element.12, f32[64,20]{0,1:T(8,128)S(1)} %get-tuple-element.47, f32[64,20]{0,1:T(8,128)S(1)} %get-tuple-element.48), kind=kOutput, calls=%fused_computation.41 | convolution fusion | flops 379062784 | bytes 10233856 | tf_op jit(solution)/shard_map/rbc,bq->rqc/dot_general | solution.py:66
  204.7 2.7 %fusion.26 = (f32[192,20,64]{2,1,0:T(8,128)S(1)}, f32[192,20,64]{2,1,0:T(8,128)}) fusion(f32[192,40,128]{2,1,0:T(8,128)S(1)} %fusion.28), kind=kLoop, calls=%fused_computation.38 | loop fusion | flops 983040 | bytes 5898240 | tf_op jit(solution)/shard_map/mul | solution.py:76
  207.4 2.0 reshape.170
  209.4 1.6 copy.42
  211.0 0.5 reshape.171
  211.4 1.6 copy.43
  (30 shorter events, 1.4 us)
Async XLA Ops:
  9.1 9.8 %copy-start.6 = (f32[6,5,32]{2,0,1:T(8,128)S(1)}, f32[6,5,32]{2,0,1:T(8,128)}, u32[]{:S(2)}) copy-start(f32[6,5,32]{2,0,1:T(8,128)} %param.7) | copy-start | bytes 11524
  9.1 9.9 %copy-start = (f32[6,32,4,1024]{3,2,1,0:T(4,128)S(1)}, f32[6,32,4,1024]{3,2,1,0:T(4,128)}, u32[]{:S(2)}) copy-start(f32[6,32,4,1024]{3,2,1,0:T(4,128)} %param.4) | copy-start | bytes 9437188
  9.1 56.5 %collective-permute-start = (f32[6,32,3,1024]{3,1,2,0:T(8,128)}, f32[6,32,3,1024]{3,1,2,0:T(8,128)}, u32[]{:S(2)}, u32[]{:S(2)}) collective-permute-start(f32[6,32,3,1024]{3,1,2,0:T(8,128)} %copy.45), channel_id=1, source_target_pairs={{0,4},{4,8},{8,12},{12,16},{16,20},{20,24},{24,28},{1,5},{5,9},{9,... | collective-permute-start | bytes 7077896 | tf_op jit(solution)/shard_map/ppermute | solution.py:26
  15.6 100.4 %collective-permute-start.1 = (f32[6,32,3,1024]{3,1,2,0:T(8,128)}, f32[6,32,3,1024]{3,1,2,0:T(8,128)}, u32[]{:S(2)}, u32[]{:S(2)}) collective-permute-start(f32[6,32,3,1024]{3,1,2,0:T(8,128)} %copy.46), channel_id=1, source_target_pairs={{4,0},{8,4},{12,8},{16,12},{20,16},{24,20},{28,24},{5,1},{9,5},{13... | collective-permute-start | bytes 7077896 | tf_op jit(solution)/shard_map/ppermute | solution.py:29
  19.0 4.7 %copy-start.3 = (f32[6,32]{1,0:T(8,128)}, f32[6,32]{1,0:T(8,128)S(1)}, u32[]{:S(2)}) copy-start(f32[6,32]{1,0:T(8,128)S(1)} %get-tuple-element.40) | copy-start | bytes 2308
  21.8 4.6 %copy-start.2 = (f32[16,4,1024]{2,1,0:T(4,128)S(1)}, f32[16,4,1024]{2,1,0:T(4,128)}, u32[]{:S(2)}) copy-start(f32[16,4,1024]{2,1,0:T(4,128)} %param.5) | copy-start | bytes 786436
  21.8 5.6 %copy-start.5 = (s32[2,4,1024]{2,1,0:T(4,128)S(1)}, s32[2,4,1024]{2,1,0:T(4,128)}, u32[]{:S(2)}) copy-start(s32[2,4,1024]{2,1,0:T(4,128)} %param.6) | copy-start | bytes 98308
  24.7 9.9 %collective-permute-start.2 = (f32[4,192,16]{2,1,0:T(8,128)}, f32[4,192,16]{2,1,0:T(8,128)}, u32[]{:S(2)}, u32[]{:S(2)}) collective-permute-start(f32[4,192,16]{2,1,0:T(8,128)} %get-tuple-element.27), channel_id=1, source_target_pairs={{0,1},{1,2},{2,3},{3,0},{4,5},{5,6},{6,7},{7,4},{8,9},{9,10},{10,1... | collective-permute-start | bytes 147464 | tf_op jit(solution)/shard_map/ppermute | solution.py:26
  24.7 10.7 %collective-permute-start.3 = (f32[4,192,16]{2,1,0:T(8,128)}, f32[4,192,16]{2,1,0:T(8,128)}, u32[]{:S(2)}, u32[]{:S(2)}) collective-permute-start(f32[4,192,16]{2,1,0:T(8,128)} %get-tuple-element.26), channel_id=1, source_target_pairs={{1,0},{2,1},{3,2},{0,3},{5,4},{6,5},{7,6},{4,7},{9,8},{10,9},{11,1... | collective-permute-start | bytes 147464 | tf_op jit(solution)/shard_map/ppermute | solution.py:29
  52.5 66.3 %copy-start.4 = (f32[6,32]{1,0:T(8,128)S(1)}, f32[6,32]{1,0:T(8,128)}, u32[]{:S(2)}) copy-start(f32[6,32]{1,0:T(8,128)} %copy-done.3) | copy-start | bytes 2308
  122.1 2.1 copy-start.1
  124.7 4.1 %collective-permute-start.4 = (f32[6,192,16]{1,2,0:T(8,128)S(1)}, f32[6,192,16]{1,2,0:T(8,128)S(1)}, u32[]{:S(2)}, u32[]{:S(2)}) collective-permute-start(f32[6,192,16]{1,2,0:T(8,128)S(1)} %copy.34), channel_id=1, source_target_pairs={{0,1},{1,2},{2,3},{3,0},{4,5},{5,6},{6,7},{7,4},{8,9},{9,10},{10,1... | collective-permute-start | bytes 221192 | tf_op jit(solution)/shard_map/ppermute | solution.py:26
  124.9 4.0 %collective-permute-start.5 = (f32[6,192,16]{1,2,0:T(8,128)S(1)}, f32[6,192,16]{1,2,0:T(8,128)S(1)}, u32[]{:S(2)}, u32[]{:S(2)}) collective-permute-start(f32[6,192,16]{1,2,0:T(8,128)S(1)} %copy.35), channel_id=1, source_target_pairs={{1,0},{2,1},{3,2},{0,3},{5,4},{6,5},{7,6},{4,7},{9,8},{10,9},{11,1... | collective-permute-start | bytes 221192 | tf_op jit(solution)/shard_map/ppermute | solution.py:29
  153.1 17.9 %collective-permute-start.6 = (f32[4,48,1024]{2,1,0:T(8,128)}, f32[4,48,1024]{2,1,0:T(8,128)}, u32[]{:S(2)}, u32[]{:S(2)}) collective-permute-start(f32[4,48,1024]{2,1,0:T(8,128)} %get-tuple-element.25), channel_id=1, source_target_pairs={{0,1},{1,2},{2,3},{3,0},{4,5},{5,6},{6,7},{7,4},{8,9},{9,10},{10,1... | collective-permute-start | bytes 2359304 | tf_op jit(solution)/shard_map/ppermute | solution.py:222
  154.7 20.8 %collective-permute-start.7 = (f32[4,48,1024]{2,1,0:T(8,128)}, f32[4,48,1024]{2,1,0:T(8,128)}, u32[]{:S(2)}, u32[]{:S(2)}) collective-permute-start(f32[4,48,1024]{2,1,0:T(8,128)} %get-tuple-element.24), channel_id=1, source_target_pairs={{0,2},{1,3},{2,0},{3,1},{4,6},{5,7},{6,4},{7,5},{8,10},{9,11},{10,... | collective-permute-start | bytes 2359304 | tf_op jit(solution)/shard_map/ppermute | solution.py:222
  155.2 33.9 %collective-permute-start.8 = (f32[4,48,1024]{2,1,0:T(8,128)}, f32[4,48,1024]{2,1,0:T(8,128)S(1)}, u32[]{:S(2)}, u32[]{:S(2)}) collective-permute-start(f32[4,48,1024]{2,1,0:T(8,128)} %get-tuple-element.23), channel_id=1, source_target_pairs={{0,3},{1,0},{2,1},{3,2},{4,7},{5,4},{6,5},{7,6},{8,11},{9,8},{10,9... | collective-permute-start | bytes 2359304 | tf_op jit(solution)/shard_map/ppermute | solution.py:222
